TPU v7x, 128 devices: a whole 4x4x4 slice. The times are simulated.
128 devices in a mesh: req: 16 (over z, y), seq: 8 (over x, core).
Axes of the slice: x: 4, y: 4, z: 4, core: 2. Of those that a mesh axis runs over, the one named last changes fastest.
Arguments:
- queries: bfloat16 [32, 48, 8192], P('req', None, 'seq')
- draft_key_value: bfloat16 [32, 48, 2048], P('req', None, 'seq'), may hold values from -6 to 6
- kv_cache: bfloat16 [32, 16384, 2048], P('req', 'seq')
- cache_lengths: int32 [32], P('req'), may hold values from 2 to 16384, as said below
- ancestors: int32 [32, 48, 48], P('req'), may hold values from 0 to 1, as said below
- dealing: int32 [32], replicated, may hold values from 0 to 31, as said below
- accepted_path: int32 [32, 8], P('req'), may hold values from 0 to 47
Outputs:
- verified_context: bfloat16 [1536, 8192], P(('req', 'seq'))
- kept_entries: bfloat16 [32, 8, 2048], P('req', None, 'seq')
Inputs may be any that keep to these rules, and one draw needn't show every extreme that they name: `dealing`: a permutation of the request ids. `cache_lengths`: at least 2 live positions; some slot's cache is full (16384). Each row is the 0/1 indicator of a draft token's ancestors in its tree, the token itself included; token 0 is the root, a token's parent has a lower index.
All inputs are finite; a program needn't handle non-finite values.
Results may differ from a plain program's by a relative error of at most 0.0046.
Values may be sent and summed in bfloat16 or wider, within the bound.
No kernel may reach another device: no remote copies, remote signals or barrier semaphores. Data moves between devices by JAX's collectives and lax.ppermute only.
A program may use at most 128 MiB of HBM per device.

v0:
```python
import jax
import jax.numpy as jnp
from jax import lax
from jax.sharding import PartitionSpec as P

HEAD_WIDTH = 128
BLK = 1024


def online_merge(earlier, later):
    max_a, sum_a, acc_a = earlier
    max_b, sum_b, acc_b = later
    row_max = jnp.maximum(max_a, max_b)
    scale_a = jnp.exp(max_a - row_max)
    scale_b = jnp.exp(max_b - row_max)
    return (
        row_max,
        sum_a * scale_a + sum_b * scale_b,
        acc_a * scale_a[..., None] + acc_b * scale_b[..., None],
    )


def block_terms(grouped, key_rows, values, allowed):
    scores = jnp.einsum(
        "tkgd,skd->tkgs", grouped, key_rows, preferred_element_type=jnp.float32
    ) * HEAD_WIDTH ** (-0.5)
    scores = jnp.where(allowed, scores, jnp.float32(-1e30))
    row_max = jnp.max(scores, axis=-1)
    weights = jnp.where(allowed, jnp.exp(scores - row_max[..., None]), jnp.float32(0.0))
    row_sum = jnp.sum(weights, axis=-1)
    row_acc = jnp.einsum(
        "tkgs,skd->tkgd", weights.astype(jnp.bfloat16), values, preferred_element_type=jnp.float32
    )
    return (row_max, row_sum, row_acc)


def attend(query_rows, cache_rows, draft_rows, length, pos_offset, tree_mask, use_draft, blk_size):
    tree_len = query_rows.shape[0]
    kv_heads = cache_rows.shape[1] // (2 * HEAD_WIDTH)
    groups = query_rows.shape[1] // (HEAD_WIDTH * kv_heads)
    grouped = query_rows.reshape(tree_len, kv_heads, groups, HEAD_WIDTH)
    draft_part = draft_rows.reshape(tree_len, kv_heads, 2, HEAD_WIDTH)
    draft_allowed = jnp.logical_and(tree_mask > 0, use_draft)[:, None, None, :]
    running = block_terms(grouped, draft_part[:, :, 0], draft_part[:, :, 1], draft_allowed)
    blk_count = cache_rows.shape[0] // blk_size

    def body_step(blk_index, state):
        blk_start = blk_index * blk_size

        def absorb(state_in):
            cache_piece = lax.dynamic_slice_in_dim(cache_rows, blk_start, blk_size, 0).reshape(
                blk_size, kv_heads, 2, HEAD_WIDTH
            )
            positions = pos_offset + blk_start + jnp.arange(blk_size, dtype=jnp.int32)
            allowed = (positions < length)[None, None, None, :]
            return online_merge(
                state_in, block_terms(grouped, cache_piece[:, :, 0], cache_piece[:, :, 1], allowed)
            )

        return lax.cond(pos_offset + blk_start < length, absorb, lambda state_in: state_in, state)

    return lax.fori_loop(0, blk_count, body_step, running)


def body(queries, draft_key_value, kv_cache, cache_lengths, ancestors, dealing, accepted_path):
    local_reqs = kv_cache.shape[0]
    tree_len = queries.shape[1]
    picker = (
        accepted_path[:, :, None] == jnp.arange(tree_len, dtype=jnp.int32)[None, None, :]
    ).astype(jnp.bfloat16)
    kept_entries = jnp.einsum(
        "rit,rtc->ric", picker, draft_key_value, preferred_element_type=jnp.float32
    ).astype(jnp.bfloat16)
    every_query, every_draft = (
        lax.all_gather(queries, "req", axis=0, tiled=True),
        lax.all_gather(draft_key_value, "req", axis=0, tiled=True),
    )
    chosen = lax.dynamic_slice_in_dim(dealing, lax.axis_index("req") * local_reqs, local_reqs)
    own_query = jnp.stack(
        [
            lax.dynamic_index_in_dim(every_query, chosen[slot], 0, keepdims=False)
            for slot in range(local_reqs)
        ],
        axis=0,
    )
    own_draft = jnp.stack(
        [
            lax.dynamic_index_in_dim(every_draft, chosen[slot], 0, keepdims=False)
            for slot in range(local_reqs)
        ],
        axis=0,
    )
    seq_count = lax.axis_size("seq")
    full_query, full_draft = (
        lax.all_gather(own_query, "seq", axis=2, tiled=True),
        lax.all_gather(own_draft, "seq", axis=2, tiled=True),
    )
    position = lax.axis_index("seq")
    pos_offset = position * kv_cache.shape[1]
    maxima, sums, partials = ([], [], [])
    for slot_index in range(local_reqs):
        row_max, row_sum, row_acc = attend(
            full_query[slot_index],
            kv_cache[slot_index],
            full_draft[slot_index],
            cache_lengths[slot_index],
            pos_offset,
            ancestors[slot_index],
            position == 0,
            BLK,
        )
        maxima.append(row_max.reshape(tree_len, -1))
        sums.append(row_sum.reshape(tree_len, -1))
        partials.append(row_acc.reshape(tree_len, -1))
    all_max = jnp.concatenate(maxima, axis=0)
    all_sum = jnp.concatenate(sums, axis=0)
    all_acc = jnp.concatenate(partials, axis=0)
    head_count = all_max.shape[1]
    recv_acc, recv_max, recv_sum = (
        lax.all_to_all(all_acc[None], "seq", split_axis=1, concat_axis=0, tiled=True),
        lax.all_to_all(all_max[None], "seq", split_axis=1, concat_axis=0, tiled=True),
        lax.all_to_all(all_sum[None], "seq", split_axis=1, concat_axis=0, tiled=True),
    )
    top_max = jnp.max(recv_max, axis=0)
    factors = jnp.exp(recv_max - top_max[None])
    denominator = jnp.sum(factors * recv_sum, axis=0)
    token_count = recv_acc.shape[1]
    numerator = jnp.sum(
        factors[..., None] * recv_acc.reshape(seq_count, token_count, head_count, HEAD_WIDTH),
        axis=0,
    )
    context = (
        (numerator / denominator[..., None])
        .reshape(token_count, head_count * HEAD_WIDTH)
        .astype(jnp.bfloat16)
    )
    return (context, kept_entries)


def solution(mesh):
    placed = (
        P("req", None, "seq"),
        P("req", None, "seq"),
        P("req", "seq", None),
        P("req"),
        P("req", None, None),
        P(),
        P("req", None),
    )
    return jax.shard_map(
        body,
        mesh=mesh,
        in_specs=placed,
        out_specs=(P(("req", "seq"), None), P("req", None, "seq")),
        check_vma=False,
    )
```

profile of v0, /device:TPU:1, one launch (start us, length us, event | category | flops | bytes accessed | tf_op | source)
XLA Modules:
  0.0 240.3 jit_solution(1700396935020122704)
XLA Ops:
  12.8 23.5 %all_gather.12 = bf16[32,48,256]{2,1,0:T(8,128)(2,1)S(1)} all-gather(bf16[2,48,256]{2,1,0:T(8,128)(2,1)} %param.16), channel_id=1, replica_groups=mesh['req'=16,'seq'=8] {'req'}, dimensions={0}, use_global_device_ids=true | all-gather | bytes 835584 | tf_op jit(solution)/shard_map/all_gather | solution.py:76
  36.4 18.4 %all_gather.13 = bf16[2,48,2048]{2,1,0:T(8,128)(2,1)S(1)} all-gather(bf16[2,48,256]{2,1,0:T(8,128)(2,1)S(1)} %pad_maximum_fusion.1), channel_id=1, replica_groups=mesh['req'=16,'seq'=8] {'seq'}, dimensions={2}, use_global_device_ids=true | all-gather | bytes 442368 | tf_op jit(solution)/shard_map/all_gather | solution.py:96
  54.8 6.8 %all-gather.3.cloned.1.call-done = bf16[32,48,1024]{2,1,0:T(8,128)(2,1)} async-done(((bf16[2,48,1024]{2,1,0:T(8,128)(2,1)}), bf16[32,48,1024]{2,1,0:T(8,128)(2,1)}) %all-gather.3.cloned.1.call-update) | async-done | bytes 3145744 | tf_op jit(solution)/shard_map/all_gather | solution.py:75
  63.6 12.0 %fusion.51 = (bf16[1,2048,2048]{2,1,0:T(8,128)(2,1)}, bf16[1,2048,2048]{2,1,0:T(8,128)(2,1)}) fusion(bf16[2,2048,2048]{2,1,0:T(8,128)(2,1)} %param.17), kind=kLoop, calls=%fused_computation.96 | loop fusion | bytes 33554432 | tf_op jit(solution)/shard_map/slice | solution.py:104
  75.6 12.4 %copy.107 = bf16[1,2048,2048]{1,2,0:T(8,128)(2,1)} copy(bf16[1,2048,2048]{2,1,0:T(8,128)(2,1)} %get-tuple-element.463) | data formatting | bytes 16777216
  88.2 12.3 %copy.104 = bf16[1,2048,2048]{1,2,0:T(8,128)(2,1)} copy(bf16[1,2048,2048]{2,1,0:T(8,128)(2,1)} %get-tuple-element.462) | data formatting | bytes 16777216
  107.2 26.6 %while.35 = (s32[]{:T(128)}, f32[48,8,8]{0,2,1:T(8,128)S(1)}, f32[48,8,8]{0,2,1:T(8,128)S(1)}, f32[48,8,8,128]{3,0,2,1:T(8,128)S(1)}, s32[]{:T(128)}, /*index=5*...) while((s32[]{:T(128)}, f32[48,8,8]{0,2,1:T(8,128)S(1)}, ...), condition=%wide.region_15.16_spmd, body=%wide.region_10.15_spmd.sunk | while | flops 1652701184 | bytes 54502720 | solution.py:62
  107.9 12.6 %conditional.5 = ((f32[48,8,8]{0,2,1:T(8,128)S(1)}, f32[48,8,8]{0,2,1:T(8,128)S(1)}, f32[48,8,8,128]{3,0,2,1:T(8,128)S(1)})) conditional(s32[]{:T(128)} %convert_element_type.58, (f32[48,8,8]{0,2,1:T(8,128)S(1)}, f32[48,8,8]{0,2,1:T(8,128)S(1)}, f32[48,8,8,128]{3,0,2,1:T(8,128)S(1)}) %tuple.103, (s32[]{:T(128)}, s32[]{:T(128)}, s32[]{:T(128)}, ...), branch_computations={%region_11.11_spmd, %region_12.14_spmd} | conditional | flops 1652701184 | bytes 54502488 | solution.py:60
  108.6 2.6 %constant_dynamic-slice_fusion.1 = bf16[1024,2048]{0,1:T(8,128)(2,1)S(1)} fusion(bf16[2048,2048]{0,1:T(8,128)(2,1)} %get-tuple-element.338, s32[]{:T(128)S(6)} %select_n.40), kind=kLoop, calls=%fused_computation.42 | loop fusion | bytes 8388612 | tf_op jit(solution)/shard_map/while/body/eval_jaxpr/cond/branch_1_fun/dynamic_slice | solution.py:51
  111.2 2.2 bitcast_reduce_fusion.1
  113.4 3.6 %fusion.18 = f32[48,8,8]{0,2,1:T(8,128)S(1)} fusion(f32[8,1024,48,8]{1,2,3,0:T(8,128)S(1)} %get-tuple-element.461, f32[48,8,8]{0,2,1:T(8,128)S(1)} %get-tuple-element.460, pred[1024]{0:T(1024)(128)(4,1)S(1)} %add_compare_fusion.1), kind=kLoop, calls=%fused_computation.29 | loop fusion | flops 15725568 | bytes 12608512 | tf_op jit(solution)/shard_map/while/body/eval_jaxpr/cond/branch_1_fun/reduce_sum | solution.py:30
  117.1 3.3 %fusion.24 = f32[48,8,8,128]{3,0,2,1:T(8,128)S(1)} fusion(f32[48,8,8,128]{3,0,2,1:T(8,128)S(1)} %get-tuple-element.341, f32[8,1024,48,8]{1,2,3,0:T(8,128)S(1)} %get-tuple-element.461, f32[48,8,8]{0,2,1:T(8,128)S(1)} %get-tuple-element.460, pred[1024]{0:T(1024)(128)(4,1)S(1)} %add_compare_fusion.1, bf16[1024,8,2,128]{0,3,2,1:T(8,128)(2,1)S(1)} %bitcast.166, ...), kind=kOutput, calls=%fused_computation.37 | convolution fusion | flops 822214656 | bytes 17926144 | tf_op jit(solution)/shard_map/while/body/eval_jaxpr/cond/branch_1_fun/tkgs,skd->tkgd/dot_general | solution.py:31
  121.1 12.6 %conditional.5 = ((f32[48,8,8]{0,2,1:T(8,128)S(1)}, f32[48,8,8]{0,2,1:T(8,128)S(1)}, f32[48,8,8,128]{3,0,2,1:T(8,128)S(1)})) conditional(s32[]{:T(128)} %convert_element_type.58, (f32[48,8,8]{0,2,1:T(8,128)S(1)}, f32[48,8,8]{0,2,1:T(8,128)S(1)}, f32[48,8,8,128]{3,0,2,1:T(8,128)S(1)}) %tuple.103, (s32[]{:T(128)}, s32[]{:T(128)}, s32[]{:T(128)}, ...), branch_computations={%region_11.11_spmd, %region_12.14_spmd} | conditional | flops 1652701184 | bytes 54502488 | solution.py:60
  121.8 2.6 %constant_dynamic-slice_fusion.1 = bf16[1024,2048]{0,1:T(8,128)(2,1)S(1)} fusion(bf16[2048,2048]{0,1:T(8,128)(2,1)} %get-tuple-element.338, s32[]{:T(128)S(6)} %select_n.40), kind=kLoop, calls=%fused_computation.42 | loop fusion | bytes 8388612 | tf_op jit(solution)/shard_map/while/body/eval_jaxpr/cond/branch_1_fun/dynamic_slice | solution.py:51
  126.6 3.6 %fusion.18 = f32[48,8,8]{0,2,1:T(8,128)S(1)} fusion(f32[8,1024,48,8]{1,2,3,0:T(8,128)S(1)} %get-tuple-element.461, f32[48,8,8]{0,2,1:T(8,128)S(1)} %get-tuple-element.460, pred[1024]{0:T(1024)(128)(4,1)S(1)} %add_compare_fusion.1), kind=kLoop, calls=%fused_computation.29 | loop fusion | flops 15725568 | bytes 12608512 | tf_op jit(solution)/shard_map/while/body/eval_jaxpr/cond/branch_1_fun/reduce_sum | solution.py:30
  130.3 3.3 %fusion.24 = f32[48,8,8,128]{3,0,2,1:T(8,128)S(1)} fusion(f32[48,8,8,128]{3,0,2,1:T(8,128)S(1)} %get-tuple-element.341, f32[8,1024,48,8]{1,2,3,0:T(8,128)S(1)} %get-tuple-element.461, f32[48,8,8]{0,2,1:T(8,128)S(1)} %get-tuple-element.460, pred[1024]{0:T(1024)(128)(4,1)S(1)} %add_compare_fusion.1, bf16[1024,8,2,128]{0,3,2,1:T(8,128)(2,1)S(1)} %bitcast.166, ...), kind=kOutput, calls=%fused_computation.37 | convolution fusion | flops 822214656 | bytes 17926144 | tf_op jit(solution)/shard_map/while/body/eval_jaxpr/cond/branch_1_fun/tkgs,skd->tkgd/dot_general | solution.py:31
  138.3 26.5 %while.34 = (s32[]{:T(128)}, f32[48,8,8]{0,2,1:T(8,128)S(1)}, f32[48,8,8]{0,2,1:T(8,128)S(1)}, f32[48,8,8,128]{3,0,2,1:T(8,128)S(1)}, s32[]{:T(128)}, /*index=5*...) while((s32[]{:T(128)}, f32[48,8,8]{0,2,1:T(8,128)S(1)}, ...), condition=%wide.region_7.8_spmd, body=%wide.region_2.7_spmd.sunk | while | flops 1652701184 | bytes 54502720 | solution.py:62
  139.0 12.6 %conditional.4 = ((f32[48,8,8]{0,2,1:T(8,128)S(1)}, f32[48,8,8]{0,2,1:T(8,128)S(1)}, f32[48,8,8,128]{3,0,2,1:T(8,128)S(1)})) conditional(s32[]{:T(128)} %convert_element_type.57, (f32[48,8,8]{0,2,1:T(8,128)S(1)}, f32[48,8,8]{0,2,1:T(8,128)S(1)}, f32[48,8,8,128]{3,0,2,1:T(8,128)S(1)}) %tuple.100, (s32[]{:T(128)}, s32[]{:T(128)}, s32[]{:T(128)}, ...), branch_computations={%region_3.3_spmd, %region_4.6_spmd} | conditional | flops 1652701184 | bytes 54502488 | solution.py:60
  139.6 2.6 %constant_dynamic-slice_fusion = bf16[1024,2048]{0,1:T(8,128)(2,1)S(1)} fusion(bf16[2048,2048]{0,1:T(8,128)(2,1)} %get-tuple-element.318, s32[]{:T(128)S(6)} %select_n.36), kind=kLoop, calls=%fused_computation.19 | loop fusion | bytes 8388612 | tf_op jit(solution)/shard_map/while/body/eval_jaxpr/cond/branch_1_fun/dynamic_slice | solution.py:51
  142.3 2.2 bitcast_reduce_fusion
  144.5 3.6 %fusion.3 = f32[48,8,8]{0,2,1:T(8,128)S(1)} fusion(f32[8,1024,48,8]{1,2,3,0:T(8,128)S(1)} %get-tuple-element.459, f32[48,8,8]{0,2,1:T(8,128)S(1)} %get-tuple-element.458, pred[1024]{0:T(1024)(128)(4,1)S(1)} %add_compare_fusion), kind=kLoop, calls=%fused_computation.6 | loop fusion | flops 15725568 | bytes 12608512 | tf_op jit(solution)/shard_map/while/body/eval_jaxpr/cond/branch_1_fun/reduce_sum | solution.py:30
  148.2 3.3 %fusion.9 = f32[48,8,8,128]{3,0,2,1:T(8,128)S(1)} fusion(f32[48,8,8,128]{3,0,2,1:T(8,128)S(1)} %get-tuple-element.321, f32[8,1024,48,8]{1,2,3,0:T(8,128)S(1)} %get-tuple-element.459, f32[48,8,8]{0,2,1:T(8,128)S(1)} %get-tuple-element.458, pred[1024]{0:T(1024)(128)(4,1)S(1)} %add_compare_fusion, bf16[1024,8,2,128]{0,3,2,1:T(8,128)(2,1)S(1)} %bitcast.168, ...), kind=kOutput, calls=%fused_computation.14 | convolution fusion | flops 822214656 | bytes 17926144 | tf_op jit(solution)/shard_map/while/body/eval_jaxpr/cond/branch_1_fun/tkgs,skd->tkgd/dot_general | solution.py:31
  152.2 12.6 %conditional.4 = ((f32[48,8,8]{0,2,1:T(8,128)S(1)}, f32[48,8,8]{0,2,1:T(8,128)S(1)}, f32[48,8,8,128]{3,0,2,1:T(8,128)S(1)})) conditional(s32[]{:T(128)} %convert_element_type.57, (f32[48,8,8]{0,2,1:T(8,128)S(1)}, f32[48,8,8]{0,2,1:T(8,128)S(1)}, f32[48,8,8,128]{3,0,2,1:T(8,128)S(1)}) %tuple.100, (s32[]{:T(128)}, s32[]{:T(128)}, s32[]{:T(128)}, ...), branch_computations={%region_3.3_spmd, %region_4.6_spmd} | conditional | flops 1652701184 | bytes 54502488 | solution.py:60
  152.9 2.6 %constant_dynamic-slice_fusion = bf16[1024,2048]{0,1:T(8,128)(2,1)S(1)} fusion(bf16[2048,2048]{0,1:T(8,128)(2,1)} %get-tuple-element.318, s32[]{:T(128)S(6)} %select_n.36), kind=kLoop, calls=%fused_computation.19 | loop fusion | bytes 8388612 | tf_op jit(solution)/shard_map/while/body/eval_jaxpr/cond/branch_1_fun/dynamic_slice | solution.py:51
  157.7 3.6 %fusion.3 = f32[48,8,8]{0,2,1:T(8,128)S(1)} fusion(f32[8,1024,48,8]{1,2,3,0:T(8,128)S(1)} %get-tuple-element.459, f32[48,8,8]{0,2,1:T(8,128)S(1)} %get-tuple-element.458, pred[1024]{0:T(1024)(128)(4,1)S(1)} %add_compare_fusion), kind=kLoop, calls=%fused_computation.6 | loop fusion | flops 15725568 | bytes 12608512 | tf_op jit(solution)/shard_map/while/body/eval_jaxpr/cond/branch_1_fun/reduce_sum | solution.py:30
  161.4 3.3 %fusion.9 = f32[48,8,8,128]{3,0,2,1:T(8,128)S(1)} fusion(f32[48,8,8,128]{3,0,2,1:T(8,128)S(1)} %get-tuple-element.321, f32[8,1024,48,8]{1,2,3,0:T(8,128)S(1)} %get-tuple-element.459, f32[48,8,8]{0,2,1:T(8,128)S(1)} %get-tuple-element.458, pred[1024]{0:T(1024)(128)(4,1)S(1)} %add_compare_fusion, bf16[1024,8,2,128]{0,3,2,1:T(8,128)(2,1)S(1)} %bitcast.168, ...), kind=kOutput, calls=%fused_computation.14 | convolution fusion | flops 822214656 | bytes 17926144 | tf_op jit(solution)/shard_map/while/body/eval_jaxpr/cond/branch_1_fun/tkgs,skd->tkgd/dot_general | solution.py:31
  168.7 4.6 %all-to-all-start.2 = ((f32[8,1,768]{2,1,0:T(1,128)}), f32[8,1,768]{2,1,0:T(1,128)S(1)}, u32[]{:S(2)}, u32[]{:S(2)}) async-start(f32[8,1,768]{2,1,0:T(1,128)} %reshape.139), calls=%async_computation.2 | async-start | bytes 49152 | tf_op jit(solution)/shard_map/all_to_all | solution.py:122
  173.3 4.1 %copy_bitcast_fusion = (f32[48,8192]{1,0:T(8,128)S(1)}, f32[48,8192]{1,0:T(8,128)S(1)}) fusion(f32[6,8,64,128]{3,2,1,0:T(8,128)} %bitcast.176, f32[6,8,64,128]{3,2,1,0:T(8,128)} %bitcast.177), kind=kLoop, calls=%fused_computation.48 | loop fusion | bytes 6291456 | tf_op jit(solution)/shard_map/reshape | solution.py:114
  179.0 4.8 %all-to-all-start = ((f32[8,1,768]{2,1,0:T(1,128)}), f32[8,1,768]{2,1,0:T(1,128)S(1)}, u32[]{:S(2)}, u32[]{:S(2)}) async-start(f32[8,1,768]{2,1,0:T(1,128)} %reshape.137), calls=%async_computation | async-start | bytes 49152 | tf_op jit(solution)/shard_map/all_to_all | solution.py:121
  184.1 4.9 %copy.84 = f32[1,96,8192]{2,0,1:T(1,128)} copy(f32[1,96,8192]{2,1,0:T(8,128)S(1)} %maximum_bitcast_fusion) | data formatting | bytes 6291456 | tf_op jit(solution)/shard_map/broadcast_in_dim | solution.py:120
  189.0 4.9 %all-to-all-start.1 = ((f32[1,96,8192]{2,0,1:T(1,128)}), f32[1,96,8192]{2,0,1:T(1,128)S(1)}, u32[]{:S(2)}, u32[]{:S(2)}) async-start(f32[1,96,8192]{2,0,1:T(1,128)} %copy.84), calls=%async_computation.1 | async-start | bytes 6291456 | tf_op jit(solution)/shard_map/all_to_all | solution.py:120
  198.6 32.8 %all-to-all-done.1 = f32[1,96,8192]{2,0,1:T(1,128)S(1)} async-done(((f32[1,96,8192]{2,0,1:T(1,128)}), f32[1,96,8192]{2,0,1:T(1,128)S(1)}, u32[]{:S(2)}, u32[]{:S(2)}) %all-to-all-start.1) | async-done | bytes 3145760 | tf_op jit(solution)/shard_map/all_to_all | solution.py:120
  (83 shorter events, 34.8 us)
Async XLA Ops:
  7.2 56.3 %copy-start.3 = (s32[2,48,48]{2,1,0:T(8,128)S(1)}, s32[2,48,48]{2,1,0:T(8,128)}, u32[]{:S(2)}) copy-start(s32[2,48,48]{2,1,0:T(8,128)} %param.19) | copy-start | bytes 55300
  7.2 54.4 %all-gather.3.cloned.1.call-start = ((), (), s32[]{:S(2)}) async-start(), calls=%async_computation.3 | async-start | bytes 3342336 | tf_op jit(solution)/shard_map/all_gather | solution.py:75
  7.9 95.1 %all-gather.5.cloned.1.call-start = ((), (), s32[]{:S(2)}) async-start(), calls=%async_computation.4 | async-start | bytes 1769472 | tf_op jit(solution)/shard_map/all_gather | solution.py:95
  88.2 12.3 %copy-start.4 = (s32[2]{0:T(128)S(1)}, s32[2]{0:T(128)}, u32[]{:S(2)}) copy-start(s32[2]{0:T(128)} %param.18) | copy-start | bytes 28
  104.7 2.0 copy-start.1
  133.9 2.4 %copy-start = (bf16[48,8,1,128]{3,2,1,0:T(2,128)(2,1)S(1)}, bf16[48,8,1,128]{3,2,1,0:T(2,128)(2,1)}, u32[]{:S(2)}) copy-start(bf16[48,8,1,128]{3,2,1,0:T(2,128)(2,1)} %get-tuple-element.473) | copy-start | bytes 294916
  168.7 10.3 %all-to-all-start.2 = ((f32[8,1,768]{2,1,0:T(1,128)}), f32[8,1,768]{2,1,0:T(1,128)S(1)}, u32[]{:S(2)}, u32[]{:S(2)}) async-start(f32[8,1,768]{2,1,0:T(1,128)} %reshape.139), calls=%async_computation.2 | async-start | bytes 49152 | tf_op jit(solution)/shard_map/all_to_all | solution.py:122
  179.0 10.0 %all-to-all-start = ((f32[8,1,768]{2,1,0:T(1,128)}), f32[8,1,768]{2,1,0:T(1,128)S(1)}, u32[]{:S(2)}, u32[]{:S(2)}) async-start(f32[8,1,768]{2,1,0:T(1,128)} %reshape.137), calls=%async_computation | async-start | bytes 49152 | tf_op jit(solution)/shard_map/all_to_all | solution.py:121
  189.0 4.9 %copy-start.2 = (bf16[2,48,256]{2,1,0:T(8,128)(2,1)S(1)}, bf16[2,48,256]{2,1,0:T(8,128)(2,1)}, u32[]{:S(2)}) copy-start(bf16[2,48,256]{2,1,0:T(8,128)(2,1)} %param.16) | copy-start | bytes 147460
  189.0 4.9 %copy-start.5 = (s32[2,8]{1,0:T(2,128)S(1)}, s32[2,8]{1,0:T(2,128)}, u32[]{:S(2)}) copy-start(s32[2,8]{1,0:T(2,128)} %param.21) | copy-start | bytes 196
  189.0 42.4 %all-to-all-start.1 = ((f32[1,96,8192]{2,0,1:T(1,128)}), f32[1,96,8192]{2,0,1:T(1,128)S(1)}, u32[]{:S(2)}, u32[]{:S(2)}) async-start(f32[1,96,8192]{2,0,1:T(1,128)} %copy.84), calls=%async_computation.1 | async-start | bytes 6291456 | tf_op jit(solution)/shard_map/all_to_all | solution.py:120
Sparse Core Ops, SparseCore 0:
  10.1 51.4 all-gather.2
  63.9 23.8 all-gather.4
where the time goes:
time: 242 us; the launch traced here: 240 us
  local copies, waits for them, and re-layouts  73 us (30%)
  blocking collectives  42 us (17%)
  waiting for transfers between devices  40.3 us (17%)
  matrix products  26.1 us (11%)
  other arithmetic  23.6 us (10%)
  between operations  18 us (7%)
  starting transfers between devices  14.4 us (6%)
  loops' own time  3.06 us (1%)
    all_to_all x1, waiting for transfers between devices, body(): lax.all_to_all(all_acc[None], 'seq', split_axis=1, concat_axis=0, tiled=T...  32.8 us
    unnamed x24, local copies, waits for them, and re-layouts  29.6 us
    all_gather x1, blocking collectives, body(): lax.all_gather(draft_key_value, 'req', axis=0, tiled=True)  23.5 us
    all_gather x1, blocking collectives, body(): lax.all_gather(own_draft, 'seq', axis=2, tiled=True)  18.4 us
    reduce_sum x6, other arithmetic, block_terms(): row_sum = jnp.sum(weights, axis=-1)  15.4 us
    dot_general x6, matrix products, block_terms(): jnp.einsum('tkgs,skd->tkgd', weights.astype(jnp.bfloat16), values, prefer...  14.4 us
    slice x1, local copies, waits for them, and re-layouts, body(): kv_cache[slot_index]  12 us
    dot_general x6, matrix products, block_terms(): jnp.einsum('tkgd,skd->tkgs', grouped, key_rows, preferred_element_type=jn...  11 us
  transfers between devices with their start and end apart: 5, of which 2 were waited for; matrix products, arithmetic and copies ran while one was open for 23% of the time, Pallas kernels for 0%

commit v1 on v0

v1 whole, which is shorter than its diff:
```python
import functools

import jax
import jax.numpy as jnp
from jax import lax
from jax.experimental import pallas as pl
from jax.experimental.pallas import tpu as pltpu
from jax.sharding import PartitionSpec as P

HEAD_WIDTH = 128
BLK = 1024
NEG = -1e30


def attn_kernel(live_ref, q_ref, kv_ref, m_ref, l_ref, acc_ref, *, n_blk, scale):
    slot = pl.program_id(0)
    live = live_ref[slot]
    q = q_ref[...]
    run_m = run_l = run_acc = None
    for b in range(n_blk):
        keys = kv_ref[b * BLK:(b + 1) * BLK, 0:HEAD_WIDTH]
        vals = kv_ref[b * BLK:(b + 1) * BLK, HEAD_WIDTH:2 * HEAD_WIDTH]
        s = lax.dot_general(
            q, keys, (((1,), (1,)), ((), ())), preferred_element_type=jnp.float32
        ) * scale
        pos = b * BLK + lax.broadcasted_iota(jnp.int32, (1, BLK), 1)
        allowed = pos < live
        s = jnp.where(allowed, s, jnp.float32(NEG))
        mb = jnp.max(s, axis=1, keepdims=True)
        w = jnp.where(allowed, jnp.exp(s - mb), jnp.float32(0.0))
        lb = jnp.sum(w, axis=1, keepdims=True)
        ob = jnp.dot(w.astype(jnp.bfloat16), vals, preferred_element_type=jnp.float32)
        if run_m is None:
            run_m, run_l, run_acc = mb, lb, ob
        else:
            new_m = jnp.maximum(run_m, mb)
            fa = jnp.exp(run_m - new_m)
            fb = jnp.exp(mb - new_m)
            run_l = run_l * fa + lb * fb
            run_acc = run_acc * fa + ob * fb
            run_m = new_m
    parts = m_ref.shape[0]
    rows = q.shape[0] // parts
    m_ref[...] = run_m.reshape(parts, rows, 1)
    l_ref[...] = run_l.reshape(parts, rows, 1)
    acc_ref[...] = run_acc.reshape(parts, rows, HEAD_WIDTH)


def local_attention(q4, kv, live, seq_count):
    slots, kvh, rows, _ = q4.shape
    positions = kv.shape[1]
    per_slot = seq_count // slots
    sub = rows // per_slot
    kern = functools.partial(attn_kernel, n_blk=positions // BLK, scale=HEAD_WIDTH ** (-0.5))
    grid_spec = pltpu.PrefetchScalarGridSpec(
        num_scalar_prefetch=1,
        grid=(slots, kvh),
        in_specs=[
            pl.BlockSpec((None, None, rows, HEAD_WIDTH), lambda i, k, lv: (i, k, 0, 0)),
            pl.BlockSpec((None, positions, 2 * HEAD_WIDTH), lambda i, k, lv: (i, 0, k)),
        ],
        out_specs=[
            pl.BlockSpec((per_slot, None, sub, 1), lambda i, k, lv: (i, k, 0, 0)),
            pl.BlockSpec((per_slot, None, sub, 1), lambda i, k, lv: (i, k, 0, 0)),
            pl.BlockSpec((per_slot, None, sub, HEAD_WIDTH), lambda i, k, lv: (i, k, 0, 0)),
        ],
    )
    return pl.pallas_call(
        kern,
        grid_spec=grid_spec,
        out_shape=[
            jax.ShapeDtypeStruct((seq_count, kvh, sub, 1), jnp.float32),
            jax.ShapeDtypeStruct((seq_count, kvh, sub, 1), jnp.float32),
            jax.ShapeDtypeStruct((seq_count, kvh, sub, HEAD_WIDTH), jnp.float32),
        ],
        compiler_params=pltpu.CompilerParams(
            dimension_semantics=("arbitrary", "arbitrary"),
            vmem_limit_bytes=48 * 1024 * 1024,
        ),
    )(live, q4, kv)


def body(queries, draft_key_value, kv_cache, cache_lengths, ancestors, dealing, accepted_path):
    local_reqs = kv_cache.shape[0]
    tree_len = queries.shape[1]
    picker = (
        accepted_path[:, :, None] == jnp.arange(tree_len, dtype=jnp.int32)[None, None, :]
    ).astype(jnp.bfloat16)
    kept_entries = jnp.einsum(
        "rit,rtc->ric", picker, draft_key_value, preferred_element_type=jnp.float32
    ).astype(jnp.bfloat16)
    every_query, every_draft = (
        lax.all_gather(queries, "req", axis=0, tiled=True),
        lax.all_gather(draft_key_value, "req", axis=0, tiled=True),
    )
    chosen = lax.dynamic_slice_in_dim(dealing, lax.axis_index("req") * local_reqs, local_reqs)
    own_query = jnp.stack(
        [
            lax.dynamic_index_in_dim(every_query, chosen[slot], 0, keepdims=False)
            for slot in range(local_reqs)
        ],
        axis=0,
    )
    own_draft = jnp.stack(
        [
            lax.dynamic_index_in_dim(every_draft, chosen[slot], 0, keepdims=False)
            for slot in range(local_reqs)
        ],
        axis=0,
    )
    seq_count = lax.axis_size("seq")
    full_query, full_draft = (
        lax.all_gather(own_query, "seq", axis=2, tiled=True),
        lax.all_gather(own_draft, "seq", axis=2, tiled=True),
    )
    position = lax.axis_index("seq")
    positions = kv_cache.shape[1]
    kv_heads = kv_cache.shape[2] // (2 * HEAD_WIDTH)
    groups = full_query.shape[2] // (HEAD_WIDTH * kv_heads)
    rows = tree_len * groups

    q4 = (
        full_query.reshape(local_reqs, tree_len, kv_heads, groups, HEAD_WIDTH)
        .transpose(0, 2, 1, 3, 4)
        .reshape(local_reqs, kv_heads, rows, HEAD_WIDTH)
    )
    live = jnp.clip(cache_lengths - position * positions, 0, positions).astype(jnp.int32)
    part_m, part_l, part_acc = local_attention(q4, kv_cache, live, seq_count)
    recv_m = lax.all_to_all(part_m, "seq", 0, 0, tiled=True)
    recv_l = lax.all_to_all(part_l, "seq", 0, 0, tiled=True)
    recv_acc = lax.all_to_all(part_acc, "seq", 0, 0, tiled=True)

    per_slot = seq_count // local_reqs
    tok = tree_len // per_slot
    my_slot = position // per_slot
    my_tok0 = (position % per_slot) * tok
    q_slot = lax.dynamic_index_in_dim(full_query, my_slot, 0, keepdims=False)
    q_mine = lax.dynamic_slice_in_dim(q_slot, my_tok0, tok, 0).reshape(
        tok, kv_heads, groups, HEAD_WIDTH
    )
    d_slot = lax.dynamic_index_in_dim(full_draft, my_slot, 0, keepdims=False).reshape(
        tree_len, kv_heads, 2, HEAD_WIDTH
    )
    anc = lax.dynamic_index_in_dim(ancestors, my_slot, 0, keepdims=False)
    anc = lax.dynamic_slice_in_dim(anc, my_tok0, tok, 0)
    allowed = (anc > 0)[None, :, None, :]
    sd = jnp.einsum(
        "tkgd,jkd->ktgj", q_mine, d_slot[:, :, 0], preferred_element_type=jnp.float32
    ) * HEAD_WIDTH ** (-0.5)
    sd = jnp.where(allowed, sd, jnp.float32(NEG))
    md = jnp.max(sd, axis=-1)
    wd = jnp.where(allowed, jnp.exp(sd - md[..., None]), jnp.float32(0.0))
    ld = jnp.sum(wd, axis=-1)
    od = jnp.einsum(
        "ktgj,jkd->ktgd", wd.astype(jnp.bfloat16), d_slot[:, :, 1], preferred_element_type=jnp.float32
    )
    md = md.reshape(kv_heads, tok * groups)
    ld = ld.reshape(kv_heads, tok * groups)
    od = od.reshape(kv_heads, tok * groups, HEAD_WIDTH)

    rm = recv_m[..., 0]
    rl = recv_l[..., 0]
    top = jnp.maximum(jnp.max(rm, axis=0), md)
    fr = jnp.exp(rm - top[None])
    fd = jnp.exp(md - top)
    den = jnp.sum(fr * rl, axis=0) + fd * ld
    num = jnp.sum(fr[..., None] * recv_acc, axis=0) + fd[..., None] * od
    res = num / den[..., None]
    context = (
        res.reshape(kv_heads, tok, groups, HEAD_WIDTH)
        .transpose(1, 0, 2, 3)
        .reshape(tok, kv_heads * groups * HEAD_WIDTH)
        .astype(jnp.bfloat16)
    )
    return (context, kept_entries)


def solution(mesh):
    placed = (
        P("req", None, "seq"),
        P("req", None, "seq"),
        P("req", "seq", None),
        P("req"),
        P("req", None, None),
        P(),
        P("req", None),
    )
    return jax.shard_map(
        body,
        mesh=mesh,
        in_specs=placed,
        out_specs=(P(("req", "seq"), None), P("req", None, "seq")),
        check_vma=False,
    )
```

time: 242 us -> 214 us (0.88)
  local copies, waits for them, and re-layouts: 73 us -> 15.7 us
  Pallas kernels: 0 us -> 32.8 us
  blocking collectives: 42 us -> 65.8 us
  matrix products: 26.1 us -> 2.92 us
  other arithmetic: 23.6 us -> 5.74 us
  waiting for transfers between devices: 40.3 us -> 56.8 us
  loops' own time: 3.06 us -> 0 us
    all_gather x1, waiting for transfers between devices: 6.81 us -> 47.5 us  [body(): lax.all_gather(queries, 'req', axis=0, tiled=True)]
    pallas_call x0 -> x1, Pallas kernels: none -> 32.8 us  [local_attention(): pl.pallas_call(kern, grid_spec=grid_spec, out_shape=[jax.ShapeDtypeStruct...]
    all_to_all x3, waiting for transfers between devices: 32.8 us -> 5.08 us  [the longest x1 4.11 us: body(): recv_l = lax.all_to_all(part_l, 'seq', 0, 0, tiled=True)]
    all_gather x1, blocking collectives: 18.4 us -> 45.4 us  [body(): lax.all_gather(own_draft, 'seq', axis=2, tiled=True)]
    unnamed x24 -> x20, local copies, waits for them, and re-layouts: 29.6 us -> 3.48 us
    dot_general x12 -> x2, matrix products: 25.3 us -> 1.33 us  [the longest x1 0.95 us: body(): jnp.einsum('tkgd,jkd->ktgj', q_mine, d_slot[:, :, 0], preferred_element_t...]
    reduce_sum x8 -> x3, other arithmetic: 16.5 us -> 2.35 us  [the longest x1 1.34 us: body(): ld = jnp.sum(wd, axis=-1)]
    slice x5 -> x1, local copies, waits for them, and re-layouts: 14.5 us -> 0.95 us  [body(): d_slot[:, :, 1]]
  transfers between devices with their start and end apart: 5 -> 5, of which waited for: 2 -> 4; matrix products, arithmetic and copies ran while one was open for 23% -> 7% of each run, Pallas kernels for 0% -> 0%
where the time goes in v1:
time: 214 us; the launch traced here: 213 us
  blocking collectives  65.8 us (31%)
  waiting for transfers between devices  56.8 us (27%)
  Pallas kernels  32.8 us (15%)
  between operations  18.1 us (8%)
  local copies, waits for them, and re-layouts  15.7 us (7%)
  starting transfers between devices  15 us (7%)
  other arithmetic  5.74 us (3%)
  matrix products  2.92 us (1%)
    all_gather x1, waiting for transfers between devices, body(): lax.all_gather(queries, 'req', axis=0, tiled=True)  47.5 us
    all_gather x1, blocking collectives, body(): lax.all_gather(own_draft, 'seq', axis=2, tiled=True)  45.4 us
    pallas_call x1, Pallas kernels, local_attention(): pl.pallas_call(kern, grid_spec=grid_spec, out_shape=[jax.ShapeDtypeStruct...  32.8 us
    all_gather x1, blocking collectives, body(): lax.all_gather(draft_key_value, 'req', axis=0, tiled=True)  20.3 us
    all_to_all x1, starting transfers between devices, body(): recv_m = lax.all_to_all(part_m, 'seq', 0, 0, tiled=True)  6.67 us
    pallas_call x2, local copies, waits for them, and re-layouts, local_attention(): pl.pallas_call(kern, grid_spec=grid_spec, out_shape=[jax.ShapeDtypeStruct...  4.8 us
    all_to_all x1, starting transfers between devices, body(): recv_acc = lax.all_to_all(part_acc, 'seq', 0, 0, tiled=True)  4.28 us
  transfers between devices with their start and end apart: 5, of which 4 were waited for; matrix products, arithmetic and copies ran while one was open for 7% of the time, Pallas kernels for 0%

profile of v1, /device:TPU:1, one launch (start us, length us, event | category | flops | bytes accessed | tf_op | source)
XLA Modules:
  0.0 212.8 jit_solution(5034108464837378803)
XLA Ops:
  7.2 0.7 all-gather.3.cloned.1.call-update
  7.9 0.7 dynamic_slice.31
  13.2 47.5 %all-gather.3.cloned.1.call-done = bf16[32,48,1024]{2,1,0:T(8,128)(2,1)} async-done(((bf16[2,48,1024]{2,1,0:T(8,128)(2,1)}), bf16[32,48,1024]{2,1,0:T(8,128)(2,1)}) %all-gather.3.cloned.1.call-update) | async-done | bytes 3145744 | tf_op jit(solution)/shard_map/all_gather | solution.py:93
  60.7 1.0 constant_dynamic-slice_fusion.5
  61.6 0.7 pad_maximum_fusion
  62.4 20.3 %all_gather.14 = bf16[32,48,256]{2,1,0:T(8,128)(2,1)} all-gather(bf16[2,48,256]{2,1,0:T(8,128)(2,1)} %param.8), channel_id=1, replica_groups=mesh['req'=16,'seq'=8] {'req'}, dimensions={0}, use_global_device_ids=true | all-gather | bytes 835584 | tf_op jit(solution)/shard_map/all_gather | solution.py:94
  82.7 0.7 subtract_clamp_fusion.live_ref
  83.4 3.5 %all-gather.5.cloned.1.call-done = bf16[2,48,8192]{2,1,0:T(8,128)(2,1)} async-done(((bf16[2,48,1024]{2,1,0:T(8,128)(2,1)}), bf16[2,48,8192]{2,1,0:T(8,128)(2,1)}) %all-gather.5.cloned.1.call-update) | async-done | bytes 1572880 | tf_op jit(solution)/shard_map/all_gather | solution.py:113
  86.9 1.8 copy.33
  89.1 32.8 %shard_map.86 = (f32[8,8,96,1]{3,2,1,0:T(8,128)S(1)}, f32[8,8,96,1]{3,2,1,0:T(8,128)}, f32[8,8,96,128]{3,2,1,0:T(8,128)}) custom-call(s32[2]{0:T(128)S(1)} %subtract_clamp_fusion.live_ref, bf16[2,8,384,128]{3,2,1,0:T(8,128)(2,1)S(1)} %bitcast.64, bf16[2,2048,2048]{2,1,0:T(8,128)(2,1)} %kv_ref.1), custom_call_target="tpu_custom_call" | custom-call | tf_op jit(solution)/shard_map/pallas_call | solution.py:68
  121.8 1.8 copy.22
  123.6 6.7 %all-to-all-start = ((f32[8,8,96,1]{2,1,3,0:T(8,128)}), f32[8,8,96,1]{2,1,3,0:T(8,128)S(1)}, u32[]{:S(2)}, u32[]{:S(2)}) async-start(f32[8,8,96,1]{2,1,3,0:T(8,128)} %copy.22), calls=%async_computation | async-start | bytes 65536 | tf_op jit(solution)/shard_map/all_to_all | solution.py:129
  130.3 0.8 constant_dynamic-slice_fusion.1
  131.1 3.0 %copy.27 = f32[8,8,96,1]{2,1,3,0:T(8,128)} copy(f32[8,8,96,1]{3,2,1,0:T(8,128)} %get-tuple-element.7) | data formatting | bytes 49152 | tf_op jit(solution)/shard_map/pallas_call | solution.py:68
  134.1 1.0 all-to-all-done
  135.0 4.0 %all-to-all-start.2 = ((f32[8,8,96,1]{2,1,3,0:T(8,128)}), f32[8,8,96,1]{2,1,3,0:T(8,128)S(1)}, u32[]{:S(2)}, u32[]{:S(2)}) async-start(f32[8,8,96,1]{2,1,3,0:T(8,128)} %copy.27), calls=%async_computation.2 | async-start | bytes 65536 | tf_op jit(solution)/shard_map/all_to_all | solution.py:130
  139.0 0.6 pad_maximum_fusion.1
  139.6 4.1 %all-to-all-done.2 = f32[8,8,96,1]{2,1,3,0:T(8,128)S(1)} async-done(((f32[8,8,96,1]{2,1,3,0:T(8,128)}), f32[8,8,96,1]{2,1,3,0:T(8,128)S(1)}, u32[]{:S(2)}, u32[]{:S(2)}) %all-to-all-start.2) | async-done | bytes 24608 | tf_op jit(solution)/shard_map/all_to_all | solution.py:130
  143.8 0.6 copy-done.4
  144.4 4.3 %all-to-all-start.1 = ((f32[8,8,96,128]{3,2,1,0:T(8,128)}), f32[8,8,96,128]{3,2,1,0:T(8,128)S(1)}, u32[]{:S(2)}, u32[]{:S(2)}) async-start(f32[8,8,96,128]{3,2,1,0:T(8,128)} %get-tuple-element.6), calls=%async_computation.1 | async-start | bytes 6291456 | tf_op jit(solution)/shard_map/all_to_all | solution.py:131
  148.6 45.4 %all_gather.15 = bf16[2,48,2048]{2,1,0:T(8,128)(2,1)S(1)} all-gather(bf16[2,48,256]{2,1,0:T(8,128)(2,1)} %pad_maximum_fusion.1), channel_id=1, replica_groups=mesh['req'=16,'seq'=8] {'seq'}, dimensions={2}, use_global_device_ids=true | all-gather | bytes 442368 | tf_op jit(solution)/shard_map/all_gather | solution.py:114
  194.1 0.7 constant_dynamic-slice_fusion.3
  194.8 1.0 reshape.77
  195.8 0.7 fusion.17
  196.6 1.6 convolution_convert_fusion
  198.2 1.0 fusion.21
  199.1 1.1 constant_dynamic-slice_fusion.2
  200.2 1.0 fusion.23
  201.3 1.3 fusion.5
  202.9 0.6 multiply_add_fusion
  203.5 1.0 multiply_reduce_fusion
  205.1 0.9 copy.35
  (32 shorter events, 1.9 us)
Async XLA Ops:
  7.2 53.5 %all-gather.3.cloned.1.call-start = ((), (), s32[]{:S(2)}) async-start(), calls=%async_computation.3 | async-start | bytes 3342336 | tf_op jit(solution)/shard_map/all_gather | solution.py:93
  7.9 79.0 %all-gather.5.cloned.1.call-start = ((), (), s32[]{:S(2)}) async-start(), calls=%async_computation.4 | async-start | bytes 1769472 | tf_op jit(solution)/shard_map/all_gather | solution.py:113
  123.6 11.4 %all-to-all-start = ((f32[8,8,96,1]{2,1,3,0:T(8,128)}), f32[8,8,96,1]{2,1,3,0:T(8,128)S(1)}, u32[]{:S(2)}, u32[]{:S(2)}) async-start(f32[8,8,96,1]{2,1,3,0:T(8,128)} %copy.22), calls=%async_computation | async-start | bytes 65536 | tf_op jit(solution)/shard_map/all_to_all | solution.py:129
  135.0 8.7 %copy-start = (f32[8,8,96,1]{2,1,3,0:T(8,128)}, f32[8,8,96,1]{2,1,3,0:T(8,128)S(1)}, u32[]{:S(2)}) copy-start(f32[8,8,96,1]{2,1,3,0:T(8,128)S(1)} %all-to-all-done) | copy-start | bytes 73732
  135.0 8.7 %all-to-all-start.2 = ((f32[8,8,96,1]{2,1,3,0:T(8,128)}), f32[8,8,96,1]{2,1,3,0:T(8,128)S(1)}, u32[]{:S(2)}, u32[]{:S(2)}) async-start(f32[8,8,96,1]{2,1,3,0:T(8,128)} %copy.27), calls=%async_computation.2 | async-start | bytes 65536 | tf_op jit(solution)/shard_map/all_to_all | solution.py:130
  143.7 0.6 copy-start.4
  143.8 52.8 %copy-start.7 = (s32[2,8]{1,0:T(2,128)S(1)}, s32[2,8]{1,0:T(2,128)}, u32[]{:S(2)}) copy-start(s32[2,8]{1,0:T(2,128)} %param.13) | copy-start | bytes 196
  144.4 59.2 %all-to-all-start.1 = ((f32[8,8,96,128]{3,2,1,0:T(8,128)}), f32[8,8,96,128]{3,2,1,0:T(8,128)S(1)}, u32[]{:S(2)}, u32[]{:S(2)}) async-start(f32[8,8,96,128]{3,2,1,0:T(8,128)} %get-tuple-element.6), calls=%async_computation.1 | async-start | bytes 6291456 | tf_op jit(solution)/shard_map/all_to_all | solution.py:131
  194.8 7.8 %copy-start.1 = (f32[8,8,96,1]{2,1,3,0:T(8,128)S(1)}, f32[8,8,96,1]{2,1,3,0:T(8,128)}, u32[]{:S(2)}) copy-start(f32[8,8,96,1]{2,1,3,0:T(8,128)} %copy-done) | copy-start | bytes 73732
  194.8 8.0 %copy-start.5 = (f32[8,8,96,1]{2,1,3,0:T(8,128)S(1)}, f32[8,8,96,1]{2,1,3,0:T(8,128)}, u32[]{:S(2)}) copy-start(f32[8,8,96,1]{2,1,3,0:T(8,128)} %copy-done.4) | copy-start | bytes 73732
  203.5 1.0 copy-start.3
  203.5 1.1 copy-start.2
  203.5 1.1 copy-start.6
Sparse Core Ops, SparseCore 0:
  10.1 50.5 all-gather.2
  63.0 23.8 all-gather.4

commit v2 on v1

--- a/solution.py
+++ b/solution.py
@@ -80,6 +80,16 @@
     )(live, q4, kv)
 
 
+def merge_pair(m, l, acc, axis):
+    top = jnp.max(m, axis=axis, keepdims=True)
+    f = jnp.exp(m - top)
+    return (
+        jnp.squeeze(top, axis),
+        jnp.sum(f * l, axis=axis),
+        jnp.sum(f[..., None] * acc, axis=axis),
+    )
+
+
 def body(queries, draft_key_value, kv_cache, cache_lengths, ancestors, dealing, accepted_path):
     local_reqs = kv_cache.shape[0]
     tree_len = queries.shape[1]
@@ -89,34 +99,37 @@
     kept_entries = jnp.einsum(
         "rit,rtc->ric", picker, draft_key_value, preferred_element_type=jnp.float32
     ).astype(jnp.bfloat16)
-    every_query, every_draft = (
-        lax.all_gather(queries, "req", axis=0, tiled=True),
-        lax.all_gather(draft_key_value, "req", axis=0, tiled=True),
-    )
-    chosen = lax.dynamic_slice_in_dim(dealing, lax.axis_index("req") * local_reqs, local_reqs)
-    own_query = jnp.stack(
-        [
-            lax.dynamic_index_in_dim(every_query, chosen[slot], 0, keepdims=False)
-            for slot in range(local_reqs)
-        ],
-        axis=0,
-    )
-    own_draft = jnp.stack(
-        [
-            lax.dynamic_index_in_dim(every_draft, chosen[slot], 0, keepdims=False)
-            for slot in range(local_reqs)
-        ],
-        axis=0,
-    )
-    seq_count = lax.axis_size("seq")
-    full_query, full_draft = (
-        lax.all_gather(own_query, "seq", axis=2, tiled=True),
-        lax.all_gather(own_draft, "seq", axis=2, tiled=True),
-    )
-    position = lax.axis_index("seq")
+
+    nz, ny, nx, nc = (lax.axis_size(a) for a in ("z", "y", "x", "c"))
+    zi, yi, xi, ci = (lax.axis_index(a) for a in ("z", "y", "x", "c"))
+    seq_count = nx * nc
+    position = xi * nc + ci
+    q_cols = queries.shape[2]
+    d_cols = draft_key_value.shape[2]
+
+    both = jnp.concatenate([queries, draft_key_value], axis=2)
+    held = lax.all_gather(both, "z", axis=0, tiled=True)
+    dest_slot = jnp.arange(ny * local_reqs, dtype=jnp.int32) + (zi * ny) * local_reqs
+    wanted = dealing[dest_slot]
+    src_group = wanted // local_reqs
+    pick = (src_group // ny) * local_reqs + wanted % local_reqs
+    send = jnp.take(held, pick, axis=0).reshape((ny, local_reqs) + both.shape[1:])
+    recv = lax.all_to_all(send, "y", 0, 0, tiled=True)
+    my_group = zi * ny + yi
+    mine = lax.dynamic_slice_in_dim(dealing, my_group * local_reqs, local_reqs)
+    from_y = (mine // local_reqs) % ny
+    recv = recv.reshape((ny * local_reqs,) + both.shape[1:])
+    own = jnp.take(recv, from_y * local_reqs + jnp.arange(local_reqs, dtype=jnp.int32), axis=0)
+
+    own = lax.all_gather(own, "x", axis=2, tiled=False)
+    own = lax.all_gather(own, "c", axis=3, tiled=False)
+    own = own.reshape(local_reqs, tree_len, seq_count, q_cols + d_cols)
+    full_query = own[..., :q_cols]
+    full_draft = own[..., q_cols:]
+
     positions = kv_cache.shape[1]
     kv_heads = kv_cache.shape[2] // (2 * HEAD_WIDTH)
-    groups = full_query.shape[2] // (HEAD_WIDTH * kv_heads)
+    groups = q_cols // HEAD_WIDTH
     rows = tree_len * groups
 
     q4 = (
@@ -126,9 +139,15 @@
     )
     live = jnp.clip(cache_lengths - position * positions, 0, positions).astype(jnp.int32)
     part_m, part_l, part_acc = local_attention(q4, kv_cache, live, seq_count)
-    recv_m = lax.all_to_all(part_m, "seq", 0, 0, tiled=True)
-    recv_l = lax.all_to_all(part_l, "seq", 0, 0, tiled=True)
-    recv_acc = lax.all_to_all(part_acc, "seq", 0, 0, tiled=True)
+    sub = part_acc.shape[2]
+    ml = jnp.stack([part_m[..., 0], part_l[..., 0]], axis=1).reshape(nx, nc, 2, kv_heads * sub)
+    acc = part_acc.reshape(nx, nc, kv_heads * sub, HEAD_WIDTH)
+    ml = lax.all_to_all(ml, "c", 1, 1, tiled=True)
+    acc = lax.all_to_all(acc, "c", 1, 1, tiled=True)
+    m1, l1, a1 = merge_pair(ml[:, :, 0], ml[:, :, 1], acc, axis=1)
+    ml = jnp.stack([m1, l1], axis=1)
+    ml = lax.all_to_all(ml, "x", 0, 0, tiled=True)
+    acc = lax.all_to_all(a1, "x", 0, 0, tiled=True)
 
     per_slot = seq_count // local_reqs
     tok = tree_len // per_slot
@@ -154,17 +173,16 @@
     od = jnp.einsum(
         "ktgj,jkd->ktgd", wd.astype(jnp.bfloat16), d_slot[:, :, 1], preferred_element_type=jnp.float32
     )
-    md = md.reshape(kv_heads, tok * groups)
-    ld = ld.reshape(kv_heads, tok * groups)
-    od = od.reshape(kv_heads, tok * groups, HEAD_WIDTH)
-
-    rm = recv_m[..., 0]
-    rl = recv_l[..., 0]
-    top = jnp.maximum(jnp.max(rm, axis=0), md)
-    fr = jnp.exp(rm - top[None])
-    fd = jnp.exp(md - top)
-    den = jnp.sum(fr * rl, axis=0) + fd * ld
-    num = jnp.sum(fr[..., None] * recv_acc, axis=0) + fd[..., None] * od
+    md = md.reshape(1, kv_heads * sub)
+    ld = ld.reshape(1, kv_heads * sub)
+    od = od.reshape(1, kv_heads * sub, HEAD_WIDTH)
+
+    _, den, num = merge_pair(
+        jnp.concatenate([ml[:, 0], md], axis=0),
+        jnp.concatenate([ml[:, 1], ld], axis=0),
+        jnp.concatenate([acc, od], axis=0),
+        axis=0,
+    )
     res = num / den[..., None]
     context = (
         res.reshape(kv_heads, tok, groups, HEAD_WIDTH)
@@ -176,19 +194,26 @@
 
 
 def solution(mesh):
+    req, seq = mesh.shape["req"], mesh.shape["seq"]
+    nc = 2
+    nx = seq // nc
+    ny = int(round(req ** 0.5))
+    nz = req // ny
+    fine = jax.sharding.Mesh(mesh.devices.reshape(nz, ny, nx, nc), ("z", "y", "x", "c"))
+    R, S = ("z", "y"), ("x", "c")
     placed = (
-        P("req", None, "seq"),
-        P("req", None, "seq"),
-        P("req", "seq", None),
-        P("req"),
-        P("req", None, None),
+        P(R, None, S),
+        P(R, None, S),
+        P(R, S, None),
+        P(R),
+        P(R, None, None),
         P(),
-        P("req", None),
+        P(R, None),
     )
     return jax.shard_map(
         body,
-        mesh=mesh,
+        mesh=fine,
         in_specs=placed,
-        out_specs=(P(("req", "seq"), None), P("req", None, "seq")),
+        out_specs=(P(R + S, None), P(R, None, S)),
         check_vma=False,
     )

time: 214 us -> 174 us (0.81)
  blocking collectives: 65.8 us -> 31 us
  waiting for transfers between devices: 56.8 us -> 48.1 us
  other arithmetic: 5.74 us -> 11.6 us
  between operations: 18.1 us -> 14.4 us
    all_gather x2, blocking collectives: 65.8 us -> 27.4 us  [the longest x1 15 us: body(): held = lax.all_gather(both, 'z', axis=0, tiled=True)]
    all_gather x2 -> x1, waiting for transfers between devices: 51 us -> 15.3 us  [body(): own = lax.all_gather(own, 'c', axis=3, tiled=False)]
    all_to_all x3 -> x4, waiting for transfers between devices: 5.08 us -> 32.8 us  [the longest x1 17.5 us: body(): acc = lax.all_to_all(a1, 'x', 0, 0, tiled=True)]
    reshape x1 -> x4, local copies, waits for them, and re-layouts: 0.08 us -> 5.22 us  [the longest x1 3.17 us: body(): own = own.reshape(local_reqs, tree_len, seq_count, q_cols + d_cols)]
    pallas_call x2 -> x0, local copies, waits for them, and re-layouts: 4.8 us -> none  [local_attention(): pl.pallas_call(kern, grid_spec=grid_spec, out_shape=[jax.ShapeDtypeStruct...]
    all_gather x0 -> x1, local copies, waits for them, and re-layouts: none -> 4.34 us  [body(): own = lax.all_gather(own, 'c', axis=3, tiled=False)]
    pallas_call x0 -> x2, other arithmetic: none -> 4.33 us  [local_attention(): pl.pallas_call(kern, grid_spec=grid_spec, out_shape=[jax.ShapeDtypeStruct...]
    dynamic_slice x5 -> x0, local copies, waits for them, and re-layouts: 4.2 us -> none  [the longest x1 1.07 us: body(): lax.dynamic_slice_in_dim(q_slot, my_tok0, tok, 0)]
  transfers between devices with their start and end apart: 5 -> 5, of which waited for: 4 -> 5; matrix products, arithmetic and copies ran while one was open for 7% -> 4% of each run, Pallas kernels for 0% -> 0%
where the time goes in v2:
time: 174 us; the launch traced here: 172 us
  waiting for transfers between devices  48.1 us (28%)
  Pallas kernels  32.8 us (19%)
  blocking collectives  31 us (18%)
  local copies, waits for them, and re-layouts  16.4 us (9%)
  starting transfers between devices  16.1 us (9%)
  between operations  14.4 us (8%)
  other arithmetic  11.6 us (7%)
    pallas_call x1, Pallas kernels, local_attention(): pl.pallas_call(kern, grid_spec=grid_spec, out_shape=[jax.ShapeDtypeStruct...  32.8 us
    all_to_all x1, waiting for transfers between devices, body(): acc = lax.all_to_all(a1, 'x', 0, 0, tiled=True)  17.5 us
    all_gather x1, waiting for transfers between devices, body(): own = lax.all_gather(own, 'c', axis=3, tiled=False)  15.3 us
    all_gather x1, blocking collectives, body(): held = lax.all_gather(both, 'z', axis=0, tiled=True)  15 us
    all_gather x1, blocking collectives, body(): own = lax.all_gather(own, 'x', axis=2, tiled=False)  12.4 us
    all_to_all x1, waiting for transfers between devices, body(): recv = lax.all_to_all(send, 'y', 0, 0, tiled=True)  11.5 us
    all_gather x1, local copies, waits for them, and re-layouts, body(): own = lax.all_gather(own, 'c', axis=3, tiled=False)  4.34 us
    pallas_call x2, other arithmetic, local_attention(): pl.pallas_call(kern, grid_spec=grid_spec, out_shape=[jax.ShapeDtypeStruct...  4.33 us
  transfers between devices with their start and end apart: 5, of which 5 were waited for; matrix products, arithmetic and copies ran while one was open for 4% of the time, Pallas kernels for 0%

profile of v2, /device:TPU:1, one launch (start us, length us, event | category | flops | bytes accessed | tf_op | source)
XLA Modules:
  0.0 171.7 jit_solution(11187767758154198180)
XLA Ops:
  7.2 1.3 gather_fusion
  8.6 1.0 pad_maximum_fusion
  9.6 15.0 %all_gather.13 = bf16[8,48,1280]{2,1,0:T(8,128)(2,1)S(1)} all-gather(bf16[2,48,1280]{2,1,0:T(8,128)(2,1)S(1)} %pad_maximum_fusion), channel_id=1, replica_groups=mesh['z'=4,'y'=4,'x'=4,'c'=2] {'z'}, dimensions={0}, use_global_device_ids=true | all-gather | bytes 1228800 | tf_op jit(solution)/shard_map/all_gather | solution.py:111
  24.6 0.6 gather_fusion.1
  25.2 1.1 broadcast_select_fusion
  26.3 4.2 %all-to-all-start = ((bf16[4,2,48,1280]{3,2,1,0:T(8,128)(2,1)}), bf16[4,2,48,1280]{3,2,1,0:T(8,128)(2,1)S(1)}, u32[]{:S(2)}, u32[]{:S(2)}) async-start(bf16[4,2,48,1280]{3,2,1,0:T(8,128)(2,1)} %broadcast_select_fusion), calls=%async_computation | async-start | bytes 1966080 | tf_op jit(solution)/shard_map/all_to_all | solution.py:117
  30.7 11.5 %all-to-all-done = bf16[4,2,48,1280]{3,2,1,0:T(8,128)(2,1)S(1)} async-done(((bf16[4,2,48,1280]{3,2,1,0:T(8,128)(2,1)}), bf16[4,2,48,1280]{3,2,1,0:T(8,128)(2,1)S(1)}, u32[]{:S(2)}, u32[]{:S(2)}) %all-to-all-start) | async-done | bytes 983072 | tf_op jit(solution)/shard_map/all_to_all | solution.py:117
  42.3 0.6 gather_fusion.2
  42.9 12.4 %all_gather.14 = bf16[2,48,4,1280]{3,1,0,2:T(8,128)(2,1)} all-gather(bf16[2,48,1,1280]{3,1,0,2:T(8,128)(2,1)S(1)} %bitcast_select_fusion), channel_id=1, replica_groups=mesh['z'=4,'y'=4,'x'=4,'c'=2] {'x'}, dimensions={2}, use_global_device_ids=true | all-gather | bytes 1228800 | tf_op jit(solution)/shard_map/all_gather | solution.py:124
  55.4 0.7 fusion.16
  56.1 0.8 convolution_convert_fusion
  56.9 15.3 %all-gather.3.cloned.1.call-done = bf16[2,48,4,2560]{3,1,0,2:T(8,128)(2,1)} async-done(((bf16[2,48,4,1280]{3,1,0,2:T(8,128)(2,1)}), bf16[2,48,4,2560]{3,1,0,2:T(8,128)(2,1)}) %all-gather.3.cloned.1.call-update) | async-done | bytes 1966096 | tf_op jit(solution)/shard_map/all_gather | solution.py:125
  72.2 4.3 %copy.29 = bf16[2,48,4,2560]{3,2,1,0:T(4,128)(2,1)} copy(bf16[2,48,4,2560]{3,1,0,2:T(8,128)(2,1)} %all-gather.3.cloned.1.call-done) | data formatting | bytes 3932160 | tf_op jit(solution)/shard_map/all_gather | solution.py:125
  76.6 3.2 %reshape.274 = bf16[2,48,8,1280]{3,2,1,0:T(8,128)(2,1)S(1)} reshape(bf16[2,48,4,2560]{3,2,1,0:T(4,128)(2,1)} %copy.29) | data formatting | bytes 3932160 | tf_op jit(solution)/shard_map/reshape | solution.py:126
  79.8 1.7 slice_bitcast_fusion.1
  81.8 32.8 %shard_map.86 = (f32[8,8,96,1]{3,2,1,0:T(8,128)S(1)}, f32[8,8,96,1]{3,2,1,0:T(8,128)}, f32[8,8,96,128]{3,2,1,0:T(8,128)}) custom-call(s32[2]{0:T(128)S(1)} %subtract_clamp_fusion.live_ref, bf16[2,8,384,128]{3,2,1,0:T(8,128)(2,1)S(1)} %bitcast.87, bf16[2,2048,2048]{2,1,0:T(8,128)(2,1)} %kv_ref.1), custom_call_target="tpu_custom_call" | custom-call | tf_op jit(solution)/shard_map/pallas_call | solution.py:68
  114.5 1.1 reduce.4
  115.7 3.2 %reduce.5 = f32[8,8,96]{2,1,0:T(8,128)S(1)} reduce(f32[8,8,96,1]{3,2,1,0:T(8,128)} %get-tuple-element.6, f32[]{:T(128)} %constant.194), dimensions={3}, to_apply=%get-tuple-element.6.reduce_sub_computation | reduce | bytes 49156 | tf_op jit(solution)/shard_map/pallas_call | solution.py:68
  119.1 3.6 %all_to_all.25 = f32[4,2,2,768]{3,0,2,1:T(4,128)S(1)} all-to-all(f32[4,2,2,768]{3,0,2,1:T(4,128)S(1)} %copy.31), channel_id=1, replica_groups=mesh['z'=4,'y'=4,'x'=4,'c'=2] {'c'}, dimensions={1} | all-to-all | bytes 98304 | tf_op jit(solution)/shard_map/all_to_all | solution.py:145
  122.8 1.9 %copy.36 = f32[4,2,768,128]{3,2,0,1:T(8,128)} copy(f32[4,2,768,128]{3,2,1,0:T(8,128)S(1)} %bitcast.89) | data formatting | bytes 6291456 | tf_op jit(solution)/shard_map/reshape | solution.py:144
  124.7 4.3 %all-to-all-start.3 = ((f32[4,2,768,128]{3,2,0,1:T(8,128)}), f32[4,2,768,128]{3,2,0,1:T(8,128)S(1)}, u32[]{:S(2)}, u32[]{:S(2)}) async-start(f32[4,2,768,128]{3,2,0,1:T(8,128)} %copy.36), calls=%async_computation.3 | async-start | bytes 6291456 | tf_op jit(solution)/shard_map/all_to_all | solution.py:146
  129.0 0.6 pad_maximum_fusion.2
  129.6 2.6 %all-to-all-done.3 = f32[4,2,768,128]{3,2,0,1:T(8,128)S(1)} async-done(((f32[4,2,768,128]{3,2,0,1:T(8,128)}), f32[4,2,768,128]{3,2,0,1:T(8,128)S(1)}, u32[]{:S(2)}, u32[]{:S(2)}) %all-to-all-start.3) | async-done | bytes 3145760 | tf_op jit(solution)/shard_map/all_to_all | solution.py:146
  132.3 4.1 %all-to-all-start.2 = ((f32[4,2,768]{2,1,0:T(2,128)}), f32[4,2,768]{2,1,0:T(2,128)S(1)}, u32[]{:S(2)}, u32[]{:S(2)}) async-start(f32[4,2,768]{2,1,0:T(2,128)} %pad_maximum_fusion.2), calls=%async_computation.2 | async-start | bytes 49152 | tf_op jit(solution)/shard_map/all_to_all | solution.py:149
  136.3 2.2 %multiply_reduce_fusion = f32[4,768,128]{2,1,0:T(8,128)} fusion(f32[4,2,768,128]{3,2,0,1:T(8,128)S(1)} %all-to-all-done.3, f32[4,2,768]{2,0,1:T(4,128)S(1)} %get-tuple-element.9), kind=kLoop, calls=%fused_computation.3 | loop fusion | flops 1179648 | bytes 4743168 | tf_op jit(solution)/shard_map/reduce_sum | solution.py:89
  138.5 0.9 dynamic-slice_bitcast_fusion.1
  139.5 1.1 all-to-all-done.2
  140.6 3.6 %all-to-all-start.4 = ((f32[4,768,128]{2,1,0:T(8,128)}), f32[4,768,128]{2,1,0:T(8,128)S(1)}, u32[]{:S(2)}, u32[]{:S(2)}) async-start(f32[4,768,128]{2,1,0:T(8,128)} %multiply_reduce_fusion), calls=%async_computation.4 | async-start | bytes 3145728 | tf_op jit(solution)/shard_map/all_to_all | solution.py:150
  144.7 0.3 fusion.2
  145.6 17.5 %all-to-all-done.4 = f32[4,768,128]{2,1,0:T(8,128)S(1)} async-done(((f32[4,768,128]{2,1,0:T(8,128)}), f32[4,768,128]{2,1,0:T(8,128)S(1)}, u32[]{:S(2)}, u32[]{:S(2)}) %all-to-all-start.4) | async-done | bytes 1572896 | tf_op jit(solution)/shard_map/all_to_all | solution.py:150
  163.1 0.7 fusion
  164.0 0.9 copy.48
  (46 shorter events, 2.3 us)
Async XLA Ops:
  25.2 5.4 %copy-start = (s32[32]{0:T(128)S(1)}, s32[32]{0:T(128)}, u32[]{:S(2)}) copy-start(s32[32]{0:T(128)} %param.12) | copy-start | bytes 388
  26.3 15.9 %all-to-all-start = ((bf16[4,2,48,1280]{3,2,1,0:T(8,128)(2,1)}), bf16[4,2,48,1280]{3,2,1,0:T(8,128)(2,1)S(1)}, u32[]{:S(2)}, u32[]{:S(2)}) async-start(bf16[4,2,48,1280]{3,2,1,0:T(8,128)(2,1)} %broadcast_select_fusion), calls=%async_computation | async-start | bytes 1966080 | tf_op jit(solution)/shard_map/all_to_all | solution.py:117
  30.5 25.6 %copy-start.4 = (s32[2]{0:T(128)S(1)}, s32[2]{0:T(128)}, u32[]{:S(2)}) copy-start(s32[2]{0:T(128)} %param.10) | copy-start | bytes 28
  30.5 25.6 %copy-start.2 = (bf16[2,48,256]{2,1,0:T(8,128)(2,1)S(1)}, bf16[2,48,256]{2,1,0:T(8,128)(2,1)}, u32[]{:S(2)}) copy-start(bf16[2,48,256]{2,1,0:T(8,128)(2,1)} %param.8) | copy-start | bytes 147460
  30.5 25.6 %copy-start.3 = (s32[2,8]{1,0:T(2,128)S(1)}, s32[2,8]{1,0:T(2,128)}, u32[]{:S(2)}) copy-start(s32[2,8]{1,0:T(2,128)} %param.13) | copy-start | bytes 196
  30.5 41.7 %all-gather.3.cloned.1.call-start = ((), (), s32[]{:S(2)}) async-start(), calls=%async_computation.5 | async-start | bytes 2949120 | tf_op jit(solution)/shard_map/all_gather | solution.py:125
  115.7 7.2 %copy-start.1 = (f32[8,8,96,128]{3,2,1,0:T(8,128)S(1)}, f32[8,8,96,128]{3,2,1,0:T(8,128)}, u32[]{:S(2)}) copy-start(f32[8,8,96,128]{3,2,1,0:T(8,128)} %get-tuple-element.7) | copy-start | bytes 9437188
  124.7 7.5 %all-to-all-start.3 = ((f32[4,2,768,128]{3,2,0,1:T(8,128)}), f32[4,2,768,128]{3,2,0,1:T(8,128)S(1)}, u32[]{:S(2)}, u32[]{:S(2)}) async-start(f32[4,2,768,128]{3,2,0,1:T(8,128)} %copy.36), calls=%async_computation.3 | async-start | bytes 6291456 | tf_op jit(solution)/shard_map/all_to_all | solution.py:146
  132.3 8.3 %all-to-all-start.2 = ((f32[4,2,768]{2,1,0:T(2,128)}), f32[4,2,768]{2,1,0:T(2,128)S(1)}, u32[]{:S(2)}, u32[]{:S(2)}) async-start(f32[4,2,768]{2,1,0:T(2,128)} %pad_maximum_fusion.2), calls=%async_computation.2 | async-start | bytes 49152 | tf_op jit(solution)/shard_map/all_to_all | solution.py:149
  140.6 22.5 %all-to-all-start.4 = ((f32[4,768,128]{2,1,0:T(8,128)}), f32[4,768,128]{2,1,0:T(8,128)S(1)}, u32[]{:S(2)}, u32[]{:S(2)}) async-start(f32[4,768,128]{2,1,0:T(8,128)} %multiply_reduce_fusion), calls=%async_computation.4 | async-start | bytes 3145728 | tf_op jit(solution)/shard_map/all_to_all | solution.py:150
Sparse Core Ops, SparseCore 0:
  55.5 16.7 all-gather.2

commit v3 on v2

--- a/solution.py
+++ b/solution.py
@@ -12,57 +12,90 @@
 NEG = -1e30
 
 
-def attn_kernel(live_ref, q_ref, kv_ref, m_ref, l_ref, acc_ref, *, n_blk, scale):
+def attn_kernel(live_ref, q_ref, kv_ref, m_ref, l_ref, acc_ref, m_sc, l_sc, acc_sc,
+                *, n_blk, scale, groups):
     slot = pl.program_id(0)
     live = live_ref[slot]
-    q = q_ref[...]
-    run_m = run_l = run_acc = None
-    for b in range(n_blk):
+    q = jnp.concatenate(
+        [q_ref[:, g * HEAD_WIDTH:(g + 1) * HEAD_WIDTH] for g in range(groups)], axis=0
+    )
+    m_sc[...] = jnp.full(m_sc.shape, NEG, jnp.float32)
+    l_sc[...] = jnp.zeros(l_sc.shape, jnp.float32)
+    acc_sc[...] = jnp.zeros(acc_sc.shape, jnp.float32)
+
+    def absorb(b, masked):
         keys = kv_ref[b * BLK:(b + 1) * BLK, 0:HEAD_WIDTH]
         vals = kv_ref[b * BLK:(b + 1) * BLK, HEAD_WIDTH:2 * HEAD_WIDTH]
         s = lax.dot_general(
             q, keys, (((1,), (1,)), ((), ())), preferred_element_type=jnp.float32
         ) * scale
-        pos = b * BLK + lax.broadcasted_iota(jnp.int32, (1, BLK), 1)
-        allowed = pos < live
-        s = jnp.where(allowed, s, jnp.float32(NEG))
+        if masked:
+            pos = b * BLK + lax.broadcasted_iota(jnp.int32, (1, BLK), 1)
+            allowed = pos < live
+            s = jnp.where(allowed, s, jnp.float32(NEG))
         mb = jnp.max(s, axis=1, keepdims=True)
-        w = jnp.where(allowed, jnp.exp(s - mb), jnp.float32(0.0))
+        w = jnp.exp(s - mb)
+        if masked:
+            w = jnp.where(allowed, w, jnp.float32(0.0))
         lb = jnp.sum(w, axis=1, keepdims=True)
         ob = jnp.dot(w.astype(jnp.bfloat16), vals, preferred_element_type=jnp.float32)
-        if run_m is None:
-            run_m, run_l, run_acc = mb, lb, ob
-        else:
-            new_m = jnp.maximum(run_m, mb)
-            fa = jnp.exp(run_m - new_m)
-            fb = jnp.exp(mb - new_m)
-            run_l = run_l * fa + lb * fb
-            run_acc = run_acc * fa + ob * fb
-            run_m = new_m
+        m_old = m_sc[...]
+        new_m = jnp.maximum(m_old, mb)
+        fa = jnp.exp(m_old - new_m)
+        fb = jnp.exp(mb - new_m)
+        l_sc[...] = l_sc[...] * fa + lb * fb
+        acc_sc[...] = acc_sc[...] * fa + ob * fb
+        m_sc[...] = new_m
+
+    for b in range(n_blk):
+        lo, hi = b * BLK, (b + 1) * BLK
+
+        @pl.when(live >= hi)
+        def _full():
+            absorb(b, False)
+
+        @pl.when(jnp.logical_and(live > lo, live < hi))
+        def _part():
+            absorb(b, True)
+
     parts = m_ref.shape[0]
-    rows = q.shape[0] // parts
-    m_ref[...] = run_m.reshape(parts, rows, 1)
-    l_ref[...] = run_l.reshape(parts, rows, 1)
-    acc_ref[...] = run_acc.reshape(parts, rows, HEAD_WIDTH)
-
-
-def local_attention(q4, kv, live, seq_count):
-    slots, kvh, rows, _ = q4.shape
+    tree_len = q_ref.shape[0]
+    tok = tree_len // parts
+    for j in range(parts):
+        for g in range(groups):
+            src = slice(g * tree_len + j * tok, g * tree_len + (j + 1) * tok)
+            dst = slice(g * tok, (g + 1) * tok)
+            m_ref[j, dst, :] = m_sc[src, :]
+            l_ref[j, dst, :] = l_sc[src, :]
+            acc_ref[j, dst, :] = acc_sc[src, :]
+
+
+def local_attention(q_all, kv, live, seq_count):
+    slots, kvh, tree_len, _ = q_all.shape
     positions = kv.shape[1]
+    groups = (q_all.shape[3] - 2 * HEAD_WIDTH) // HEAD_WIDTH
+    rows = tree_len * groups
     per_slot = seq_count // slots
     sub = rows // per_slot
-    kern = functools.partial(attn_kernel, n_blk=positions // BLK, scale=HEAD_WIDTH ** (-0.5))
+    kern = functools.partial(
+        attn_kernel, n_blk=positions // BLK, scale=HEAD_WIDTH ** (-0.5), groups=groups
+    )
     grid_spec = pltpu.PrefetchScalarGridSpec(
         num_scalar_prefetch=1,
         grid=(slots, kvh),
         in_specs=[
-            pl.BlockSpec((None, None, rows, HEAD_WIDTH), lambda i, k, lv: (i, k, 0, 0)),
+            pl.BlockSpec((None, None, tree_len, groups * HEAD_WIDTH), lambda i, k, lv: (i, k, 0, 0)),
             pl.BlockSpec((None, positions, 2 * HEAD_WIDTH), lambda i, k, lv: (i, 0, k)),
         ],
         out_specs=[
             pl.BlockSpec((per_slot, None, sub, 1), lambda i, k, lv: (i, k, 0, 0)),
             pl.BlockSpec((per_slot, None, sub, 1), lambda i, k, lv: (i, k, 0, 0)),
             pl.BlockSpec((per_slot, None, sub, HEAD_WIDTH), lambda i, k, lv: (i, k, 0, 0)),
+        ],
+        scratch_shapes=[
+            pltpu.VMEM((rows, 1), jnp.float32),
+            pltpu.VMEM((rows, 1), jnp.float32),
+            pltpu.VMEM((rows, HEAD_WIDTH), jnp.float32),
         ],
     )
     return pl.pallas_call(
@@ -77,7 +110,7 @@
             dimension_semantics=("arbitrary", "arbitrary"),
             vmem_limit_bytes=48 * 1024 * 1024,
         ),
-    )(live, q4, kv)
+    )(live, q_all, kv)
 
 
 def merge_pair(m, l, acc, axis):
@@ -121,24 +154,15 @@
     recv = recv.reshape((ny * local_reqs,) + both.shape[1:])
     own = jnp.take(recv, from_y * local_reqs + jnp.arange(local_reqs, dtype=jnp.int32), axis=0)
 
-    own = lax.all_gather(own, "x", axis=2, tiled=False)
-    own = lax.all_gather(own, "c", axis=3, tiled=False)
-    own = own.reshape(local_reqs, tree_len, seq_count, q_cols + d_cols)
-    full_query = own[..., :q_cols]
-    full_draft = own[..., q_cols:]
+    own = lax.all_gather(own, "x", axis=1, tiled=False)
+    own = lax.all_gather(own, "c", axis=2, tiled=False)
+    q_all = own.reshape(local_reqs, seq_count, tree_len, q_cols + d_cols)
 
     positions = kv_cache.shape[1]
     kv_heads = kv_cache.shape[2] // (2 * HEAD_WIDTH)
     groups = q_cols // HEAD_WIDTH
-    rows = tree_len * groups
-
-    q4 = (
-        full_query.reshape(local_reqs, tree_len, kv_heads, groups, HEAD_WIDTH)
-        .transpose(0, 2, 1, 3, 4)
-        .reshape(local_reqs, kv_heads, rows, HEAD_WIDTH)
-    )
     live = jnp.clip(cache_lengths - position * positions, 0, positions).astype(jnp.int32)
-    part_m, part_l, part_acc = local_attention(q4, kv_cache, live, seq_count)
+    part_m, part_l, part_acc = local_attention(q_all, kv_cache, live, seq_count)
     sub = part_acc.shape[2]
     ml = jnp.stack([part_m[..., 0], part_l[..., 0]], axis=1).reshape(nx, nc, 2, kv_heads * sub)
     acc = part_acc.reshape(nx, nc, kv_heads * sub, HEAD_WIDTH)
@@ -146,32 +170,32 @@
     acc = lax.all_to_all(acc, "c", 1, 1, tiled=True)
     m1, l1, a1 = merge_pair(ml[:, :, 0], ml[:, :, 1], acc, axis=1)
     ml = jnp.stack([m1, l1], axis=1)
+    x1 = jnp.where(l1[..., None] > 0, a1 / l1[..., None], jnp.float32(0.0)).astype(jnp.bfloat16)
     ml = lax.all_to_all(ml, "x", 0, 0, tiled=True)
-    acc = lax.all_to_all(a1, "x", 0, 0, tiled=True)
+    x1 = lax.all_to_all(x1, "x", 0, 0, tiled=True)
+    acc = x1.astype(jnp.float32) * ml[:, 1][..., None]
 
     per_slot = seq_count // local_reqs
     tok = tree_len // per_slot
     my_slot = position // per_slot
     my_tok0 = (position % per_slot) * tok
-    q_slot = lax.dynamic_index_in_dim(full_query, my_slot, 0, keepdims=False)
-    q_mine = lax.dynamic_slice_in_dim(q_slot, my_tok0, tok, 0).reshape(
-        tok, kv_heads, groups, HEAD_WIDTH
-    )
-    d_slot = lax.dynamic_index_in_dim(full_draft, my_slot, 0, keepdims=False).reshape(
-        tree_len, kv_heads, 2, HEAD_WIDTH
-    )
+    mine_all = lax.dynamic_index_in_dim(q_all, my_slot, 0, keepdims=False)
+    q_mine = lax.dynamic_slice_in_dim(mine_all[..., :q_cols], my_tok0, tok, 1).reshape(
+        kv_heads, tok, groups, HEAD_WIDTH
+    )
+    d_slot = mine_all[..., q_cols:].reshape(kv_heads, tree_len, 2, HEAD_WIDTH)
     anc = lax.dynamic_index_in_dim(ancestors, my_slot, 0, keepdims=False)
     anc = lax.dynamic_slice_in_dim(anc, my_tok0, tok, 0)
-    allowed = (anc > 0)[None, :, None, :]
+    allowed = (anc > 0)[None, None, :, :]
     sd = jnp.einsum(
-        "tkgd,jkd->ktgj", q_mine, d_slot[:, :, 0], preferred_element_type=jnp.float32
+        "ktgd,kjd->kgtj", q_mine, d_slot[:, :, 0], preferred_element_type=jnp.float32
     ) * HEAD_WIDTH ** (-0.5)
     sd = jnp.where(allowed, sd, jnp.float32(NEG))
     md = jnp.max(sd, axis=-1)
     wd = jnp.where(allowed, jnp.exp(sd - md[..., None]), jnp.float32(0.0))
     ld = jnp.sum(wd, axis=-1)
     od = jnp.einsum(
-        "ktgj,jkd->ktgd", wd.astype(jnp.bfloat16), d_slot[:, :, 1], preferred_element_type=jnp.float32
+        "kgtj,kjd->kgtd", wd.astype(jnp.bfloat16), d_slot[:, :, 1], preferred_element_type=jnp.float32
     )
     md = md.reshape(1, kv_heads * sub)
     ld = ld.reshape(1, kv_heads * sub)
@@ -185,8 +209,8 @@
     )
     res = num / den[..., None]
     context = (
-        res.reshape(kv_heads, tok, groups, HEAD_WIDTH)
-        .transpose(1, 0, 2, 3)
+        res.reshape(kv_heads, groups, tok, HEAD_WIDTH)
+        .transpose(2, 0, 1, 3)
         .reshape(tok, kv_heads * groups * HEAD_WIDTH)
         .astype(jnp.bfloat16)
     )

time: 174 us -> 183 us (1.052)
  blocking collectives: 31 us -> 42.3 us
  waiting for transfers between devices: 48.1 us -> 38.8 us
  Pallas kernels: 32.8 us -> 39.3 us
  other arithmetic: 11.6 us -> 16.5 us
  local copies, waits for them, and re-layouts: 16.4 us -> 12.3 us
    all_to_all x1, blocking collectives: 3.64 us -> 15 us  [body(): ml = lax.all_to_all(ml, 'c', 1, 1, tiled=True)]
    all_to_all x1, waiting for transfers between devices: 17.5 us -> 10.1 us  [body(): x1 = lax.all_to_all(x1, 'x', 0, 0, tiled=True)]
    pallas_call x1, Pallas kernels: 32.8 us -> 39.3 us  [local_attention(): pl.pallas_call(kern, grid_spec=grid_spec, out_shape=[jax.ShapeDtypeStruct...]
    reshape x4 -> x3, local copies, waits for them, and re-layouts: 5.12 us -> 0.24 us  [the longest x1 0.15 us: body(): lax.dynamic_slice_in_dim(mine_all[..., :q_cols], my_tok0, tok, 1)]
    all_gather x1 -> x0, local copies, waits for them, and re-layouts: 4.34 us -> none  [body(): own = lax.all_gather(own, 'c', axis=3, tiled=False)]
    convert_element_type x0 -> x2, other arithmetic: none -> 2.36 us  [the longest x1 2.15 us: body(): jnp.where(l1[..., None] > 0, a1 / l1[..., None], jnp.float32(0.0))]
    reshape x1, local copies, waits for them, and re-layouts: 1.88 us -> 3.82 us  [body(): acc = part_acc.reshape(nx, nc, kv_heads * sub, HEAD_WIDTH)]
  transfers between devices with their start and end apart: 5 -> 5, of which waited for: 5 -> 4; matrix products, arithmetic and copies ran while one was open for 4% -> 5% of each run, Pallas kernels for 0% -> 0%
where the time goes in v3:
time: 183 us; the launch traced here: 182 us
  blocking collectives  42.3 us (23%)
  Pallas kernels  39.3 us (21%)
  waiting for transfers between devices  38.8 us (21%)
  other arithmetic  16.5 us (9%)
  starting transfers between devices  16.5 us (9%)
  between operations  14.4 us (8%)
  local copies, waits for them, and re-layouts  12.3 us (7%)
    pallas_call x1, Pallas kernels, local_attention(): pl.pallas_call(kern, grid_spec=grid_spec, out_shape=[jax.ShapeDtypeStruct...  39.3 us
    all_gather x1, waiting for transfers between devices, body(): own = lax.all_gather(own, 'c', axis=2, tiled=False)  15.3 us
    all_gather x1, blocking collectives, body(): held = lax.all_gather(both, 'z', axis=0, tiled=True)  15 us
    all_to_all x1, blocking collectives, body(): ml = lax.all_to_all(ml, 'c', 1, 1, tiled=True)  15 us
    all_gather x1, blocking collectives, body(): own = lax.all_gather(own, 'x', axis=1, tiled=False)  12.4 us
    all_to_all x1, waiting for transfers between devices, body(): recv = lax.all_to_all(send, 'y', 0, 0, tiled=True)  11.5 us
    all_to_all x1, waiting for transfers between devices, body(): x1 = lax.all_to_all(x1, 'x', 0, 0, tiled=True)  10.1 us
    all_to_all x1, starting transfers between devices, body(): acc = lax.all_to_all(acc, 'c', 1, 1, tiled=True)  4.28 us
  transfers between devices with their start and end apart: 5, of which 4 were waited for; matrix products, arithmetic and copies ran while one was open for 5% of the time, Pallas kernels for 0%

profile of v3, /device:TPU:1, one launch (start us, length us, event | category | flops | bytes accessed | tf_op | source)
XLA Modules:
  0.0 181.7 jit_solution(12889476575319932108)
XLA Ops:
  7.2 1.3 gather_fusion
  8.6 1.0 pad_maximum_fusion
  9.6 15.0 %all_gather.13 = bf16[8,48,1280]{2,1,0:T(8,128)(2,1)S(1)} all-gather(bf16[2,48,1280]{2,1,0:T(8,128)(2,1)S(1)} %pad_maximum_fusion), channel_id=1, replica_groups=mesh['z'=4,'y'=4,'x'=4,'c'=2] {'z'}, dimensions={0}, use_global_device_ids=true | all-gather | bytes 1228800 | tf_op jit(solution)/shard_map/all_gather | solution.py:144
  24.6 0.6 gather_fusion.1
  25.2 1.1 broadcast_select_fusion
  26.3 4.2 %all-to-all-start = ((bf16[4,2,48,1280]{3,2,1,0:T(8,128)(2,1)}), bf16[4,2,48,1280]{3,2,1,0:T(8,128)(2,1)S(1)}, u32[]{:S(2)}, u32[]{:S(2)}) async-start(bf16[4,2,48,1280]{3,2,1,0:T(8,128)(2,1)} %broadcast_select_fusion), calls=%async_computation | async-start | bytes 1966080 | tf_op jit(solution)/shard_map/all_to_all | solution.py:150
  30.7 11.5 %all-to-all-done = bf16[4,2,48,1280]{3,2,1,0:T(8,128)(2,1)S(1)} async-done(((bf16[4,2,48,1280]{3,2,1,0:T(8,128)(2,1)}), bf16[4,2,48,1280]{3,2,1,0:T(8,128)(2,1)S(1)}, u32[]{:S(2)}, u32[]{:S(2)}) %all-to-all-start) | async-done | bytes 983072 | tf_op jit(solution)/shard_map/all_to_all | solution.py:150
  42.9 12.4 %all_gather.14 = bf16[2,4,48,1280]{3,2,1,0:T(8,128)(2,1)} all-gather(bf16[2,1,48,1280]{3,2,1,0:T(8,128)(2,1)S(1)} %bitcast_select_fusion), channel_id=1, replica_groups=mesh['z'=4,'y'=4,'x'=4,'c'=2] {'x'}, dimensions={1}, use_global_device_ids=true | all-gather | bytes 1228800 | tf_op jit(solution)/shard_map/all_gather | solution.py:157
  55.4 0.7 fusion.17
  56.1 0.8 convolution_convert_fusion
  56.9 15.3 %all-gather.3.cloned.1.call-done = bf16[2,4,96,1280]{3,2,1,0:T(8,128)(2,1)} async-done(((bf16[2,4,48,1280]{3,2,1,0:T(8,128)(2,1)}), bf16[2,4,96,1280]{3,2,1,0:T(8,128)(2,1)}) %all-gather.3.cloned.1.call-update) | async-done | bytes 1966096 | tf_op jit(solution)/shard_map/all_gather | solution.py:158
  72.2 1.4 dynamic-slice_bitcast_fusion
  74.0 39.3 %shard_map.86 = (f32[8,8,96,1]{3,2,1,0:T(8,128)S(1)}, f32[8,8,96,1]{3,2,1,0:T(8,128)}, f32[8,8,96,128]{3,2,1,0:T(8,128)}) custom-call(s32[2]{0:T(128)S(1)} %subtract_clamp_fusion.live_ref, bf16[2,8,48,1280]{3,2,1,0:T(8,128)(2,1)S(1)} %bitcast.77, bf16[2,2048,2048]{2,1,0:T(8,128)(2,1)} %kv_ref.1), custom_call_target="tpu_custom_call" | custom-call | tf_op jit(solution)/shard_map/pallas_call | solution.py:101
  113.3 1.1 reduce.4
  114.6 3.1 %reduce.5 = f32[8,8,96]{2,1,0:T(8,128)S(1)} reduce(f32[8,8,96,1]{3,2,1,0:T(8,128)} %get-tuple-element.6, f32[]{:T(128)} %constant.171), dimensions={3}, to_apply=%get-tuple-element.6.reduce_sub_computation | reduce | bytes 49156 | tf_op jit(solution)/shard_map/pallas_call | solution.py:101
  117.9 15.0 %all_to_all.25 = f32[4,2,2,768]{3,0,2,1:T(4,128)S(1)} all-to-all(f32[4,2,2,768]{3,0,2,1:T(4,128)S(1)} %copy.27), channel_id=1, replica_groups=mesh['z'=4,'y'=4,'x'=4,'c'=2] {'c'}, dimensions={1} | all-to-all | bytes 98304 | tf_op jit(solution)/shard_map/all_to_all | solution.py:169
  132.8 0.6 broadcast_in_dim.71
  133.4 0.6 fusion.13
  134.1 0.6 stack.16
  135.6 1.0 fusion.32
  136.5 3.8 %copy.33 = f32[4,2,768,128]{3,2,0,1:T(8,128)} copy(f32[4,2,768,128]{3,2,1,0:T(8,128)} %bitcast.79) | data formatting | bytes 6291456 | tf_op jit(solution)/shard_map/reshape | solution.py:168
  140.3 4.3 %all-to-all-start.3 = ((f32[4,2,768,128]{3,2,0,1:T(8,128)}), f32[4,2,768,128]{3,2,0,1:T(8,128)S(1)}, u32[]{:S(2)}, u32[]{:S(2)}) async-start(f32[4,2,768,128]{3,2,0,1:T(8,128)} %copy.33), calls=%async_computation.3 | async-start | bytes 6291456 | tf_op jit(solution)/shard_map/all_to_all | solution.py:170
  144.6 1.4 pad_maximum_fusion.2
  146.0 1.9 %all-to-all-done.3 = f32[4,2,768,128]{3,2,0,1:T(8,128)S(1)} async-done(((f32[4,2,768,128]{3,2,0,1:T(8,128)}), f32[4,2,768,128]{3,2,0,1:T(8,128)S(1)}, u32[]{:S(2)}, u32[]{:S(2)}) %all-to-all-start.3) | async-done | bytes 3145760 | tf_op jit(solution)/shard_map/all_to_all | solution.py:170
  147.9 3.9 %all-to-all-start.2 = ((f32[4,2,768]{2,1,0:T(2,128)}), f32[4,2,768]{2,1,0:T(2,128)}, u32[]{:S(2)}, u32[]{:S(2)}) async-start(f32[4,2,768]{2,1,0:T(2,128)} %pad_maximum_fusion.2), calls=%async_computation.2 | async-start | bytes 49152 | tf_op jit(solution)/shard_map/all_to_all | solution.py:174
  151.7 1.8 multiply_reduce_fusion
  153.6 2.2 %select_convert_fusion = bf16[4,768,128]{2,1,0:T(8,128)(2,1)} fusion(f32[4,768,128]{2,1,0:T(8,128)S(1)} %multiply_reduce_fusion, f32[4,768]{1,0:T(4,128)S(1)} %get-tuple-element.8, pred[4,768]{1,0:T(4,128)(4,1)S(1)} %copy-done.5), kind=kLoop, calls=%fused_computation.7 | loop fusion | flops 1179648 | bytes 2374656 | tf_op jit(solution)/shard_map/convert_element_type | solution.py:173
  156.8 4.2 %all-to-all-start.4 = ((bf16[4,768,128]{2,1,0:T(8,128)(2,1)}), bf16[4,768,128]{2,1,0:T(8,128)(2,1)S(1)}, u32[]{:S(2)}, u32[]{:S(2)}) async-start(bf16[4,768,128]{2,1,0:T(8,128)(2,1)} %select_convert_fusion), calls=%async_computation.4 | async-start | bytes 1572864 | tf_op jit(solution)/shard_map/all_to_all | solution.py:175
  161.4 0.8 slice_reduce_fusion
  162.4 10.1 %all-to-all-done.4 = bf16[4,768,128]{2,1,0:T(8,128)(2,1)S(1)} async-done(((bf16[4,768,128]{2,1,0:T(8,128)(2,1)}), bf16[4,768,128]{2,1,0:T(8,128)(2,1)S(1)}, u32[]{:S(2)}, u32[]{:S(2)}) %all-to-all-start.4) | async-done | bytes 786464 | tf_op jit(solution)/shard_map/all_to_all | solution.py:175
  172.9 0.7 fusion
  174.0 0.9 copy.46
  (60 shorter events, 4.9 us)
Async XLA Ops:
  25.2 5.4 %copy-start.1 = (s32[32]{0:T(128)S(1)}, s32[32]{0:T(128)}, u32[]{:S(2)}) copy-start(s32[32]{0:T(128)} %param.12) | copy-start | bytes 388
  26.3 15.9 %all-to-all-start = ((bf16[4,2,48,1280]{3,2,1,0:T(8,128)(2,1)}), bf16[4,2,48,1280]{3,2,1,0:T(8,128)(2,1)S(1)}, u32[]{:S(2)}, u32[]{:S(2)}) async-start(bf16[4,2,48,1280]{3,2,1,0:T(8,128)(2,1)} %broadcast_select_fusion), calls=%async_computation | async-start | bytes 1966080 | tf_op jit(solution)/shard_map/all_to_all | solution.py:150
  30.5 25.6 %copy-start.7 = (s32[2]{0:T(128)S(1)}, s32[2]{0:T(128)}, u32[]{:S(2)}) copy-start(s32[2]{0:T(128)} %param.10) | copy-start | bytes 28
  30.5 25.6 %copy-start.4 = (bf16[2,48,256]{2,1,0:T(8,128)(2,1)S(1)}, bf16[2,48,256]{2,1,0:T(8,128)(2,1)}, u32[]{:S(2)}) copy-start(bf16[2,48,256]{2,1,0:T(8,128)(2,1)} %param.8) | copy-start | bytes 147460
  30.5 25.6 %copy-start.6 = (s32[2,8]{1,0:T(2,128)S(1)}, s32[2,8]{1,0:T(2,128)}, u32[]{:S(2)}) copy-start(s32[2,8]{1,0:T(2,128)} %param.13) | copy-start | bytes 196
  30.5 41.7 %all-gather.3.cloned.1.call-start = ((), (), s32[]{:S(2)}) async-start(), calls=%async_computation.5 | async-start | bytes 2949120 | tf_op jit(solution)/shard_map/all_gather | solution.py:158
  72.2 1.8 %copy-start = (bf16[2,4,96,1280]{3,2,1,0:T(8,128)(2,1)S(1)}, bf16[2,4,96,1280]{3,2,1,0:T(8,128)(2,1)}, u32[]{:S(2)}) copy-start(bf16[2,4,96,1280]{3,2,1,0:T(8,128)(2,1)} %all-gather.3.cloned.1.call-done) | copy-start | bytes 5898244
  73.6 39.7 %copy-start.2 = (bf16[8,48,1280]{2,1,0:T(8,128)(2,1)}, bf16[8,48,1280]{2,1,0:T(8,128)(2,1)S(1)}, u32[]{:S(2)}) copy-start(bf16[8,48,1280]{2,1,0:T(8,128)(2,1)S(1)} %dynamic-slice_bitcast_fusion) | copy-start | bytes 2949124
  114.5 20.8 %slice-start = ((bf16[8,48,1280]{2,1,0:T(8,128)(2,1)}), bf16[8,48,1024]{2,1,0:T(8,128)(2,1)S(1)}, s32[]{:S(2)}) async-start(bf16[8,48,1280]{2,1,0:T(8,128)(2,1)} %copy-done.2), calls=%async_computation.6 | async-start | bytes 1572864 | tf_op jit(solution)/shard_map/slice | solution.py:183
  114.6 20.9 %slice-start.1 = ((bf16[8,48,1280]{2,1,0:T(8,128)(2,1)}), bf16[8,48,256]{2,1,0:T(8,128)(2,1)S(1)}, s32[]{:S(2)}) async-start(bf16[8,48,1280]{2,1,0:T(8,128)(2,1)} %copy-done.2), calls=%async_computation.7 | async-start | bytes 393216 | tf_op jit(solution)/shard_map/slice | solution.py:186
  140.3 7.5 %all-to-all-start.3 = ((f32[4,2,768,128]{3,2,0,1:T(8,128)}), f32[4,2,768,128]{3,2,0,1:T(8,128)S(1)}, u32[]{:S(2)}, u32[]{:S(2)}) async-start(f32[4,2,768,128]{3,2,0,1:T(8,128)} %copy.33), calls=%async_computation.3 | async-start | bytes 6291456 | tf_op jit(solution)/shard_map/all_to_all | solution.py:170
  147.9 8.9 %all-to-all-start.2 = ((f32[4,2,768]{2,1,0:T(2,128)}), f32[4,2,768]{2,1,0:T(2,128)}, u32[]{:S(2)}, u32[]{:S(2)}) async-start(f32[4,2,768]{2,1,0:T(2,128)} %pad_maximum_fusion.2), calls=%async_computation.2 | async-start | bytes 49152 | tf_op jit(solution)/shard_map/all_to_all | solution.py:174
  151.7 1.8 copy-start.5
  153.5 2.2 %copy-start.3 = (bf16[8,48,1,128]{3,2,1,0:T(2,128)(2,1)S(1)}, bf16[8,48,1,128]{3,2,1,0:T(2,128)(2,1)}, u32[]{:S(2)}) copy-start(bf16[8,48,1,128]{3,2,1,0:T(2,128)(2,1)} %get-tuple-element.13) | copy-start | bytes 294916
  156.8 15.6 %all-to-all-start.4 = ((bf16[4,768,128]{2,1,0:T(8,128)(2,1)}), bf16[4,768,128]{2,1,0:T(8,128)(2,1)S(1)}, u32[]{:S(2)}, u32[]{:S(2)}) async-start(bf16[4,768,128]{2,1,0:T(8,128)(2,1)} %select_convert_fusion), calls=%async_computation.4 | async-start | bytes 1572864 | tf_op jit(solution)/shard_map/all_to_all | solution.py:175
Sparse Core Ops, SparseCore 0:
  55.4 16.7 all-gather.2

commit v4 on v3

--- a/solution.py
+++ b/solution.py
@@ -12,63 +12,44 @@
 NEG = -1e30
 
 
-def attn_kernel(live_ref, q_ref, kv_ref, m_ref, l_ref, acc_ref, m_sc, l_sc, acc_sc,
-                *, n_blk, scale, groups):
+def attn_kernel(live_ref, q_ref, kv_ref, m_ref, l_ref, acc_ref, *, n_blk, scale, groups):
     slot = pl.program_id(0)
     live = live_ref[slot]
-    q = jnp.concatenate(
-        [q_ref[:, g * HEAD_WIDTH:(g + 1) * HEAD_WIDTH] for g in range(groups)], axis=0
-    )
-    m_sc[...] = jnp.full(m_sc.shape, NEG, jnp.float32)
-    l_sc[...] = jnp.zeros(l_sc.shape, jnp.float32)
-    acc_sc[...] = jnp.zeros(acc_sc.shape, jnp.float32)
-
-    def absorb(b, masked):
-        keys = kv_ref[b * BLK:(b + 1) * BLK, 0:HEAD_WIDTH]
-        vals = kv_ref[b * BLK:(b + 1) * BLK, HEAD_WIDTH:2 * HEAD_WIDTH]
-        s = lax.dot_general(
-            q, keys, (((1,), (1,)), ((), ())), preferred_element_type=jnp.float32
-        ) * scale
-        if masked:
+    tree_len = q_ref.shape[0]
+    rows = tree_len * groups
+    q = jnp.concatenate([q_ref[:, g * HEAD_WIDTH:(g + 1) * HEAD_WIDTH] for g in range(groups)], axis=0)
+    outs_m, outs_l, outs_a = [], [], []
+    for c0 in range(0, rows, rows):
+        qc = q[c0:c0 + rows]
+        run = None
+        for b in range(n_blk):
+            keys = kv_ref[b * BLK:(b + 1) * BLK, 0:HEAD_WIDTH]
+            vals = kv_ref[b * BLK:(b + 1) * BLK, HEAD_WIDTH:2 * HEAD_WIDTH]
+            s = lax.dot_general(qc, keys, (((1,), (1,)), ((), ())), preferred_element_type=jnp.float32) * scale
             pos = b * BLK + lax.broadcasted_iota(jnp.int32, (1, BLK), 1)
-            allowed = pos < live
-            s = jnp.where(allowed, s, jnp.float32(NEG))
-        mb = jnp.max(s, axis=1, keepdims=True)
-        w = jnp.exp(s - mb)
-        if masked:
-            w = jnp.where(allowed, w, jnp.float32(0.0))
-        lb = jnp.sum(w, axis=1, keepdims=True)
-        ob = jnp.dot(w.astype(jnp.bfloat16), vals, preferred_element_type=jnp.float32)
-        m_old = m_sc[...]
-        new_m = jnp.maximum(m_old, mb)
-        fa = jnp.exp(m_old - new_m)
-        fb = jnp.exp(mb - new_m)
-        l_sc[...] = l_sc[...] * fa + lb * fb
-        acc_sc[...] = acc_sc[...] * fa + ob * fb
-        m_sc[...] = new_m
-
-    for b in range(n_blk):
-        lo, hi = b * BLK, (b + 1) * BLK
-
-        @pl.when(live >= hi)
-        def _full():
-            absorb(b, False)
-
-        @pl.when(jnp.logical_and(live > lo, live < hi))
-        def _part():
-            absorb(b, True)
-
+            bias = jnp.where(pos < live, jnp.float32(0.0), jnp.float32(NEG))
+            s = s + bias
+            mb = jnp.max(s, axis=1, keepdims=True)
+            w = jnp.exp(s - mb)
+            lb = jnp.sum(w, axis=1, keepdims=True)
+            ob = jnp.dot(w.astype(jnp.bfloat16), vals, preferred_element_type=jnp.float32)
+            if run is None:
+                run = (mb, lb, ob)
+            else:
+                rm, rl, ra = run
+                nm = jnp.maximum(rm, mb); fa = jnp.exp(rm - nm); fb = jnp.exp(mb - nm)
+                run = (nm, rl * fa + lb * fb, ra * fa + ob * fb)
+        outs_m.append(run[0]); outs_l.append(run[1]); outs_a.append(run[2])
+    rm = jnp.concatenate(outs_m, 0); rl = jnp.concatenate(outs_l, 0); ra = jnp.concatenate(outs_a, 0)
     parts = m_ref.shape[0]
-    tree_len = q_ref.shape[0]
     tok = tree_len // parts
     for j in range(parts):
         for g in range(groups):
             src = slice(g * tree_len + j * tok, g * tree_len + (j + 1) * tok)
             dst = slice(g * tok, (g + 1) * tok)
-            m_ref[j, dst, :] = m_sc[src, :]
-            l_ref[j, dst, :] = l_sc[src, :]
-            acc_ref[j, dst, :] = acc_sc[src, :]
-
+            m_ref[j, dst, :] = rm[src]
+            l_ref[j, dst, :] = rl[src]
+            acc_ref[j, dst, :] = ra[src]
 
 def local_attention(q_all, kv, live, seq_count):
     slots, kvh, tree_len, _ = q_all.shape
@@ -77,39 +58,19 @@
     rows = tree_len * groups
     per_slot = seq_count // slots
     sub = rows // per_slot
-    kern = functools.partial(
-        attn_kernel, n_blk=positions // BLK, scale=HEAD_WIDTH ** (-0.5), groups=groups
-    )
+    kern = functools.partial(attn_kernel, n_blk=positions // BLK, scale=HEAD_WIDTH ** (-0.5), groups=groups)
     grid_spec = pltpu.PrefetchScalarGridSpec(
-        num_scalar_prefetch=1,
-        grid=(slots, kvh),
-        in_specs=[
-            pl.BlockSpec((None, None, tree_len, groups * HEAD_WIDTH), lambda i, k, lv: (i, k, 0, 0)),
-            pl.BlockSpec((None, positions, 2 * HEAD_WIDTH), lambda i, k, lv: (i, 0, k)),
-        ],
-        out_specs=[
-            pl.BlockSpec((per_slot, None, sub, 1), lambda i, k, lv: (i, k, 0, 0)),
-            pl.BlockSpec((per_slot, None, sub, 1), lambda i, k, lv: (i, k, 0, 0)),
-            pl.BlockSpec((per_slot, None, sub, HEAD_WIDTH), lambda i, k, lv: (i, k, 0, 0)),
-        ],
-        scratch_shapes=[
-            pltpu.VMEM((rows, 1), jnp.float32),
-            pltpu.VMEM((rows, 1), jnp.float32),
-            pltpu.VMEM((rows, HEAD_WIDTH), jnp.float32),
-        ],
-    )
-    return pl.pallas_call(
-        kern,
-        grid_spec=grid_spec,
-        out_shape=[
-            jax.ShapeDtypeStruct((seq_count, kvh, sub, 1), jnp.float32),
-            jax.ShapeDtypeStruct((seq_count, kvh, sub, 1), jnp.float32),
-            jax.ShapeDtypeStruct((seq_count, kvh, sub, HEAD_WIDTH), jnp.float32),
-        ],
-        compiler_params=pltpu.CompilerParams(
-            dimension_semantics=("arbitrary", "arbitrary"),
-            vmem_limit_bytes=48 * 1024 * 1024,
-        ),
+        num_scalar_prefetch=1, grid=(slots, kvh),
+        in_specs=[pl.BlockSpec((None, None, tree_len, groups * HEAD_WIDTH), lambda i, k, lv: (i, k, 0, 0)),
+                  pl.BlockSpec((None, positions, 2 * HEAD_WIDTH), lambda i, k, lv: (i, 0, k))],
+        out_specs=[pl.BlockSpec((per_slot, None, sub, 1), lambda i, k, lv: (i, k, 0, 0)),
+                   pl.BlockSpec((per_slot, None, sub, 1), lambda i, k, lv: (i, k, 0, 0)),
+                   pl.BlockSpec((per_slot, None, sub, HEAD_WIDTH), lambda i, k, lv: (i, k, 0, 0))])
+    return pl.pallas_call(kern, grid_spec=grid_spec,
+        out_shape=[jax.ShapeDtypeStruct((seq_count, kvh, sub, 1), jnp.float32),
+                   jax.ShapeDtypeStruct((seq_count, kvh, sub, 1), jnp.float32),
+                   jax.ShapeDtypeStruct((seq_count, kvh, sub, HEAD_WIDTH), jnp.float32)],
+        compiler_params=pltpu.CompilerParams(dimension_semantics=("arbitrary", "arbitrary"), vmem_limit_bytes=48 * 1024 * 1024),
     )(live, q_all, kv)
 
 
@@ -164,16 +125,33 @@
     live = jnp.clip(cache_lengths - position * positions, 0, positions).astype(jnp.int32)
     part_m, part_l, part_acc = local_attention(q_all, kv_cache, live, seq_count)
     sub = part_acc.shape[2]
-    ml = jnp.stack([part_m[..., 0], part_l[..., 0]], axis=1).reshape(nx, nc, 2, kv_heads * sub)
-    acc = part_acc.reshape(nx, nc, kv_heads * sub, HEAD_WIDTH)
-    ml = lax.all_to_all(ml, "c", 1, 1, tiled=True)
-    acc = lax.all_to_all(acc, "c", 1, 1, tiled=True)
-    m1, l1, a1 = merge_pair(ml[:, :, 0], ml[:, :, 1], acc, axis=1)
-    ml = jnp.stack([m1, l1], axis=1)
-    x1 = jnp.where(l1[..., None] > 0, a1 / l1[..., None], jnp.float32(0.0)).astype(jnp.bfloat16)
-    ml = lax.all_to_all(ml, "x", 0, 0, tiled=True)
-    x1 = lax.all_to_all(x1, "x", 0, 0, tiled=True)
-    acc = x1.astype(jnp.float32) * ml[:, 1][..., None]
+    rows_acc = kv_heads * sub
+    stat_rows = rows_acc // HEAD_WIDTH
+    pad = (-(rows_acc + 2 * stat_rows)) % 8
+
+    def pack(acc, m, l):
+        lead = acc.shape[:-2]
+        parts = [acc, m.reshape(lead + (stat_rows, HEAD_WIDTH)), l.reshape(lead + (stat_rows, HEAD_WIDTH))]
+        if pad:
+            parts.append(jnp.zeros(lead + (pad, HEAD_WIDTH), jnp.float32))
+        return jnp.concatenate(parts, axis=-2)
+
+    def unpack(pk):
+        lead = pk.shape[:-2]
+        acc = pk[..., :rows_acc, :]
+        m = pk[..., rows_acc:rows_acc + stat_rows, :].reshape(lead + (rows_acc,))
+        l = pk[..., rows_acc + stat_rows:rows_acc + 2 * stat_rows, :].reshape(lead + (rows_acc,))
+        return m, l, acc
+
+    pk = pack(
+        part_acc.reshape(nx, nc, rows_acc, HEAD_WIDTH),
+        part_m.reshape(nx, nc, rows_acc),
+        part_l.reshape(nx, nc, rows_acc),
+    )
+    pk = lax.all_to_all(pk, "c", 1, 1, tiled=True)
+    m1, l1, a1 = merge_pair(*unpack(pk), axis=1)
+    pk = lax.all_to_all(pack(a1, m1, l1), "x", 0, 0, tiled=True)
+    rm, rl, acc = unpack(pk)
 
     per_slot = seq_count // local_reqs
     tok = tree_len // per_slot
@@ -202,8 +180,8 @@
     od = od.reshape(1, kv_heads * sub, HEAD_WIDTH)
 
     _, den, num = merge_pair(
-        jnp.concatenate([ml[:, 0], md], axis=0),
-        jnp.concatenate([ml[:, 1], ld], axis=0),
+        jnp.concatenate([rm, md], axis=0),
+        jnp.concatenate([rl, ld], axis=0),
         jnp.concatenate([acc, od], axis=0),
         axis=0,
     )

time: 183 us -> 155 us (0.85)
  blocking collectives: 42.3 us -> 33.5 us
  Pallas kernels: 39.3 us -> 30.6 us
  starting transfers between devices: 16.5 us -> 8.52 us
  waiting for transfers between devices: 38.8 us -> 45.4 us
  local copies, waits for them, and re-layouts: 12.3 us -> 8.1 us
  other arithmetic: 16.5 us -> 12.3 us
    all_to_all x1, blocking collectives: 15 us -> 6.16 us  [body(): pk = lax.all_to_all(pk, 'c', 1, 1, tiled=True)]
    pallas_call x1, Pallas kernels: 39.3 us -> 30.6 us  [local_attention(): pl.pallas_call(kern, grid_spec=grid_spec, out_shape=[jax.ShapeDtypeStruct...]
    all_to_all x3 -> x1, starting transfers between devices: 12.3 us -> 4.34 us  [body(): pk = lax.all_to_all(pack(a1, m1, l1), 'x', 0, 0, tiled=True)]
    all_to_all x3 -> x1, waiting for transfers between devices: 11.9 us -> 18.5 us  [body(): pk = lax.all_to_all(pack(a1, m1, l1), 'x', 0, 0, tiled=True)]
    reshape x1 -> x2, local copies, waits for them, and re-layouts: 3.82 us -> 0.02 us  [the longest x1 0.01 us: unpack(): m = pk[..., rows_acc:rows_acc + stat_rows, :].reshape(lead + (rows_acc,))]
    convert_element_type x1 -> x0, other arithmetic: 2.15 us -> none  [body(): jnp.where(l1[..., None] > 0, a1 / l1[..., None], jnp.float32(0.0))]
  transfers between devices with their start and end apart: 5 -> 3, of which waited for: 4 -> 3; matrix products, arithmetic and copies ran while one was open for 5% -> 2% of each run, Pallas kernels for 0% -> 0%
where the time goes in v4:
time: 155 us; the launch traced here: 154 us
  waiting for transfers between devices  45.4 us (29%)
  blocking collectives  33.5 us (22%)
  Pallas kernels  30.6 us (20%)
  between operations  14.4 us (9%)
  other arithmetic  12.3 us (8%)
  starting transfers between devices  8.52 us (5%)
  local copies, waits for them, and re-layouts  8.1 us (5%)
    pallas_call x1, Pallas kernels, local_attention(): pl.pallas_call(kern, grid_spec=grid_spec, out_shape=[jax.ShapeDtypeStruct...  30.6 us
    all_to_all x1, waiting for transfers between devices, body(): pk = lax.all_to_all(pack(a1, m1, l1), 'x', 0, 0, tiled=True)  18.5 us
    all_gather x1, waiting for transfers between devices, body(): own = lax.all_gather(own, 'c', axis=2, tiled=False)  15.2 us
    all_gather x1, blocking collectives, body(): held = lax.all_gather(both, 'z', axis=0, tiled=True)  15 us
    all_gather x1, blocking collectives, body(): own = lax.all_gather(own, 'x', axis=1, tiled=False)  12.4 us
    all_to_all x1, waiting for transfers between devices, body(): recv = lax.all_to_all(send, 'y', 0, 0, tiled=True)  11.6 us
    all_to_all x1, blocking collectives, body(): pk = lax.all_to_all(pk, 'c', 1, 1, tiled=True)  6.16 us
    all_to_all x1, starting transfers between devices, body(): pk = lax.all_to_all(pack(a1, m1, l1), 'x', 0, 0, tiled=True)  4.34 us
  transfers between devices with their start and end apart: 3, of which 3 were waited for; matrix products, arithmetic and copies ran while one was open for 2% of the time, Pallas kernels for 0%

profile of v4, /device:TPU:1, one launch (start us, length us, event | category | flops | bytes accessed | tf_op | source)
XLA Modules:
  0.0 154.3 jit_solution(3862381663776976942)
XLA Ops:
  7.2 1.3 gather_fusion
  8.6 1.0 pad_maximum_fusion
  9.6 15.0 %all_gather.13 = bf16[8,48,1280]{2,1,0:T(8,128)(2,1)S(1)} all-gather(bf16[2,48,1280]{2,1,0:T(8,128)(2,1)S(1)} %pad_maximum_fusion), channel_id=1, replica_groups=mesh['z'=4,'y'=4,'x'=4,'c'=2] {'z'}, dimensions={0}, use_global_device_ids=true | all-gather | bytes 1228800 | tf_op jit(solution)/shard_map/all_gather | solution.py:105
  24.6 0.6 gather_fusion.1
  25.2 1.1 broadcast_select_fusion
  26.3 4.2 %all-to-all-start = ((bf16[4,2,48,1280]{3,2,1,0:T(8,128)(2,1)}), bf16[4,2,48,1280]{3,2,1,0:T(8,128)(2,1)S(1)}, u32[]{:S(2)}, u32[]{:S(2)}) async-start(bf16[4,2,48,1280]{3,2,1,0:T(8,128)(2,1)} %broadcast_select_fusion), calls=%async_computation | async-start | bytes 1966080 | tf_op jit(solution)/shard_map/all_to_all | solution.py:111
  30.6 11.6 %all-to-all-done = bf16[4,2,48,1280]{3,2,1,0:T(8,128)(2,1)S(1)} async-done(((bf16[4,2,48,1280]{3,2,1,0:T(8,128)(2,1)}), bf16[4,2,48,1280]{3,2,1,0:T(8,128)(2,1)S(1)}, u32[]{:S(2)}, u32[]{:S(2)}) %all-to-all-start) | async-done | bytes 983072 | tf_op jit(solution)/shard_map/all_to_all | solution.py:111
  42.3 0.6 gather_fusion.2
  42.9 12.4 %all_gather.14 = bf16[2,4,48,1280]{3,2,1,0:T(8,128)(2,1)} all-gather(bf16[2,1,48,1280]{3,2,1,0:T(8,128)(2,1)S(1)} %bitcast_select_fusion), channel_id=1, replica_groups=mesh['z'=4,'y'=4,'x'=4,'c'=2] {'x'}, dimensions={1}, use_global_device_ids=true | all-gather | bytes 1228800 | tf_op jit(solution)/shard_map/all_gather | solution.py:118
  55.5 0.7 fusion.17
  56.2 0.8 convolution_convert_fusion
  57.0 15.2 %all-gather.3.cloned.1.call-done = bf16[2,4,96,1280]{3,2,1,0:T(8,128)(2,1)} async-done(((bf16[2,4,48,1280]{3,2,1,0:T(8,128)(2,1)}), bf16[2,4,96,1280]{3,2,1,0:T(8,128)(2,1)}) %all-gather.3.cloned.1.call-update) | async-done | bytes 1966096 | tf_op jit(solution)/shard_map/all_gather | solution.py:119
  72.2 1.5 %copy-done = bf16[2,4,96,1280]{3,2,1,0:T(8,128)(2,1)S(1)} copy-done((bf16[2,4,96,1280]{3,2,1,0:T(8,128)(2,1)S(1)}, bf16[2,4,96,1280]{3,2,1,0:T(8,128)(2,1)}, u32[]{:S(2)}) %copy-start) | copy-done | bytes 1966104
  73.7 30.6 %shard_map.86 = (f32[8,8,96,1]{3,2,1,0:T(8,128)S(1)}, f32[8,8,96,1]{3,2,1,0:T(8,128)}, f32[8,8,96,128]{3,2,1,0:T(8,128)}) custom-call(s32[2]{0:T(128)S(1)} %subtract_clamp_fusion.live_ref, bf16[2,8,48,1280]{3,2,1,0:T(8,128)(2,1)S(1)} %bitcast.72, bf16[2,2048,2048]{2,1,0:T(8,128)(2,1)} %kv_ref.1), custom_call_target="tpu_custom_call" | custom-call | tf_op jit(solution)/shard_map/pallas_call | solution.py:69
  104.4 1.1 reduce.5
  105.6 3.2 %reduce.6 = f32[8,8,96]{2,1,0:T(8,128)S(1)} reduce(f32[8,8,96,1]{3,2,1,0:T(8,128)} %get-tuple-element.7, f32[]{:T(128)} %constant.172), dimensions={3}, to_apply=%get-tuple-element.7.reduce_sub_computation | reduce | bytes 49156 | tf_op jit(solution)/shard_map/pallas_call | solution.py:69
  108.9 0.3 maximum_maximum_fusion
  109.2 6.2 %all_to_all.15 = f32[4,2,784,128]{3,2,0,1:T(8,128)S(1)} all-to-all(f32[4,2,784,128]{3,2,0,1:T(8,128)S(1)} %maximum_maximum_fusion), channel_id=1, replica_groups=mesh['z'=4,'y'=4,'x'=4,'c'=2] {'c'}, dimensions={1} | all-to-all | bytes 6422528 | tf_op jit(solution)/shard_map/all_to_all | solution.py:151
  115.4 1.1 fusion
  116.5 1.3 maximum_maximum_fusion.1
  117.9 4.3 %all-to-all-start.2 = ((f32[4,784,128]{2,1,0:T(8,128)}), f32[4,784,128]{2,1,0:T(8,128)}, u32[]{:S(2)}, u32[]{:S(2)}) async-start(f32[4,784,128]{2,1,0:T(8,128)} %maximum_maximum_fusion.1), calls=%async_computation.2 | async-start | bytes 3211264 | tf_op jit(solution)/shard_map/all_to_all | solution.py:153
  122.5 0.1 reshape.319
  122.7 0.3 fusion.32
  123.0 0.4 fusion.33
  123.6 0.4 fusion.4
  124.1 0.3 fusion.6
  124.5 18.5 %all-to-all-done.2 = f32[4,784,128]{2,1,0:T(8,128)} async-done(((f32[4,784,128]{2,1,0:T(8,128)}), f32[4,784,128]{2,1,0:T(8,128)}, u32[]{:S(2)}, u32[]{:S(2)}) %all-to-all-start.2) | async-done | bytes 1605664 | tf_op jit(solution)/shard_map/all_to_all | solution.py:153
  143.0 0.8 slice_bitcast_fusion
  143.9 1.5 slice.53
  145.4 0.7 fusion.1
  146.2 0.2 fusion.11
  146.6 0.9 copy.38
  (51 shorter events, 1.6 us)
Async XLA Ops:
  24.6 6.0 %copy-start.2 = (s32[32]{0:T(128)S(1)}, s32[32]{0:T(128)}, u32[]{:S(2)}) copy-start(s32[32]{0:T(128)} %param.12) | copy-start | bytes 388
  25.2 31.0 %copy-start.6 = (s32[2]{0:T(128)S(1)}, s32[2]{0:T(128)}, u32[]{:S(2)}) copy-start(s32[2]{0:T(128)} %param.10) | copy-start | bytes 28
  25.2 31.0 %copy-start.4 = (bf16[2,48,256]{2,1,0:T(8,128)(2,1)S(1)}, bf16[2,48,256]{2,1,0:T(8,128)(2,1)}, u32[]{:S(2)}) copy-start(bf16[2,48,256]{2,1,0:T(8,128)(2,1)} %param.8) | copy-start | bytes 147460
  25.2 31.0 %copy-start.5 = (s32[2,8]{1,0:T(2,128)S(1)}, s32[2,8]{1,0:T(2,128)}, u32[]{:S(2)}) copy-start(s32[2,8]{1,0:T(2,128)} %param.13) | copy-start | bytes 196
  26.3 15.9 %all-to-all-start = ((bf16[4,2,48,1280]{3,2,1,0:T(8,128)(2,1)}), bf16[4,2,48,1280]{3,2,1,0:T(8,128)(2,1)S(1)}, u32[]{:S(2)}, u32[]{:S(2)}) async-start(bf16[4,2,48,1280]{3,2,1,0:T(8,128)(2,1)} %broadcast_select_fusion), calls=%async_computation | async-start | bytes 1966080 | tf_op jit(solution)/shard_map/all_to_all | solution.py:111
  30.5 41.7 %all-gather.3.cloned.1.call-start = ((), (), s32[]{:S(2)}) async-start(), calls=%async_computation.3 | async-start | bytes 2949120 | tf_op jit(solution)/shard_map/all_gather | solution.py:119
  72.2 1.5 %copy-start = (bf16[2,4,96,1280]{3,2,1,0:T(8,128)(2,1)S(1)}, bf16[2,4,96,1280]{3,2,1,0:T(8,128)(2,1)}, u32[]{:S(2)}) copy-start(bf16[2,4,96,1280]{3,2,1,0:T(8,128)(2,1)} %all-gather.3.cloned.1.call-done) | copy-start | bytes 5898244
  105.5 3.4 %copy-start.3 = (f32[8,8,96,128]{3,2,1,0:T(8,128)S(1)}, f32[8,8,96,128]{3,2,1,0:T(8,128)}, u32[]{:S(2)}) copy-start(f32[8,8,96,128]{3,2,1,0:T(8,128)} %get-tuple-element.5) | copy-start | bytes 9437188
  116.5 5.7 %copy-start.1 = (bf16[2,4,96,1280]{3,2,1,0:T(8,128)(2,1)S(1)}, bf16[2,4,96,1280]{3,2,1,0:T(8,128)(2,1)}, u32[]{:S(2)}) copy-start(bf16[2,4,96,1280]{3,2,1,0:T(8,128)(2,1)} %all-gather.3.cloned.1.call-done) | copy-start | bytes 5898244
  117.9 25.1 %all-to-all-start.2 = ((f32[4,784,128]{2,1,0:T(8,128)}), f32[4,784,128]{2,1,0:T(8,128)}, u32[]{:S(2)}, u32[]{:S(2)}) async-start(f32[4,784,128]{2,1,0:T(8,128)} %maximum_maximum_fusion.1), calls=%async_computation.2 | async-start | bytes 3211264 | tf_op jit(solution)/shard_map/all_to_all | solution.py:153
Sparse Core Ops, SparseCore 0:
  55.5 16.6 all-gather.2

commit v5 on v4

--- a/solution.py
+++ b/solution.py
@@ -51,7 +51,7 @@
             l_ref[j, dst, :] = rl[src]
             acc_ref[j, dst, :] = ra[src]
 
-def local_attention(q_all, kv, live, seq_count):
+def local_attention(q_all, kv, pref, seq_count, nc):
     slots, kvh, tree_len, _ = q_all.shape
     positions = kv.shape[1]
     groups = (q_all.shape[3] - 2 * HEAD_WIDTH) // HEAD_WIDTH
@@ -62,7 +62,7 @@
     grid_spec = pltpu.PrefetchScalarGridSpec(
         num_scalar_prefetch=1, grid=(slots, kvh),
         in_specs=[pl.BlockSpec((None, None, tree_len, groups * HEAD_WIDTH), lambda i, k, lv: (i, k, 0, 0)),
-                  pl.BlockSpec((None, positions, 2 * HEAD_WIDTH), lambda i, k, lv: (i, 0, k))],
+                  pl.BlockSpec((None, positions, 2 * HEAD_WIDTH), lambda i, k, lv: (i, 0, k * nc + lv[slots]))],
         out_specs=[pl.BlockSpec((per_slot, None, sub, 1), lambda i, k, lv: (i, k, 0, 0)),
                    pl.BlockSpec((per_slot, None, sub, 1), lambda i, k, lv: (i, k, 0, 0)),
                    pl.BlockSpec((per_slot, None, sub, HEAD_WIDTH), lambda i, k, lv: (i, k, 0, 0))])
@@ -71,7 +71,7 @@
                    jax.ShapeDtypeStruct((seq_count, kvh, sub, 1), jnp.float32),
                    jax.ShapeDtypeStruct((seq_count, kvh, sub, HEAD_WIDTH), jnp.float32)],
         compiler_params=pltpu.CompilerParams(dimension_semantics=("arbitrary", "arbitrary"), vmem_limit_bytes=48 * 1024 * 1024),
-    )(live, q_all, kv)
+    )(pref, q_all, kv)
 
 
 def merge_pair(m, l, acc, axis):
@@ -115,15 +115,28 @@
     recv = recv.reshape((ny * local_reqs,) + both.shape[1:])
     own = jnp.take(recv, from_y * local_reqs + jnp.arange(local_reqs, dtype=jnp.int32), axis=0)
 
-    own = lax.all_gather(own, "x", axis=1, tiled=False)
-    own = lax.all_gather(own, "c", axis=2, tiled=False)
-    q_all = own.reshape(local_reqs, seq_count, tree_len, q_cols + d_cols)
+    own_x = lax.all_gather(own, "x", axis=1, tiled=False)
+    other_x = lax.ppermute(own_x, "c", perm=[(0, 1), (1, 0)])
 
     positions = kv_cache.shape[1]
     kv_heads = kv_cache.shape[2] // (2 * HEAD_WIDTH)
     groups = q_cols // HEAD_WIDTH
     live = jnp.clip(cache_lengths - position * positions, 0, positions).astype(jnp.int32)
-    part_m, part_l, part_acc = local_attention(q_all, kv_cache, live, seq_count)
+    pm_a, pl_a, pa_a = local_attention(own_x, kv_cache, jnp.concatenate([live, ci[None]]), seq_count, nc)
+    pm_b, pl_b, pa_b = local_attention(
+        other_x, kv_cache, jnp.concatenate([live, (1 - ci)[None]]), seq_count, nc
+    )
+    first = ci == 0
+
+    def by_parity(a, b):
+        return jnp.where(first, jnp.concatenate([a, b], axis=1), jnp.concatenate([b, a], axis=1))
+
+    part_m = by_parity(pm_a, pm_b)
+    part_l = by_parity(pl_a, pl_b)
+    part_acc = by_parity(pa_a, pa_b)
+    q_all = jnp.where(
+        first, jnp.concatenate([own_x, other_x], axis=1), jnp.concatenate([other_x, own_x], axis=1)
+    )
     sub = part_acc.shape[2]
     rows_acc = kv_heads * sub
     stat_rows = rows_acc // HEAD_WIDTH
@@ -187,8 +200,8 @@
     )
     res = num / den[..., None]
     context = (
-        res.reshape(kv_heads, groups, tok, HEAD_WIDTH)
-        .transpose(2, 0, 1, 3)
+        res.reshape(nc, kv_heads // nc, groups, tok, HEAD_WIDTH)
+        .transpose(3, 1, 0, 2, 4)
         .reshape(tok, kv_heads * groups * HEAD_WIDTH)
         .astype(jnp.bfloat16)
     )

time: 155 us -> 150 us (0.968)
  waiting for transfers between devices: 45.4 us -> 30.1 us
  between operations: 14.4 us -> 1 us
  local copies, waits for them, and re-layouts: 8.1 us -> 20.5 us
  starting transfers between devices: 8.52 us -> 15.7 us
  other arithmetic: 12.3 us -> 15.4 us
    all_gather x1 -> x0, waiting for transfers between devices: 15.2 us -> none  [body(): own = lax.all_gather(own, 'c', axis=2, tiled=False)]
    pallas_call x0 -> x4, local copies, waits for them, and re-layouts: none -> 7.19 us  [local_attention(): pl.pallas_call(kern, grid_spec=grid_spec, out_shape=[jax.ShapeDtypeStruct...]
    ppermute x0 -> x1, starting transfers between devices: none -> 7.01 us  [body(): other_x = lax.ppermute(own_x, 'c', perm=[(0, 1), (1, 0)])]
    unnamed x17 -> x29, local copies, waits for them, and re-layouts: 2.48 us -> 7.22 us
    pallas_call x2 -> x0, other arithmetic: 4.33 us -> none  [local_attention(): pl.pallas_call(kern, grid_spec=grid_spec, out_shape=[jax.ShapeDtypeStruct...]
    select_n x0 -> x2, other arithmetic: none -> 4.32 us  [by_parity(): jnp.where(first, jnp.concatenate([a, b], axis=1), jnp.concatenate([b, a],...]
    pallas_call x1 -> x2, Pallas kernels: 30.6 us -> 32 us  [local_attention(): pl.pallas_call(kern, grid_spec=grid_spec, out_shape=[jax.ShapeDtypeStruct...]
  transfers between devices with their start and end apart: 3 -> 3, of which waited for: 3 -> 2; matrix products, arithmetic and copies ran while one was open for 2% -> 6% of each run, Pallas kernels for 0% -> 11%
where the time goes in v5:
time: 150 us; the launch traced here: 149 us
  blocking collectives  32.9 us (22%)
  Pallas kernels  32 us (21%)
  waiting for transfers between devices  30.1 us (20%)
  local copies, waits for them, and re-layouts  20.5 us (14%)
  starting transfers between devices  15.7 us (10%)
  other arithmetic  15.4 us (10%)
    pallas_call x2, Pallas kernels, local_attention(): pl.pallas_call(kern, grid_spec=grid_spec, out_shape=[jax.ShapeDtypeStruct...  32 us
    all_to_all x1, waiting for transfers between devices, body(): pk = lax.all_to_all(pack(a1, m1, l1), 'x', 0, 0, tiled=True)  18.5 us
    all_gather x1, blocking collectives, body(): held = lax.all_gather(both, 'z', axis=0, tiled=True)  15 us
    all_gather x1, blocking collectives, body(): own_x = lax.all_gather(own, 'x', axis=1, tiled=False)  12 us
    all_to_all x1, waiting for transfers between devices, body(): recv = lax.all_to_all(send, 'y', 0, 0, tiled=True)  11.6 us
    unnamed x29, local copies, waits for them, and re-layouts  7.22 us
    pallas_call x4, local copies, waits for them, and re-layouts, local_attention(): pl.pallas_call(kern, grid_spec=grid_spec, out_shape=[jax.ShapeDtypeStruct...  7.19 us
    ppermute x1, starting transfers between devices, body(): other_x = lax.ppermute(own_x, 'c', perm=[(0, 1), (1, 0)])  7.01 us
  transfers between devices with their start and end apart: 3, of which 2 were waited for; matrix products, arithmetic and copies ran while one was open for 6% of the time, Pallas kernels for 11%

profile of v5, /device:TPU:1, one launch (start us, length us, event | category | flops | bytes accessed | tf_op | source)
XLA Modules:
  0.0 149.2 jit_solution(10141662636979288669)
XLA Ops:
  0.7 1.3 gather_fusion
  2.1 1.0 pad_maximum_fusion
  3.1 15.0 %all_gather.7 = bf16[8,48,1280]{2,1,0:T(8,128)(2,1)S(1)} all-gather(bf16[2,48,1280]{2,1,0:T(8,128)(2,1)S(1)} %pad_maximum_fusion), channel_id=1, replica_groups=mesh['z'=4,'y'=4,'x'=4,'c'=2] {'z'}, dimensions={0}, use_global_device_ids=true | all-gather | bytes 1228800 | tf_op jit(solution)/shard_map/all_gather | solution.py:105
  18.7 1.1 broadcast_select_fusion
  19.8 4.3 %all-to-all-start = ((bf16[4,2,48,1280]{3,2,1,0:T(8,128)(2,1)}), bf16[4,2,48,1280]{3,2,1,0:T(8,128)(2,1)S(1)}, u32[]{:S(2)}, u32[]{:S(2)}) async-start(bf16[4,2,48,1280]{3,2,1,0:T(8,128)(2,1)} %broadcast_select_fusion), calls=%async_computation | async-start | bytes 1966080 | tf_op jit(solution)/shard_map/all_to_all | solution.py:111
  24.2 11.6 %all-to-all-done = bf16[4,2,48,1280]{3,2,1,0:T(8,128)(2,1)S(1)} async-done(((bf16[4,2,48,1280]{3,2,1,0:T(8,128)(2,1)}), bf16[4,2,48,1280]{3,2,1,0:T(8,128)(2,1)S(1)}, u32[]{:S(2)}, u32[]{:S(2)}) %all-to-all-start) | async-done | bytes 983072 | tf_op jit(solution)/shard_map/all_to_all | solution.py:111
  36.5 12.0 %all_gather.8.q_ref = bf16[2,4,48,1280]{3,2,1,0:T(8,128)(2,1)S(1)} all-gather(bf16[2,1,48,1280]{3,2,1,0:T(8,128)(2,1)S(1)} %bitcast_select_fusion), channel_id=1, replica_groups=mesh['z'=4,'y'=4,'x'=4,'c'=2] {'x'}, dimensions={1}, use_global_device_ids=true | all-gather | bytes 1228800 | tf_op jit(solution)/shard_map/all_gather | solution.py:118
  48.5 7.0 %collective-permute-start = (bf16[2,4,48,1280]{3,2,1,0:T(8,128)(2,1)S(1)}, bf16[2,4,48,1280]{3,2,1,0:T(8,128)(2,1)S(1)}, u32[]{:S(2)}, u32[]{:S(2)}) collective-permute-start(bf16[2,4,48,1280]{3,2,1,0:T(8,128)(2,1)S(1)} %all_gather.8.q_ref), channel_id=1, source_target_pairs={{0,1},{1,0},{2,3},{3,2},{4,5},{5,4},{6,7},{7,6},{8,9},{9,8},{10,11... | collective-permute-start | bytes 2949128 | tf_op jit(solution)/shard_map/ppermute | solution.py:119
  56.3 1.3 fusion.21
  57.6 0.8 convolution_convert_fusion
  58.3 16.0 %shard_map.86 = (f32[8,4,96,1]{3,2,1,0:T(8,128)S(1)}, f32[8,4,96,1]{3,2,1,0:T(8,128)S(1)}, f32[8,4,96,128]{3,2,1,0:T(8,128)S(1)}) custom-call(s32[3]{0:T(128)S(1)} %get-tuple-element.25.live_ref, bf16[2,4,48,1280]{3,2,1,0:T(8,128)(2,1)S(1)} %all_gather.8.q_ref, bf16[2,2048,2048]{2,1,0:T(8,128)(2,1)} %kv_ref.3), custom_call_target="tpu_custom_call" | custom-call | tf_op jit(solution)/shard_map/pallas_call | solution.py:69
  74.4 1.1 copy-done
  75.5 1.2 copy-done.2
  76.7 2.5 %copy.18 = f32[8,4,96,1]{2,1,3,0:T(4,128)} copy(f32[8,4,96,1]{3,2,1,0:T(8,128)} %copy-done) | data formatting | bytes 24576 | tf_op jit(solution)/shard_map/pallas_call | solution.py:69
  79.2 1.1 copy.22
  80.3 16.0 %shard_map.87 = (f32[8,4,96,1]{3,2,1,0:T(8,128)S(1)}, f32[8,4,96,1]{3,2,1,0:T(8,128)S(1)}, f32[8,4,96,128]{3,2,1,0:T(8,128)S(1)}) custom-call(s32[3]{0:T(128)S(1)} %get-tuple-element.26.live_ref, bf16[2,4,48,1280]{3,2,1,0:T(8,128)(2,1)S(1)} %collective-permute-done.q_ref, bf16[2,2048,2048]{2,1,0:T(8,128)(2,1)} %kv_ref.3), custom_call_target="tpu_custom_call" | custom-call | tf_op jit(solution)/shard_map/pallas_call | solution.py:69
  96.3 1.1 copy-done.1
  97.5 1.2 copy-done.3
  98.6 2.5 %copy.19 = f32[8,4,96,1]{2,1,3,0:T(4,128)} copy(f32[8,4,96,1]{3,2,1,0:T(8,128)} %copy-done.1) | data formatting | bytes 24576 | tf_op jit(solution)/shard_map/pallas_call | solution.py:69
  101.2 1.1 copy.23
  102.2 0.8 maximum_select_fusion.1
  103.3 3.5 %maximum_select_fusion = f32[8,8,96,128]{3,2,1,0:T(8,128)S(1)} fusion(f32[8,4,96,128]{3,2,1,0:T(8,128)} %copy-done.3, f32[8,4,96,128]{3,2,1,0:T(8,128)} %copy-done.2, pred[]{:T(512)S(6)} %eq.22), kind=kLoop, calls=%fused_computation.6 | loop fusion | flops 2359296 | bytes 6291457 | tf_op jit(solution)/shard_map/jit(_where)/select_n | solution.py:132
  107.0 6.0 %all_to_all.15 = f32[4,2,784,128]{3,2,0,1:T(8,128)S(1)} all-to-all(f32[4,2,784,128]{3,2,0,1:T(8,128)S(1)} %maximum_maximum_fusion), channel_id=1, replica_groups=mesh['z'=4,'y'=4,'x'=4,'c'=2] {'c'}, dimensions={1} | all-to-all | bytes 6422528 | tf_op jit(solution)/shard_map/all_to_all | solution.py:164
  113.0 1.7 %copy-done.5 = f32[4,2,784,128]{3,2,0,1:T(8,128)} copy-done((f32[4,2,784,128]{3,2,0,1:T(8,128)}, f32[4,2,784,128]{3,2,0,1:T(8,128)S(1)}, u32[]{:S(2)}) %copy-start.5) | copy-done | bytes 3211288
  114.7 0.9 fusion.17
  115.7 2.5 %fusion = f32[4,768,128]{2,1,0:T(8,128)S(1)} fusion(f32[4,2,784,128]{3,2,0,1:T(8,128)} %copy-done.5, f32[4,2,768]{2,0,1:T(4,128)S(1)} %copy.30), kind=kLoop, calls=%fused_computation.5 | loop fusion | flops 1179648 | bytes 4743168 | tf_op jit(solution)/shard_map/reduce_sum | solution.py:83
  118.2 1.3 maximum_maximum_fusion.1
  119.5 4.4 %all-to-all-start.2 = ((f32[4,784,128]{2,1,0:T(8,128)}), f32[4,784,128]{2,1,0:T(8,128)}, u32[]{:S(2)}, u32[]{:S(2)}) async-start(f32[4,784,128]{2,1,0:T(8,128)} %maximum_maximum_fusion.1), calls=%async_computation.2 | async-start | bytes 3211264 | tf_op jit(solution)/shard_map/all_to_all | solution.py:166
  126.2 18.5 %all-to-all-done.2 = f32[4,784,128]{2,1,0:T(8,128)} async-done(((f32[4,784,128]{2,1,0:T(8,128)}), f32[4,784,128]{2,1,0:T(8,128)}, u32[]{:S(2)}, u32[]{:S(2)}) %all-to-all-start.2) | async-done | bytes 1605664 | tf_op jit(solution)/shard_map/all_to_all | solution.py:166
  144.7 0.8 slice_bitcast_fusion
  145.6 1.5 %slice.53 = f32[4,768,128]{2,1,0:T(8,128)S(1)} slice(f32[4,784,128]{2,1,0:T(8,128)} %all-to-all-done.2), slice={[0:4], [0:768], [0:128]} | slice | bytes 3145728 | tf_op jit(solution)/shard_map/slice | solution.py:154
  148.3 0.9 copy.46
  (67 shorter events, 6.2 us)
Async XLA Ops:
  18.7 5.5 %copy-start.4 = (s32[32]{0:T(128)S(1)}, s32[32]{0:T(128)}, u32[]{:S(2)}) copy-start(s32[32]{0:T(128)} %param.12) | copy-start | bytes 388
  19.8 36.4 %copy-start.11 = (s32[2]{0:T(128)S(1)}, s32[2]{0:T(128)}, u32[]{:S(2)}) copy-start(s32[2]{0:T(128)} %param.10) | copy-start | bytes 28
  19.8 37.7 %copy-start.7 = (bf16[2,48,256]{2,1,0:T(8,128)(2,1)S(1)}, bf16[2,48,256]{2,1,0:T(8,128)(2,1)}, u32[]{:S(2)}) copy-start(bf16[2,48,256]{2,1,0:T(8,128)(2,1)} %param.8) | copy-start | bytes 147460
  19.8 37.7 %copy-start.10 = (s32[2,8]{1,0:T(2,128)S(1)}, s32[2,8]{1,0:T(2,128)}, u32[]{:S(2)}) copy-start(s32[2,8]{1,0:T(2,128)} %param.13) | copy-start | bytes 196
  19.8 16.0 %all-to-all-start = ((bf16[4,2,48,1280]{3,2,1,0:T(8,128)(2,1)}), bf16[4,2,48,1280]{3,2,1,0:T(8,128)(2,1)S(1)}, u32[]{:S(2)}, u32[]{:S(2)}) async-start(bf16[4,2,48,1280]{3,2,1,0:T(8,128)(2,1)} %broadcast_select_fusion), calls=%async_computation | async-start | bytes 1966080 | tf_op jit(solution)/shard_map/all_to_all | solution.py:111
  48.5 31.8 %collective-permute-start = (bf16[2,4,48,1280]{3,2,1,0:T(8,128)(2,1)S(1)}, bf16[2,4,48,1280]{3,2,1,0:T(8,128)(2,1)S(1)}, u32[]{:S(2)}, u32[]{:S(2)}) collective-permute-start(bf16[2,4,48,1280]{3,2,1,0:T(8,128)(2,1)S(1)} %all_gather.8.q_ref), channel_id=1, source_target_pairs={{0,1},{1,0},{2,3},{3,2},{4,5},{5,4},{6,7},{7,6},{8,9},{9,8},{10,11... | collective-permute-start | bytes 2949128 | tf_op jit(solution)/shard_map/ppermute | solution.py:119
  74.4 1.2 copy-start
  75.5 1.2 copy-start.2
  96.3 1.2 copy-start.1
  97.5 1.2 copy-start.3
  98.6 3.6 %copy-start.6 = (f32[8,4,96,1]{2,1,3,0:T(4,128)S(1)}, f32[8,4,96,1]{2,1,3,0:T(4,128)}, u32[]{:S(2)}) copy-start(f32[8,4,96,1]{2,1,3,0:T(4,128)} %copy.18) | copy-start | bytes 36868
  103.2 3.5 %copy-start.8 = (f32[784]{0:T(1024)S(1)}, f32[784]{0:T(1024)}, u32[]{:S(2)}) copy-start(f32[784]{0:T(1024)} %pad.17.clone) | copy-start | bytes 9412
  113.0 1.7 %copy-start.5 = (f32[4,2,784,128]{3,2,0,1:T(8,128)}, f32[4,2,784,128]{3,2,0,1:T(8,128)S(1)}, u32[]{:S(2)}) copy-start(f32[4,2,784,128]{3,2,0,1:T(8,128)S(1)} %all_to_all.15) | copy-start | bytes 9633796
  119.5 25.2 %all-to-all-start.2 = ((f32[4,784,128]{2,1,0:T(8,128)}), f32[4,784,128]{2,1,0:T(8,128)}, u32[]{:S(2)}, u32[]{:S(2)}) async-start(f32[4,784,128]{2,1,0:T(8,128)} %maximum_maximum_fusion.1), calls=%async_computation.2 | async-start | bytes 3211264 | tf_op jit(solution)/shard_map/all_to_all | solution.py:166
  124.0 0.7 copy-start.9

commit v6 on v5

--- a/solution.py
+++ b/solution.py
@@ -12,66 +12,94 @@
 NEG = -1e30
 
 
-def attn_kernel(live_ref, q_ref, kv_ref, m_ref, l_ref, acc_ref, *, n_blk, scale, groups):
+def attn_kernel(live_ref, q_ref, kv_ref, *refs, n_blk, scale, groups):
+    m_ref, l_ref, acc_ref = refs[-3:]
     slot = pl.program_id(0)
     live = live_ref[slot]
     tree_len = q_ref.shape[0]
     rows = tree_len * groups
-    q = jnp.concatenate([q_ref[:, g * HEAD_WIDTH:(g + 1) * HEAD_WIDTH] for g in range(groups)], axis=0)
-    outs_m, outs_l, outs_a = [], [], []
-    for c0 in range(0, rows, rows):
-        qc = q[c0:c0 + rows]
-        run = None
-        for b in range(n_blk):
-            keys = kv_ref[b * BLK:(b + 1) * BLK, 0:HEAD_WIDTH]
-            vals = kv_ref[b * BLK:(b + 1) * BLK, HEAD_WIDTH:2 * HEAD_WIDTH]
-            s = lax.dot_general(qc, keys, (((1,), (1,)), ((), ())), preferred_element_type=jnp.float32) * scale
-            pos = b * BLK + lax.broadcasted_iota(jnp.int32, (1, BLK), 1)
-            bias = jnp.where(pos < live, jnp.float32(0.0), jnp.float32(NEG))
-            s = s + bias
-            mb = jnp.max(s, axis=1, keepdims=True)
-            w = jnp.exp(s - mb)
-            lb = jnp.sum(w, axis=1, keepdims=True)
-            ob = jnp.dot(w.astype(jnp.bfloat16), vals, preferred_element_type=jnp.float32)
-            if run is None:
-                run = (mb, lb, ob)
-            else:
-                rm, rl, ra = run
-                nm = jnp.maximum(rm, mb); fa = jnp.exp(rm - nm); fb = jnp.exp(mb - nm)
-                run = (nm, rl * fa + lb * fb, ra * fa + ob * fb)
-        outs_m.append(run[0]); outs_l.append(run[1]); outs_a.append(run[2])
-    rm = jnp.concatenate(outs_m, 0); rl = jnp.concatenate(outs_l, 0); ra = jnp.concatenate(outs_a, 0)
-    parts = m_ref.shape[0]
+    q = jnp.concatenate(
+        [q_ref[:, g * HEAD_WIDTH:(g + 1) * HEAD_WIDTH] for g in range(groups)], axis=0
+    )
+    run = None
+    for b in range(n_blk):
+        keys = kv_ref[b * BLK:(b + 1) * BLK, 0:HEAD_WIDTH]
+        vals = kv_ref[b * BLK:(b + 1) * BLK, HEAD_WIDTH:2 * HEAD_WIDTH]
+        s = lax.dot_general(
+            q, keys, (((1,), (1,)), ((), ())), preferred_element_type=jnp.float32
+        ) * scale
+        pos = b * BLK + lax.broadcasted_iota(jnp.int32, (1, BLK), 1)
+        s = s + jnp.where(pos < live, jnp.float32(0.0), jnp.float32(NEG))
+        mb = jnp.max(s, axis=1, keepdims=True)
+        w = jnp.exp(s - mb)
+        lb = jnp.sum(w, axis=1, keepdims=True)
+        ob = jnp.dot(w.astype(jnp.bfloat16), vals, preferred_element_type=jnp.float32)
+        if run is None:
+            run = (mb, lb, ob)
+        else:
+            rm, rl, ra = run
+            nm = jnp.maximum(rm, mb)
+            fa = jnp.exp(rm - nm)
+            fb = jnp.exp(mb - nm)
+            run = (nm, rl * fa + lb * fb, ra * fa + ob * fb)
+    rm, rl, ra = run
+    m_ref[...] = jnp.transpose(jnp.broadcast_to(rm, (rows, HEAD_WIDTH)))[0:8]
+    l_ref[...] = jnp.transpose(jnp.broadcast_to(rl, (rows, HEAD_WIDTH)))[0:8]
+    parts = acc_ref.shape[0]
     tok = tree_len // parts
     for j in range(parts):
         for g in range(groups):
             src = slice(g * tree_len + j * tok, g * tree_len + (j + 1) * tok)
-            dst = slice(g * tok, (g + 1) * tok)
-            m_ref[j, dst, :] = rm[src]
-            l_ref[j, dst, :] = rl[src]
-            acc_ref[j, dst, :] = ra[src]
-
-def local_attention(q_all, kv, pref, seq_count, nc):
-    slots, kvh, tree_len, _ = q_all.shape
+            acc_ref[j, g * tok:(g + 1) * tok, :] = ra[src]
+
+
+def local_attention(q_half, kv, pref, seq_count, nc, prev=None):
+    slots, kh, tree_len, cols = q_half.shape
     positions = kv.shape[1]
-    groups = (q_all.shape[3] - 2 * HEAD_WIDTH) // HEAD_WIDTH
+    groups = (cols - 2 * HEAD_WIDTH) // HEAD_WIDTH
+    kvh = kh * nc
     rows = tree_len * groups
     per_slot = seq_count // slots
     sub = rows // per_slot
-    kern = functools.partial(attn_kernel, n_blk=positions // BLK, scale=HEAD_WIDTH ** (-0.5), groups=groups)
+    kern = functools.partial(
+        attn_kernel, n_blk=positions // BLK, scale=HEAD_WIDTH ** (-0.5), groups=groups
+    )
+    in_specs = [
+        pl.BlockSpec((None, None, tree_len, groups * HEAD_WIDTH), lambda i, k, lv: (i, k, 0, 0)),
+        pl.BlockSpec((None, positions, 2 * HEAD_WIDTH), lambda i, k, lv: (i, 0, k * nc + lv[slots])),
+    ]
+    operands = [pref, q_half, kv]
+    aliases = {}
+    if prev is not None:
+        in_specs += [pl.BlockSpec(memory_space=pl.ANY)] * 3
+        operands += list(prev)
+        aliases = {3: 0, 4: 1, 5: 2}
     grid_spec = pltpu.PrefetchScalarGridSpec(
-        num_scalar_prefetch=1, grid=(slots, kvh),
-        in_specs=[pl.BlockSpec((None, None, tree_len, groups * HEAD_WIDTH), lambda i, k, lv: (i, k, 0, 0)),
-                  pl.BlockSpec((None, positions, 2 * HEAD_WIDTH), lambda i, k, lv: (i, 0, k * nc + lv[slots]))],
-        out_specs=[pl.BlockSpec((per_slot, None, sub, 1), lambda i, k, lv: (i, k, 0, 0)),
-                   pl.BlockSpec((per_slot, None, sub, 1), lambda i, k, lv: (i, k, 0, 0)),
-                   pl.BlockSpec((per_slot, None, sub, HEAD_WIDTH), lambda i, k, lv: (i, k, 0, 0))])
-    return pl.pallas_call(kern, grid_spec=grid_spec,
-        out_shape=[jax.ShapeDtypeStruct((seq_count, kvh, sub, 1), jnp.float32),
-                   jax.ShapeDtypeStruct((seq_count, kvh, sub, 1), jnp.float32),
-                   jax.ShapeDtypeStruct((seq_count, kvh, sub, HEAD_WIDTH), jnp.float32)],
-        compiler_params=pltpu.CompilerParams(dimension_semantics=("arbitrary", "arbitrary"), vmem_limit_bytes=48 * 1024 * 1024),
-    )(pref, q_all, kv)
+        num_scalar_prefetch=1,
+        grid=(slots, kh),
+        in_specs=in_specs,
+        out_specs=[
+            pl.BlockSpec((None, None, 8, rows), lambda i, k, lv: (i, lv[slots] * kh + k, 0, 0)),
+            pl.BlockSpec((None, None, 8, rows), lambda i, k, lv: (i, lv[slots] * kh + k, 0, 0)),
+            pl.BlockSpec(
+                (per_slot, None, sub, HEAD_WIDTH), lambda i, k, lv: (i, lv[slots] * kh + k, 0, 0)
+            ),
+        ],
+    )
+    return pl.pallas_call(
+        kern,
+        grid_spec=grid_spec,
+        out_shape=[
+            jax.ShapeDtypeStruct((slots, kvh, 8, rows), jnp.float32),
+            jax.ShapeDtypeStruct((slots, kvh, 8, rows), jnp.float32),
+            jax.ShapeDtypeStruct((seq_count, kvh, sub, HEAD_WIDTH), jnp.float32),
+        ],
+        input_output_aliases=aliases,
+        compiler_params=pltpu.CompilerParams(
+            dimension_semantics=("arbitrary", "arbitrary"),
+            vmem_limit_bytes=48 * 1024 * 1024,
+        ),
+    )(*operands)
 
 
 def merge_pair(m, l, acc, axis):
@@ -122,21 +150,20 @@
     kv_heads = kv_cache.shape[2] // (2 * HEAD_WIDTH)
     groups = q_cols // HEAD_WIDTH
     live = jnp.clip(cache_lengths - position * positions, 0, positions).astype(jnp.int32)
-    pm_a, pl_a, pa_a = local_attention(own_x, kv_cache, jnp.concatenate([live, ci[None]]), seq_count, nc)
-    pm_b, pl_b, pa_b = local_attention(
-        other_x, kv_cache, jnp.concatenate([live, (1 - ci)[None]]), seq_count, nc
+    first_out = local_attention(own_x, kv_cache, jnp.concatenate([live, ci[None]]), seq_count, nc)
+    m_rows, l_rows, part_acc = local_attention(
+        other_x, kv_cache, jnp.concatenate([live, (1 - ci)[None]]), seq_count, nc, prev=first_out
     )
     first = ci == 0
-
-    def by_parity(a, b):
-        return jnp.where(first, jnp.concatenate([a, b], axis=1), jnp.concatenate([b, a], axis=1))
-
-    part_m = by_parity(pm_a, pm_b)
-    part_l = by_parity(pl_a, pl_b)
-    part_acc = by_parity(pa_a, pa_b)
-    q_all = jnp.where(
-        first, jnp.concatenate([own_x, other_x], axis=1), jnp.concatenate([other_x, own_x], axis=1)
-    )
+    per_slot = seq_count // local_reqs
+    tok = tree_len // per_slot
+
+    def dest_major(rows_arr):
+        r = rows_arr[:, :, 0, :].reshape(local_reqs, kv_heads, groups, per_slot, tok)
+        return r.transpose(0, 3, 1, 2, 4).reshape(seq_count, kv_heads, groups * tok)
+
+    part_m = dest_major(m_rows)
+    part_l = dest_major(l_rows)
     sub = part_acc.shape[2]
     rows_acc = kv_heads * sub
     stat_rows = rows_acc // HEAD_WIDTH
@@ -166,11 +193,15 @@
     pk = lax.all_to_all(pack(a1, m1, l1), "x", 0, 0, tiled=True)
     rm, rl, acc = unpack(pk)
 
-    per_slot = seq_count // local_reqs
-    tok = tree_len // per_slot
     my_slot = position // per_slot
     my_tok0 = (position % per_slot) * tok
-    mine_all = lax.dynamic_index_in_dim(q_all, my_slot, 0, keepdims=False)
+    mine_own = lax.dynamic_index_in_dim(own_x, my_slot, 0, keepdims=False)
+    mine_other = lax.dynamic_index_in_dim(other_x, my_slot, 0, keepdims=False)
+    mine_all = jnp.where(
+        first,
+        jnp.concatenate([mine_own, mine_other], axis=0),
+        jnp.concatenate([mine_other, mine_own], axis=0),
+    )
     q_mine = lax.dynamic_slice_in_dim(mine_all[..., :q_cols], my_tok0, tok, 1).reshape(
         kv_heads, tok, groups, HEAD_WIDTH
     )

time: 150 us -> 131 us (0.87)
  local copies, waits for them, and re-layouts: 20.5 us -> 12.3 us
  other arithmetic: 15.4 us -> 7.38 us
    pallas_call x4 -> x0, local copies, waits for them, and re-layouts: 7.19 us -> none  [local_attention(): pl.pallas_call(kern, grid_spec=grid_spec, out_shape=[jax.ShapeDtypeStruct...]
    unnamed x29 -> x15, local copies, waits for them, and re-layouts: 7.22 us -> 0.94 us
    another operation x0 -> x6, local copies, waits for them, and re-layouts: none -> 4.37 us  [the longest x4 2.13 us: dest_major(): rows_arr[:, :, 0, :].reshape(local_reqs, kv_heads, groups, per_slot, tok)]
    select_n x2 -> x1, other arithmetic: 4.32 us -> 0.15 us  [body(): jnp.where(first, jnp.concatenate([mine_own, mine_other], axis=0), jnp.con...]
    squeeze x0 -> x2, local copies, waits for them, and re-layouts: none -> 2.93 us  [the longest x1 1.86 us: body(): mine_own = lax.dynamic_index_in_dim(own_x, my_slot, 0, keepdims=False)]
  transfers between devices with their start and end apart: 3 -> 3, of which waited for: 2 -> 2; matrix products, arithmetic and copies ran while one was open for 6% -> 5% of each run, Pallas kernels for 11% -> 12%
where the time goes in v6:
time: 131 us; the launch traced here: 130 us
  blocking collectives  33.3 us (25%)
  Pallas kernels  30.8 us (24%)
  waiting for transfers between devices  29 us (22%)
  starting transfers between devices  15.1 us (12%)
  local copies, waits for them, and re-layouts  12.3 us (9%)
  other arithmetic  7.38 us (6%)
  matrix products  1.48 us (1%)
    pallas_call x2, Pallas kernels, local_attention(): pl.pallas_call(kern, grid_spec=grid_spec, out_shape=[jax.ShapeDtypeStruct...  30.8 us
    all_to_all x1, waiting for transfers between devices, body(): pk = lax.all_to_all(pack(a1, m1, l1), 'x', 0, 0, tiled=True)  17.3 us
    all_gather x1, blocking collectives, body(): held = lax.all_gather(both, 'z', axis=0, tiled=True)  15 us
    all_gather x1, blocking collectives, body(): own_x = lax.all_gather(own, 'x', axis=1, tiled=False)  12.4 us
    all_to_all x1, waiting for transfers between devices, body(): recv = lax.all_to_all(send, 'y', 0, 0, tiled=True)  11.6 us
    ppermute x1, starting transfers between devices, body(): other_x = lax.ppermute(own_x, 'c', perm=[(0, 1), (1, 0)])  7.33 us
    all_to_all x1, blocking collectives, body(): pk = lax.all_to_all(pk, 'c', 1, 1, tiled=True)  5.95 us
    all_to_all x1, starting transfers between devices, body(): recv = lax.all_to_all(send, 'y', 0, 0, tiled=True)  4.18 us
  transfers between devices with their start and end apart: 3, of which 2 were waited for; matrix products, arithmetic and copies ran while one was open for 5% of the time, Pallas kernels for 12%

profile of v6, /device:TPU:1, one launch (start us, length us, event | category | flops | bytes accessed | tf_op | source)
XLA Modules:
  0.0 130.3 jit_solution(10158008160919887725)
XLA Ops:
  0.7 1.3 gather_fusion
  2.1 1.0 pad_maximum_fusion
  3.1 15.0 %all_gather.7 = bf16[8,48,1280]{2,1,0:T(8,128)(2,1)S(1)} all-gather(bf16[2,48,1280]{2,1,0:T(8,128)(2,1)S(1)} %pad_maximum_fusion), channel_id=1, replica_groups=mesh['z'=4,'y'=4,'x'=4,'c'=2] {'z'}, dimensions={0}, use_global_device_ids=true | all-gather | bytes 1228800 | tf_op jit(solution)/shard_map/all_gather | solution.py:133
  18.1 0.6 gather_fusion.1
  18.7 1.1 broadcast_select_fusion
  19.8 4.2 %all-to-all-start = ((bf16[4,2,48,1280]{3,2,1,0:T(8,128)(2,1)}), bf16[4,2,48,1280]{3,2,1,0:T(8,128)(2,1)S(1)}, u32[]{:S(2)}, u32[]{:S(2)}) async-start(bf16[4,2,48,1280]{3,2,1,0:T(8,128)(2,1)} %broadcast_select_fusion), calls=%async_computation | async-start | bytes 1966080 | tf_op jit(solution)/shard_map/all_to_all | solution.py:139
  24.1 11.6 %all-to-all-done = bf16[4,2,48,1280]{3,2,1,0:T(8,128)(2,1)S(1)} async-done(((bf16[4,2,48,1280]{3,2,1,0:T(8,128)(2,1)}), bf16[4,2,48,1280]{3,2,1,0:T(8,128)(2,1)S(1)}, u32[]{:S(2)}, u32[]{:S(2)}) %all-to-all-start) | async-done | bytes 983072 | tf_op jit(solution)/shard_map/all_to_all | solution.py:139
  35.7 0.6 gather_fusion.2
  36.4 12.4 %all_gather.8.q_ref = bf16[2,4,48,1280]{3,2,1,0:T(8,128)(2,1)} all-gather(bf16[2,1,48,1280]{3,2,1,0:T(8,128)(2,1)S(1)} %bitcast_select_fusion), channel_id=1, replica_groups=mesh['z'=4,'y'=4,'x'=4,'c'=2] {'x'}, dimensions={1}, use_global_device_ids=true | all-gather | bytes 1228800 | tf_op jit(solution)/shard_map/all_gather | solution.py:146
  48.8 7.3 %collective-permute-start = (bf16[2,4,48,1280]{3,2,1,0:T(8,128)(2,1)}, bf16[2,4,48,1280]{3,2,1,0:T(8,128)(2,1)}, u32[]{:S(2)}, u32[]{:S(2)}) collective-permute-start(bf16[2,4,48,1280]{3,2,1,0:T(8,128)(2,1)} %all_gather.8.q_ref), channel_id=1, source_target_pairs={{0,1},{1,0},{2,3},{3,2},{4,5},{5,4},{6,7},{7,6},{8,9},{9,8},{10,11... | collective-permute-start | bytes 2949128 | tf_op jit(solution)/shard_map/ppermute | solution.py:147
  56.3 0.7 fusion.17
  57.0 0.8 convolution_convert_fusion
  57.8 15.4 %shard_map.86 = (f32[2,8,8,384]{3,2,1,0:T(8,128)S(1)}, f32[2,8,8,384]{3,2,1,0:T(8,128)S(1)}, f32[8,8,96,128]{3,2,1,0:T(8,128)S(1)}) custom-call(s32[3]{0:T(128)S(1)} %get-tuple-element.25.live_ref, bf16[2,4,48,1280]{3,2,1,0:T(8,128)(2,1)} %all_gather.8.q_ref, bf16[2,2048,2048]{2,1,0:T(8,128)(2,1)} %kv_ref.3), custom_call_target="tpu_custom_call" | custom-call | tf_op jit(solution)/shard_map/pallas_call | solution.py:89
  73.2 1.9 %dynamic-slice_bitcast_fusion.1 = bf16[4,48,1280]{2,1,0:T(8,128)(2,1)} fusion(bf16[2,4,48,1280]{3,2,1,0:T(8,128)(2,1)} %all_gather.8.q_ref, s32[]{:T(128)S(6)} %select_n.167), kind=kLoop, calls=%fused_computation.18 | loop fusion | bytes 983044 | tf_op jit(solution)/shard_map/jit(dynamic_index_in_dim)/squeeze | solution.py:198
  75.1 15.4 %shard_map.87 = (f32[2,8,8,384]{3,2,1,0:T(8,128)S(1)}, f32[2,8,8,384]{3,2,1,0:T(8,128)S(1)}, f32[8,8,96,128]{3,2,1,0:T(8,128)S(1)}) custom-call(s32[3]{0:T(128)S(1)} %get-tuple-element.26.live_ref, bf16[2,4,48,1280]{3,2,1,0:T(8,128)(2,1)} %collective-permute-done.q_ref, ...), custom_call_target="tpu_custom_call", output_to_operand_aliasing={{0}: (3, {}), {1}: (4, {}), {2}: (5, {})} | custom-call | tf_op jit(solution)/shard_map/pallas_call | solution.py:89
  90.6 0.3 reshape_squeeze.7
  91.0 0.7 copy.74
  91.7 1.1 reshape_reshape_reshape.7
  92.8 0.3 reshape_squeeze.6
  93.2 0.7 copy.75
  93.9 1.1 reshape_reshape_reshape.6
  95.3 6.0 %all_to_all.15 = f32[4,2,784,128]{3,2,0,1:T(8,128)S(1)} all-to-all(f32[4,2,784,128]{3,2,0,1:T(8,128)S(1)} %maximum_maximum_fusion), channel_id=1, replica_groups=mesh['z'=4,'y'=4,'x'=4,'c'=2] {'c'}, dimensions={1} | all-to-all | bytes 6422528 | tf_op jit(solution)/shard_map/all_to_all | solution.py:191
  101.4 1.1 fusion
  102.5 1.3 %maximum_maximum_fusion.1 = f32[4,784,128]{2,1,0:T(8,128)} fusion(f32[4,6,128]{2,1,0:T(8,128)S(1)} %fusion.13, f32[4,6,128]{2,1,0:T(8,128)S(1)} %get-tuple-element.17, f32[4,768,128]{2,1,0:T(8,128)S(1)} %fusion, f32[784]{0:T(1024)S(1)} %pad.17.clone), kind=kLoop, calls=%fused_computation.8 | loop fusion | flops 1204224 | bytes 3206208 | tf_op jit(solution)/shard_map/concatenate | solution.py:177
  103.8 3.6 %all-to-all-start.2 = ((f32[4,784,128]{2,1,0:T(8,128)}), f32[4,784,128]{2,1,0:T(8,128)S(1)}, u32[]{:S(2)}, u32[]{:S(2)}) async-start(f32[4,784,128]{2,1,0:T(8,128)} %maximum_maximum_fusion.1), calls=%async_computation.2 | async-start | bytes 3211264 | tf_op jit(solution)/shard_map/all_to_all | solution.py:193
  107.4 1.1 dynamic-slice_bitcast_fusion
  109.3 0.4 fusion.33
  109.9 0.3 fusion.6
  110.3 0.4 fusion.4
  110.8 17.3 %all-to-all-done.2 = f32[4,784,128]{2,1,0:T(8,128)S(1)} async-done(((f32[4,784,128]{2,1,0:T(8,128)}), f32[4,784,128]{2,1,0:T(8,128)S(1)}, u32[]{:S(2)}, u32[]{:S(2)}) %all-to-all-start.2) | async-done | bytes 1605664 | tf_op jit(solution)/shard_map/all_to_all | solution.py:193
  128.4 0.7 fusion.1
  129.5 0.9 copy.49
  (54 shorter events, 2.7 us)
Async XLA Ops:
  18.1 6.0 %copy-start = (s32[32]{0:T(128)S(1)}, s32[32]{0:T(128)}, u32[]{:S(2)}) copy-start(s32[32]{0:T(128)} %param.12) | copy-start | bytes 388
  18.7 37.5 %copy-start.4 = (s32[2]{0:T(128)S(1)}, s32[2]{0:T(128)}, u32[]{:S(2)}) copy-start(s32[2]{0:T(128)} %param.10) | copy-start | bytes 28
  18.7 38.3 %copy-start.2 = (bf16[2,48,256]{2,1,0:T(8,128)(2,1)S(1)}, bf16[2,48,256]{2,1,0:T(8,128)(2,1)}, u32[]{:S(2)}) copy-start(bf16[2,48,256]{2,1,0:T(8,128)(2,1)} %param.8) | copy-start | bytes 147460
  18.7 38.3 %copy-start.3 = (s32[2,8]{1,0:T(2,128)S(1)}, s32[2,8]{1,0:T(2,128)}, u32[]{:S(2)}) copy-start(s32[2,8]{1,0:T(2,128)} %param.13) | copy-start | bytes 196
  19.8 15.9 %all-to-all-start = ((bf16[4,2,48,1280]{3,2,1,0:T(8,128)(2,1)}), bf16[4,2,48,1280]{3,2,1,0:T(8,128)(2,1)S(1)}, u32[]{:S(2)}, u32[]{:S(2)}) async-start(bf16[4,2,48,1280]{3,2,1,0:T(8,128)(2,1)} %broadcast_select_fusion), calls=%async_computation | async-start | bytes 1966080 | tf_op jit(solution)/shard_map/all_to_all | solution.py:139
  48.8 26.3 %collective-permute-start = (bf16[2,4,48,1280]{3,2,1,0:T(8,128)(2,1)}, bf16[2,4,48,1280]{3,2,1,0:T(8,128)(2,1)}, u32[]{:S(2)}, u32[]{:S(2)}) collective-permute-start(bf16[2,4,48,1280]{3,2,1,0:T(8,128)(2,1)} %all_gather.8.q_ref), channel_id=1, source_target_pairs={{0,1},{1,0},{2,3},{3,2},{4,5},{5,4},{6,7},{7,6},{8,9},{9,8},{10,11... | collective-permute-start | bytes 2949128 | tf_op jit(solution)/shard_map/ppermute | solution.py:147
  102.4 6.0 %copy-start.1 = (bf16[4,48,1280]{2,1,0:T(8,128)(2,1)S(1)}, bf16[4,48,1280]{2,1,0:T(8,128)(2,1)}, u32[]{:S(2)}) copy-start(bf16[4,48,1280]{2,1,0:T(8,128)(2,1)} %dynamic-slice_bitcast_fusion.1) | copy-start | bytes 1474564
  103.8 24.3 %all-to-all-start.2 = ((f32[4,784,128]{2,1,0:T(8,128)}), f32[4,784,128]{2,1,0:T(8,128)S(1)}, u32[]{:S(2)}, u32[]{:S(2)}) async-start(f32[4,784,128]{2,1,0:T(8,128)} %maximum_maximum_fusion.1), calls=%async_computation.2 | async-start | bytes 3211264 | tf_op jit(solution)/shard_map/all_to_all | solution.py:193

commit v7 on v6

--- a/solution.py
+++ b/solution.py
@@ -21,36 +21,50 @@
     q = jnp.concatenate(
         [q_ref[:, g * HEAD_WIDTH:(g + 1) * HEAD_WIDTH] for g in range(groups)], axis=0
     )
-    run = None
-    for b in range(n_blk):
-        keys = kv_ref[b * BLK:(b + 1) * BLK, 0:HEAD_WIDTH]
-        vals = kv_ref[b * BLK:(b + 1) * BLK, HEAD_WIDTH:2 * HEAD_WIDTH]
-        s = lax.dot_general(
-            q, keys, (((1,), (1,)), ((), ())), preferred_element_type=jnp.float32
-        ) * scale
-        pos = b * BLK + lax.broadcasted_iota(jnp.int32, (1, BLK), 1)
-        s = s + jnp.where(pos < live, jnp.float32(0.0), jnp.float32(NEG))
-        mb = jnp.max(s, axis=1, keepdims=True)
-        w = jnp.exp(s - mb)
-        lb = jnp.sum(w, axis=1, keepdims=True)
-        ob = jnp.dot(w.astype(jnp.bfloat16), vals, preferred_element_type=jnp.float32)
-        if run is None:
-            run = (mb, lb, ob)
-        else:
-            rm, rl, ra = run
-            nm = jnp.maximum(rm, mb)
-            fa = jnp.exp(rm - nm)
-            fb = jnp.exp(mb - nm)
-            run = (nm, rl * fa + lb * fb, ra * fa + ob * fb)
-    rm, rl, ra = run
-    m_ref[...] = jnp.transpose(jnp.broadcast_to(rm, (rows, HEAD_WIDTH)))[0:8]
-    l_ref[...] = jnp.transpose(jnp.broadcast_to(rl, (rows, HEAD_WIDTH)))[0:8]
-    parts = acc_ref.shape[0]
-    tok = tree_len // parts
-    for j in range(parts):
-        for g in range(groups):
-            src = slice(g * tree_len + j * tok, g * tree_len + (j + 1) * tok)
-            acc_ref[j, g * tok:(g + 1) * tok, :] = ra[src]
+    def blocks(masked):
+        run = None
+        for b in range(n_blk):
+            keys = kv_ref[b * BLK:(b + 1) * BLK, 0:HEAD_WIDTH]
+            vals = kv_ref[b * BLK:(b + 1) * BLK, HEAD_WIDTH:2 * HEAD_WIDTH]
+            s = lax.dot_general(
+                q, keys, (((1,), (1,)), ((), ())), preferred_element_type=jnp.float32
+            ) * scale
+            if masked:
+                pos = b * BLK + lax.broadcasted_iota(jnp.int32, (1, BLK), 1)
+                s = s + jnp.where(pos < live, jnp.float32(0.0), jnp.float32(NEG))
+            mb = jnp.max(s, axis=1, keepdims=True)
+            w = jnp.exp(s - mb)
+            lb = jnp.sum(w, axis=1, keepdims=True)
+            ob = jnp.dot(w.astype(jnp.bfloat16), vals, preferred_element_type=jnp.float32)
+            if run is None:
+                run = (mb, lb, ob)
+            else:
+                rm, rl, ra = run
+                nm = jnp.maximum(rm, mb)
+                fa = jnp.exp(rm - nm)
+                fb = jnp.exp(mb - nm)
+                run = (nm, rl * fa + lb * fb, ra * fa + ob * fb)
+        write(*run)
+
+    def write(rm, rl, ra):
+        m_ref[...] = jnp.transpose(jnp.broadcast_to(rm, (rows, HEAD_WIDTH)))[0:8]
+        l_ref[...] = jnp.transpose(jnp.broadcast_to(rl, (rows, HEAD_WIDTH)))[0:8]
+        parts = acc_ref.shape[0]
+        tok = tree_len // parts
+        for j in range(parts):
+            for g in range(groups):
+                src = slice(g * tree_len + j * tok, g * tree_len + (j + 1) * tok)
+                acc_ref[j, g * tok:(g + 1) * tok, :] = ra[src]
+
+    full = live >= n_blk * BLK
+
+    @pl.when(full)
+    def _full():
+        blocks(False)
+
+    @pl.when(jnp.logical_not(full))
+    def _part():
+        blocks(True)
 
 
 def local_attention(q_half, kv, pref, seq_count, nc, prev=None):

time: 131 us -> 132 us (level)
  no operation moved by 1% of the time
where the time goes in v7:
time: 132 us
  blocking collectives  33.3 us (25%)
  Pallas kernels  32 us (24%)
  waiting for transfers between devices  28.8 us (22%)
  starting transfers between devices  15.3 us (12%)
  local copies, waits for them, and re-layouts  12.3 us (9%)
  other arithmetic  7.38 us (6%)
  matrix products  1.48 us (1%)
    pallas_call x2, Pallas kernels, local_attention(): pl.pallas_call(kern, grid_spec=grid_spec, out_shape=[jax.ShapeDtypeStruct...  32 us
    all_to_all x1, waiting for transfers between devices, body(): pk = lax.all_to_all(pack(a1, m1, l1), 'x', 0, 0, tiled=True)  17.2 us
    all_gather x1, blocking collectives, body(): held = lax.all_gather(both, 'z', axis=0, tiled=True)  15 us
    all_gather x1, blocking collectives, body(): own_x = lax.all_gather(own, 'x', axis=1, tiled=False)  12.4 us
    all_to_all x1, waiting for transfers between devices, body(): recv = lax.all_to_all(send, 'y', 0, 0, tiled=True)  11.6 us
    ppermute x1, starting transfers between devices, body(): other_x = lax.ppermute(own_x, 'c', perm=[(0, 1), (1, 0)])  7.33 us
    all_to_all x1, blocking collectives, body(): pk = lax.all_to_all(pk, 'c', 1, 1, tiled=True)  5.95 us
    all_to_all x1, starting transfers between devices, body(): recv = lax.all_to_all(send, 'y', 0, 0, tiled=True)  4.18 us
  transfers between devices with their start and end apart: 3, of which 2 were waited for; matrix products, arithmetic and copies ran while one was open for 5% of the time, Pallas kernels for 12%

profile of v7, /device:TPU:1, one launch (start us, length us, event | category | flops | bytes accessed | tf_op | source)
XLA Modules:
  0.0 131.6 jit_solution(2445435110332943868)
XLA Ops:
  0.7 1.3 gather_fusion
  2.1 1.0 pad_maximum_fusion
  3.1 15.0 %all_gather.7 = bf16[8,48,1280]{2,1,0:T(8,128)(2,1)S(1)} all-gather(bf16[2,48,1280]{2,1,0:T(8,128)(2,1)S(1)} %pad_maximum_fusion), channel_id=1, replica_groups=mesh['z'=4,'y'=4,'x'=4,'c'=2] {'z'}, dimensions={0}, use_global_device_ids=true | all-gather | bytes 1228800 | tf_op jit(solution)/shard_map/all_gather | solution.py:147
  18.1 0.6 gather_fusion.1
  18.7 1.1 broadcast_select_fusion
  19.8 4.2 %all-to-all-start = ((bf16[4,2,48,1280]{3,2,1,0:T(8,128)(2,1)}), bf16[4,2,48,1280]{3,2,1,0:T(8,128)(2,1)S(1)}, u32[]{:S(2)}, u32[]{:S(2)}) async-start(bf16[4,2,48,1280]{3,2,1,0:T(8,128)(2,1)} %broadcast_select_fusion), calls=%async_computation | async-start | bytes 1966080 | tf_op jit(solution)/shard_map/all_to_all | solution.py:153
  24.1 11.6 %all-to-all-done = bf16[4,2,48,1280]{3,2,1,0:T(8,128)(2,1)S(1)} async-done(((bf16[4,2,48,1280]{3,2,1,0:T(8,128)(2,1)}), bf16[4,2,48,1280]{3,2,1,0:T(8,128)(2,1)S(1)}, u32[]{:S(2)}, u32[]{:S(2)}) %all-to-all-start) | async-done | bytes 983072 | tf_op jit(solution)/shard_map/all_to_all | solution.py:153
  35.7 0.6 gather_fusion.2
  36.4 12.4 %all_gather.8.q_ref = bf16[2,4,48,1280]{3,2,1,0:T(8,128)(2,1)} all-gather(bf16[2,1,48,1280]{3,2,1,0:T(8,128)(2,1)S(1)} %bitcast_select_fusion), channel_id=1, replica_groups=mesh['z'=4,'y'=4,'x'=4,'c'=2] {'x'}, dimensions={1}, use_global_device_ids=true | all-gather | bytes 1228800 | tf_op jit(solution)/shard_map/all_gather | solution.py:160
  48.8 7.3 %collective-permute-start = (bf16[2,4,48,1280]{3,2,1,0:T(8,128)(2,1)}, bf16[2,4,48,1280]{3,2,1,0:T(8,128)(2,1)}, u32[]{:S(2)}, u32[]{:S(2)}) collective-permute-start(bf16[2,4,48,1280]{3,2,1,0:T(8,128)(2,1)} %all_gather.8.q_ref), channel_id=1, source_target_pairs={{0,1},{1,0},{2,3},{3,2},{4,5},{5,4},{6,7},{7,6},{8,9},{9,8},{10,11... | collective-permute-start | bytes 2949128 | tf_op jit(solution)/shard_map/ppermute | solution.py:161
  56.3 0.7 fusion.17
  57.0 0.8 convolution_convert_fusion
  57.8 16.0 %shard_map.86 = (f32[2,8,8,384]{3,2,1,0:T(8,128)S(1)}, f32[2,8,8,384]{3,2,1,0:T(8,128)S(1)}, f32[8,8,96,128]{3,2,1,0:T(8,128)S(1)}) custom-call(s32[3]{0:T(128)S(1)} %get-tuple-element.25.live_ref, bf16[2,4,48,1280]{3,2,1,0:T(8,128)(2,1)} %all_gather.8.q_ref, bf16[2,2048,2048]{2,1,0:T(8,128)(2,1)} %kv_ref.3), custom_call_target="tpu_custom_call" | custom-call | tf_op jit(solution)/shard_map/pallas_call | solution.py:103
  73.8 1.9 %dynamic-slice_bitcast_fusion.1 = bf16[4,48,1280]{2,1,0:T(8,128)(2,1)} fusion(bf16[2,4,48,1280]{3,2,1,0:T(8,128)(2,1)} %all_gather.8.q_ref, s32[]{:T(128)S(6)} %select_n.167), kind=kLoop, calls=%fused_computation.18 | loop fusion | bytes 983044 | tf_op jit(solution)/shard_map/jit(dynamic_index_in_dim)/squeeze | solution.py:212
  75.7 16.0 %shard_map.87 = (f32[2,8,8,384]{3,2,1,0:T(8,128)S(1)}, f32[2,8,8,384]{3,2,1,0:T(8,128)S(1)}, f32[8,8,96,128]{3,2,1,0:T(8,128)S(1)}) custom-call(s32[3]{0:T(128)S(1)} %get-tuple-element.26.live_ref, bf16[2,4,48,1280]{3,2,1,0:T(8,128)(2,1)} %collective-permute-done.q_ref, ...), custom_call_target="tpu_custom_call", output_to_operand_aliasing={{0}: (3, {}), {1}: (4, {}), {2}: (5, {})} | custom-call | tf_op jit(solution)/shard_map/pallas_call | solution.py:103
  91.9 0.3 reshape_squeeze.7
  92.2 0.7 copy.74
  92.9 1.1 reshape_reshape_reshape.7
  94.1 0.3 reshape_squeeze.6
  94.4 0.7 copy.75
  95.1 1.1 reshape_reshape_reshape.6
  96.5 6.0 %all_to_all.15 = f32[4,2,784,128]{3,2,0,1:T(8,128)S(1)} all-to-all(f32[4,2,784,128]{3,2,0,1:T(8,128)S(1)} %maximum_maximum_fusion), channel_id=1, replica_groups=mesh['z'=4,'y'=4,'x'=4,'c'=2] {'c'}, dimensions={1} | all-to-all | bytes 6422528 | tf_op jit(solution)/shard_map/all_to_all | solution.py:205
  102.6 1.1 fusion
  103.7 1.3 %maximum_maximum_fusion.1 = f32[4,784,128]{2,1,0:T(8,128)} fusion(f32[4,6,128]{2,1,0:T(8,128)S(1)} %fusion.13, f32[4,6,128]{2,1,0:T(8,128)S(1)} %get-tuple-element.17, f32[4,768,128]{2,1,0:T(8,128)S(1)} %fusion, f32[784]{0:T(1024)S(1)} %pad.17.clone), kind=kLoop, calls=%fused_computation.8 | loop fusion | flops 1204224 | bytes 3206208 | tf_op jit(solution)/shard_map/concatenate | solution.py:191
  105.0 3.7 %all-to-all-start.2 = ((f32[4,784,128]{2,1,0:T(8,128)}), f32[4,784,128]{2,1,0:T(8,128)S(1)}, u32[]{:S(2)}, u32[]{:S(2)}) async-start(f32[4,784,128]{2,1,0:T(8,128)} %maximum_maximum_fusion.1), calls=%async_computation.2 | async-start | bytes 3211264 | tf_op jit(solution)/shard_map/all_to_all | solution.py:207
  108.8 1.1 dynamic-slice_bitcast_fusion
  110.7 0.4 fusion.33
  111.3 0.3 fusion.6
  111.7 0.4 fusion.4
  112.2 17.2 %all-to-all-done.2 = f32[4,784,128]{2,1,0:T(8,128)S(1)} async-done(((f32[4,784,128]{2,1,0:T(8,128)}), f32[4,784,128]{2,1,0:T(8,128)S(1)}, u32[]{:S(2)}, u32[]{:S(2)}) %all-to-all-start.2) | async-done | bytes 1605664 | tf_op jit(solution)/shard_map/all_to_all | solution.py:207
  129.7 0.7 fusion.1
  130.7 0.9 copy.49
  (54 shorter events, 2.7 us)
Async XLA Ops:
  18.1 6.0 %copy-start = (s32[32]{0:T(128)S(1)}, s32[32]{0:T(128)}, u32[]{:S(2)}) copy-start(s32[32]{0:T(128)} %param.12) | copy-start | bytes 388
  18.7 37.5 %copy-start.4 = (s32[2]{0:T(128)S(1)}, s32[2]{0:T(128)}, u32[]{:S(2)}) copy-start(s32[2]{0:T(128)} %param.10) | copy-start | bytes 28
  18.7 38.3 %copy-start.2 = (bf16[2,48,256]{2,1,0:T(8,128)(2,1)S(1)}, bf16[2,48,256]{2,1,0:T(8,128)(2,1)}, u32[]{:S(2)}) copy-start(bf16[2,48,256]{2,1,0:T(8,128)(2,1)} %param.8) | copy-start | bytes 147460
  18.7 38.3 %copy-start.3 = (s32[2,8]{1,0:T(2,128)S(1)}, s32[2,8]{1,0:T(2,128)}, u32[]{:S(2)}) copy-start(s32[2,8]{1,0:T(2,128)} %param.13) | copy-start | bytes 196
  19.8 15.9 %all-to-all-start = ((bf16[4,2,48,1280]{3,2,1,0:T(8,128)(2,1)}), bf16[4,2,48,1280]{3,2,1,0:T(8,128)(2,1)S(1)}, u32[]{:S(2)}, u32[]{:S(2)}) async-start(bf16[4,2,48,1280]{3,2,1,0:T(8,128)(2,1)} %broadcast_select_fusion), calls=%async_computation | async-start | bytes 1966080 | tf_op jit(solution)/shard_map/all_to_all | solution.py:153
  48.8 26.9 %collective-permute-start = (bf16[2,4,48,1280]{3,2,1,0:T(8,128)(2,1)}, bf16[2,4,48,1280]{3,2,1,0:T(8,128)(2,1)}, u32[]{:S(2)}, u32[]{:S(2)}) collective-permute-start(bf16[2,4,48,1280]{3,2,1,0:T(8,128)(2,1)} %all_gather.8.q_ref), channel_id=1, source_target_pairs={{0,1},{1,0},{2,3},{3,2},{4,5},{5,4},{6,7},{7,6},{8,9},{9,8},{10,11... | collective-permute-start | bytes 2949128 | tf_op jit(solution)/shard_map/ppermute | solution.py:161
  103.7 6.2 %copy-start.1 = (bf16[4,48,1280]{2,1,0:T(8,128)(2,1)S(1)}, bf16[4,48,1280]{2,1,0:T(8,128)(2,1)}, u32[]{:S(2)}) copy-start(bf16[4,48,1280]{2,1,0:T(8,128)(2,1)} %dynamic-slice_bitcast_fusion.1) | copy-start | bytes 1474564
  105.0 24.3 %all-to-all-start.2 = ((f32[4,784,128]{2,1,0:T(8,128)}), f32[4,784,128]{2,1,0:T(8,128)S(1)}, u32[]{:S(2)}, u32[]{:S(2)}) async-start(f32[4,784,128]{2,1,0:T(8,128)} %maximum_maximum_fusion.1), calls=%async_computation.2 | async-start | bytes 3211264 | tf_op jit(solution)/shard_map/all_to_all | solution.py:207

commit v8 on v6

--- a/solution.py
+++ b/solution.py
@@ -6,6 +6,7 @@
 from jax.experimental import pallas as pl
 from jax.experimental.pallas import tpu as pltpu
 from jax.sharding import PartitionSpec as P
+
 
 HEAD_WIDTH = 128
 BLK = 1024
@@ -57,7 +58,6 @@
     slots, kh, tree_len, cols = q_half.shape
     positions = kv.shape[1]
     groups = (cols - 2 * HEAD_WIDTH) // HEAD_WIDTH
-    kvh = kh * nc
     rows = tree_len * groups
     per_slot = seq_count // slots
     sub = rows // per_slot
@@ -79,10 +79,10 @@
         grid=(slots, kh),
         in_specs=in_specs,
         out_specs=[
-            pl.BlockSpec((None, None, 8, rows), lambda i, k, lv: (i, lv[slots] * kh + k, 0, 0)),
-            pl.BlockSpec((None, None, 8, rows), lambda i, k, lv: (i, lv[slots] * kh + k, 0, 0)),
+            pl.BlockSpec((None, None, 8, rows), lambda i, k, lv: (i, k, 0, 0)),
+            pl.BlockSpec((None, None, 8, rows), lambda i, k, lv: (i, k, 0, 0)),
             pl.BlockSpec(
-                (per_slot, None, sub, HEAD_WIDTH), lambda i, k, lv: (i, lv[slots] * kh + k, 0, 0)
+                (per_slot, None, sub, HEAD_WIDTH), lambda i, k, lv: (i, k, 0, 0)
             ),
         ],
     )
@@ -90,9 +90,9 @@
         kern,
         grid_spec=grid_spec,
         out_shape=[
-            jax.ShapeDtypeStruct((slots, kvh, 8, rows), jnp.float32),
-            jax.ShapeDtypeStruct((slots, kvh, 8, rows), jnp.float32),
-            jax.ShapeDtypeStruct((seq_count, kvh, sub, HEAD_WIDTH), jnp.float32),
+            jax.ShapeDtypeStruct((slots, kh, 8, rows), jnp.float32),
+            jax.ShapeDtypeStruct((slots, kh, 8, rows), jnp.float32),
+            jax.ShapeDtypeStruct((seq_count, kh, sub, HEAD_WIDTH), jnp.float32),
         ],
         input_output_aliases=aliases,
         compiler_params=pltpu.CompilerParams(
@@ -112,7 +112,7 @@
     )
 
 
-def body(queries, draft_key_value, kv_cache, cache_lengths, ancestors, dealing, accepted_path):
+def body_inner(queries, draft_key_value, kv_cache, cache_lengths, ancestors, dealing, accepted_path):
     local_reqs = kv_cache.shape[0]
     tree_len = queries.shape[1]
     picker = (
@@ -122,12 +122,11 @@
         "rit,rtc->ric", picker, draft_key_value, preferred_element_type=jnp.float32
     ).astype(jnp.bfloat16)
 
-    nz, ny, nx, nc = (lax.axis_size(a) for a in ("z", "y", "x", "c"))
+    _, ny, nx, nc = (lax.axis_size(a) for a in ("z", "y", "x", "c"))
     zi, yi, xi, ci = (lax.axis_index(a) for a in ("z", "y", "x", "c"))
     seq_count = nx * nc
     position = xi * nc + ci
     q_cols = queries.shape[2]
-    d_cols = draft_key_value.shape[2]
 
     both = jnp.concatenate([queries, draft_key_value], axis=2)
     held = lax.all_gather(both, "z", axis=0, tiled=True)
@@ -150,24 +149,16 @@
     kv_heads = kv_cache.shape[2] // (2 * HEAD_WIDTH)
     groups = q_cols // HEAD_WIDTH
     live = jnp.clip(cache_lengths - position * positions, 0, positions).astype(jnp.int32)
-    first_out = local_attention(own_x, kv_cache, jnp.concatenate([live, ci[None]]), seq_count, nc)
-    m_rows, l_rows, part_acc = local_attention(
-        other_x, kv_cache, jnp.concatenate([live, (1 - ci)[None]]), seq_count, nc, prev=first_out
-    )
-    first = ci == 0
     per_slot = seq_count // local_reqs
     tok = tree_len // per_slot
-
-    def dest_major(rows_arr):
-        r = rows_arr[:, :, 0, :].reshape(local_reqs, kv_heads, groups, per_slot, tok)
-        return r.transpose(0, 3, 1, 2, 4).reshape(seq_count, kv_heads, groups * tok)
-
-    part_m = dest_major(m_rows)
-    part_l = dest_major(l_rows)
-    sub = part_acc.shape[2]
-    rows_acc = kv_heads * sub
+    kh = kv_heads // nc
+    rows_acc = kh * groups * tok
     stat_rows = rows_acc // HEAD_WIDTH
     pad = (-(rows_acc + 2 * stat_rows)) % 8
+
+    def dest_major(rows_arr):
+        r = rows_arr[:, :, 0, :].reshape(local_reqs, kh, groups, per_slot, tok)
+        return r.transpose(0, 3, 1, 2, 4).reshape(seq_count, rows_acc)
 
     def pack(acc, m, l):
         lead = acc.shape[:-2]
@@ -183,25 +174,44 @@
         l = pk[..., rows_acc + stat_rows:rows_acc + 2 * stat_rows, :].reshape(lead + (rows_acc,))
         return m, l, acc
 
-    pk = pack(
-        part_acc.reshape(nx, nc, rows_acc, HEAD_WIDTH),
-        part_m.reshape(nx, nc, rows_acc),
-        part_l.reshape(nx, nc, rows_acc),
-    )
-    pk = lax.all_to_all(pk, "c", 1, 1, tiled=True)
-    m1, l1, a1 = merge_pair(*unpack(pk), axis=1)
-    pk = lax.all_to_all(pack(a1, m1, l1), "x", 0, 0, tiled=True)
-    rm, rl, acc = unpack(pk)
+    def packed(out):
+        m_rows, l_rows, acc = out
+        pk = pack(acc.reshape(seq_count, rows_acc, HEAD_WIDTH), dest_major(m_rows), dest_major(l_rows))
+        return pk.reshape((nx, nc) + pk.shape[1:])
+
+    def split_c(pk):
+        mine = lax.dynamic_index_in_dim(pk, ci, 1, keepdims=False)
+        theirs = lax.dynamic_index_in_dim(pk, 1 - ci, 1, keepdims=False)
+        return mine, theirs
+
+    swap = [(0, 1), (1, 0)]
+    pk_a = packed(local_attention(own_x, kv_cache, jnp.concatenate([live, ci[None]]), seq_count, nc))
+    mine_a, theirs_a = split_c(pk_a)
+    theirs_a, mine_a, other_b = lax.optimization_barrier((theirs_a, mine_a, other_x))
+    got_a = lax.ppermute(theirs_a, "c", perm=swap)
+    pref_b = jnp.concatenate([live, (1 - ci)[None]])
+    out_b = local_attention(other_b, kv_cache, pref_b, seq_count, nc)
+    pk_b = packed(out_b)
+    mine_b, theirs_b = split_c(pk_b)
+    got_b = lax.ppermute(theirs_b, "c", perm=swap)
+
+    m_c, l_c, a_c = merge_pair(*(jnp.stack(t, 1) for t in zip(unpack(mine_a), unpack(got_b))), axis=1)
+    m_o, l_o, a_o = merge_pair(*(jnp.stack(t, 1) for t in zip(unpack(mine_b), unpack(got_a))), axis=1)
+    merged = jnp.concatenate([pack(a_c, m_c, l_c), pack(a_o, m_o, l_o)], axis=1)
+    pk = lax.all_to_all(merged, "x", 0, 0, tiled=True)
+    half = pk.shape[1] // 2
+    rm_c, rl_c, acc_c = unpack(pk[:, :half])
+    rm_o, rl_o, acc_o = unpack(pk[:, half:])
+    rm = jnp.concatenate([rm_c, rm_o], axis=1)
+    rl = jnp.concatenate([rl_c, rl_o], axis=1)
+    acc = jnp.concatenate([acc_c, acc_o], axis=1)
+    sub = groups * tok
 
     my_slot = position // per_slot
     my_tok0 = (position % per_slot) * tok
     mine_own = lax.dynamic_index_in_dim(own_x, my_slot, 0, keepdims=False)
     mine_other = lax.dynamic_index_in_dim(other_x, my_slot, 0, keepdims=False)
-    mine_all = jnp.where(
-        first,
-        jnp.concatenate([mine_own, mine_other], axis=0),
-        jnp.concatenate([mine_other, mine_own], axis=0),
-    )
+    mine_all = jnp.concatenate([mine_own, mine_other], axis=0)
     q_mine = lax.dynamic_slice_in_dim(mine_all[..., :q_cols], my_tok0, tok, 1).reshape(
         kv_heads, tok, groups, HEAD_WIDTH
     )
@@ -229,10 +239,10 @@
         jnp.concatenate([acc, od], axis=0),
         axis=0,
     )
-    res = num / den[..., None]
+    res = (num / den[..., None]).reshape(nc, kh, groups, tok, HEAD_WIDTH)
+    res = jnp.where(ci == 0, res, res[::-1])
     context = (
-        res.reshape(nc, kv_heads // nc, groups, tok, HEAD_WIDTH)
-        .transpose(3, 1, 0, 2, 4)
+        res.transpose(3, 1, 0, 2, 4)
         .reshape(tok, kv_heads * groups * HEAD_WIDTH)
         .astype(jnp.bfloat16)
     )
@@ -257,7 +267,7 @@
         P(R, None),
     )
     return jax.shard_map(
-        body,
+        body_inner,
         mesh=fine,
         in_specs=placed,
         out_specs=(P(R + S, None), P(R, None, S)),

time: 131 us -> 157 us (1.20)
  local copies, waits for them, and re-layouts: 12.3 us -> 39.4 us
  blocking collectives: 33.3 us -> 26.9 us
  other arithmetic: 7.38 us -> 12.8 us
    another operation x6 -> x21, local copies, waits for them, and re-layouts: 4.37 us -> 14.1 us  [the longest x8 10.3 us: dest_major(): r = rows_arr[:, :, 0, :].reshape(local_reqs, kh, groups, per_slot, tok)]
    concatenate x1 -> x3, local copies, waits for them, and re-layouts: 0.11 us -> 7.86 us  [the longest x1 7.75 us: body_inner(): merged = jnp.concatenate([pack(a_c, m_c, l_c), pack(a_o, m_o, l_o)], axis=1)]
    concatenate x1 -> x6, local copies, waits for them, and re-layouts: 0.08 us -> 7.18 us  [pack(): return jnp.concatenate(parts, axis=-2)]
    all_to_all x1 -> x0, blocking collectives: 5.95 us -> none  [body(): pk = lax.all_to_all(pk, 'c', 1, 1, tiled=True)]
    reduce_sum x2 -> x3, other arithmetic: 1.75 us -> 3.43 us  [merge_pair(): jnp.sum(f[..., None] * acc, axis=axis)]
    slice x1 -> x2, other arithmetic: 0.01 us -> 1.67 us  [unpack(): m = pk[..., rows_acc:rows_acc + stat_rows, :].reshape(lead + (rows_acc,))]
    squeeze x2 -> x4, local copies, waits for them, and re-layouts: 2.93 us -> 3.51 us  [the longest x2 2.64 us: split_c(): mine = lax.dynamic_index_in_dim(pk, ci, 1, keepdims=False)]
    ppermute x1 -> x3, starting transfers between devices: 7.33 us -> 7.6 us  [the longest x1 7.01 us: body_inner(): other_x = lax.ppermute(own_x, 'c', perm=[(0, 1), (1, 0)])]
  transfers between devices with their start and end apart: 3 -> 5, of which waited for: 2 -> 3; matrix products, arithmetic and copies ran while one was open for 5% -> 13% of each run, Pallas kernels for 12% -> 10%
where the time goes in v8:
time: 157 us; the launch traced here: 156 us
  local copies, waits for them, and re-layouts  39.4 us (25%)
  Pallas kernels  30.7 us (20%)
  waiting for transfers between devices  28 us (18%)
  blocking collectives  26.9 us (17%)
  starting transfers between devices  15.3 us (10%)
  other arithmetic  12.8 us (8%)
    pallas_call x2, Pallas kernels, local_attention(): pl.pallas_call(kern, grid_spec=grid_spec, out_shape=[jax.ShapeDtypeStruct...  30.7 us
    all_to_all x1, waiting for transfers between devices, body_inner(): pk = lax.all_to_all(merged, 'x', 0, 0, tiled=True)  16.2 us
    all_gather x1, blocking collectives, body_inner(): held = lax.all_gather(both, 'z', axis=0, tiled=True)  15 us
    all_gather x1, blocking collectives, body_inner(): own_x = lax.all_gather(own, 'x', axis=1, tiled=False)  12 us
    all_to_all x1, waiting for transfers between devices, body_inner(): recv = lax.all_to_all(send, 'y', 0, 0, tiled=True)  11.6 us
    another operation x8, local copies, waits for them, and re-layouts, dest_major(): r = rows_arr[:, :, 0, :].reshape(local_reqs, kh, groups, per_slot, tok)  10.3 us
    concatenate x1, local copies, waits for them, and re-layouts, body_inner(): merged = jnp.concatenate([pack(a_c, m_c, l_c), pack(a_o, m_o, l_o)], axis=1)  7.75 us
    concatenate x6, local copies, waits for them, and re-layouts, pack(): return jnp.concatenate(parts, axis=-2)  7.18 us
  transfers between devices with their start and end apart: 5, of which 3 were waited for; matrix products, arithmetic and copies ran while one was open for 13% of the time, Pallas kernels for 10%

profile of v8, /device:TPU:1, one launch (start us, length us, event | category | flops | bytes accessed | tf_op | source)
XLA Modules:
  0.0 155.7 jit_solution(15829346007045136774)
XLA Ops:
  0.7 1.3 gather_fusion
  2.1 1.0 pad_maximum_fusion
  3.1 15.0 %all_gather.7 = bf16[8,48,1280]{2,1,0:T(8,128)(2,1)S(1)} all-gather(bf16[2,48,1280]{2,1,0:T(8,128)(2,1)S(1)} %pad_maximum_fusion), channel_id=1, replica_groups=mesh['z'=4,'y'=4,'x'=4,'c'=2] {'z'}, dimensions={0}, use_global_device_ids=true | all-gather | bytes 1228800 | tf_op jit(solution)/shard_map/all_gather | solution.py:132
  18.7 1.1 broadcast_select_fusion
  19.8 4.2 %all-to-all-start = ((bf16[4,2,48,1280]{3,2,1,0:T(8,128)(2,1)}), bf16[4,2,48,1280]{3,2,1,0:T(8,128)(2,1)S(1)}, u32[]{:S(2)}, u32[]{:S(2)}) async-start(bf16[4,2,48,1280]{3,2,1,0:T(8,128)(2,1)} %broadcast_select_fusion), calls=%async_computation | async-start | bytes 1966080 | tf_op jit(solution)/shard_map/all_to_all | solution.py:138
  24.1 11.6 %all-to-all-done = bf16[4,2,48,1280]{3,2,1,0:T(8,128)(2,1)S(1)} async-done(((bf16[4,2,48,1280]{3,2,1,0:T(8,128)(2,1)}), bf16[4,2,48,1280]{3,2,1,0:T(8,128)(2,1)S(1)}, u32[]{:S(2)}, u32[]{:S(2)}) %all-to-all-start) | async-done | bytes 983072 | tf_op jit(solution)/shard_map/all_to_all | solution.py:138
  36.4 12.0 %all_gather.8.q_ref = bf16[2,4,48,1280]{3,2,1,0:T(8,128)(2,1)S(1)} all-gather(bf16[2,1,48,1280]{3,2,1,0:T(8,128)(2,1)S(1)} %bitcast_select_fusion), channel_id=1, replica_groups=mesh['z'=4,'y'=4,'x'=4,'c'=2] {'x'}, dimensions={1}, use_global_device_ids=true | all-gather | bytes 1228800 | tf_op jit(solution)/shard_map/all_gather | solution.py:145
  48.3 7.0 %collective-permute-start = (bf16[2,4,48,1280]{3,2,1,0:T(8,128)(2,1)S(1)}, bf16[2,4,48,1280]{3,2,1,0:T(8,128)(2,1)S(1)}, u32[]{:S(2)}, u32[]{:S(2)}) collective-permute-start(bf16[2,4,48,1280]{3,2,1,0:T(8,128)(2,1)S(1)} %all_gather.8.q_ref), channel_id=1, source_target_pairs={{0,1},{1,0},{2,3},{3,2},{4,5},{5,4},{6,7},{7,6},{8,9},{9,8},{10,11... | collective-permute-start | bytes 2949128 | tf_op jit(solution)/shard_map/ppermute | solution.py:146
  56.9 15.4 %shard_map.86 = (f32[2,4,8,384]{3,2,1,0:T(8,128)S(1)}, f32[2,4,8,384]{3,2,1,0:T(8,128)S(1)}, f32[8,4,96,128]{3,2,1,0:T(8,128)S(1)}) custom-call(s32[3]{0:T(128)S(1)} %get-tuple-element.50.live_ref, bf16[2,4,48,1280]{3,2,1,0:T(8,128)(2,1)S(1)} %all_gather.8.q_ref, bf16[2,2048,2048]{2,1,0:T(8,128)(2,1)} %kv_ref.3), custom_call_target="tpu_custom_call" | custom-call | tf_op jit(solution)/shard_map/pallas_call | solution.py:89
  72.9 1.6 reshape_squeeze.13
  74.5 1.6 copy.92
  76.0 1.6 %concatenate.73 = f32[4,2,3,128]{3,2,1,0:T(4,128)} reshape(f32[2,4,4,8,12]{4,3,2,1,0:T(8,128)} %bitcast.128) | data formatting | bytes 24576 | tf_op jit(solution)/shard_map/concatenate | solution.py:168
  78.5 1.6 copy.93
  80.1 1.6 %concatenate.72 = f32[4,2,3,128]{3,2,1,0:T(4,128)} reshape(f32[2,4,4,8,12]{4,3,2,1,0:T(8,128)} %bitcast.129) | data formatting | bytes 24576 | tf_op jit(solution)/shard_map/concatenate | solution.py:168
  82.6 1.3 dynamic-slice_bitcast_fusion.2
  83.9 15.4 %shard_map.87 = (f32[2,4,8,384]{3,2,1,0:T(8,128)S(1)}, f32[2,4,8,384]{3,2,1,0:T(8,128)S(1)}, f32[8,4,96,128]{3,2,1,0:T(8,128)S(1)}) custom-call(s32[3]{0:T(128)S(1)} %get-tuple-element.51.live_ref, bf16[2,4,48,1280]{3,2,1,0:T(8,128)(2,1)S(1)} %collective-permute-done.q_ref, bf16[2,2048,2048]{2,1,0:T(8,128)(2,1)} %kv_ref.3), custom_call_target="tpu_custom_call" | custom-call | tf_op jit(solution)/shard_map/pallas_call | solution.py:89
  100.8 1.6 %copy.90 = f32[2,4,8,4,12]{4,2,1,3,0:T(8,128)} copy(f32[2,4,8,4,12]{4,3,2,1,0:T(4,128)} %reshape_squeeze.15) | data formatting | bytes 24576 | tf_op jit(solution)/shard_map/reshape;squeeze | solution.py:160
  102.4 1.6 %concatenate.79 = f32[4,2,3,128]{3,2,1,0:T(4,128)} reshape(f32[2,4,4,8,12]{4,3,2,1,0:T(8,128)} %bitcast.130) | data formatting | bytes 24576 | tf_op jit(solution)/shard_map/concatenate | solution.py:168
  104.0 0.9 slice_reduce_fusion.1
  105.8 1.6 %copy.91 = f32[2,4,8,4,12]{4,2,1,3,0:T(8,128)} copy(f32[2,4,8,4,12]{4,3,2,1,0:T(4,128)} %reshape_squeeze.14) | data formatting | bytes 24576 | tf_op jit(solution)/shard_map/reshape;squeeze | solution.py:160
  107.4 1.6 %concatenate.78 = f32[4,2,3,128]{3,2,1,0:T(4,128)} reshape(f32[2,4,4,8,12]{4,3,2,1,0:T(8,128)} %bitcast.131) | data formatting | bytes 24576 | tf_op jit(solution)/shard_map/concatenate | solution.py:168
  109.9 1.3 dynamic-slice_bitcast_fusion
  112.6 1.2 slice_bitcast_fusion.3
  116.0 1.2 slice_bitcast_fusion.2
  117.2 1.4 fusion.1
  118.6 1.2 slice_bitcast_fusion
  119.8 1.4 fusion.2
  121.1 7.7 %concatenate.81 = f32[4,784,128]{2,1,0:T(8,128)} concatenate(f32[4,384,128]{2,1,0:T(8,128)} %fusion.1, f32[4,3,128]{2,1,0:T(4,128)S(1)} %get-tuple-element.42, f32[4,3,128]{2,1,0:T(4,128)S(1)} %copy.50, f32[4,2,128]{2,1,0:T(2,128)S(1)} %broadcast.347, f32[4,384,128]{2,1,0:T(8,128)} %fusion.2, f32[4,3,128]{2,1,0:T(4,128)S(1)} %get-tuple-element.37, f32[4,3,128]{2,1,0:T(4,128)S(1)} %copy.51, ...), dimensions={1} | concatenate | bytes 3211264 | tf_op jit(solution)/shard_map/concatenate | solution.py:200
  128.9 3.6 %all-to-all-start.1 = ((f32[4,784,128]{2,1,0:T(8,128)}), f32[4,784,128]{2,1,0:T(8,128)S(1)}, u32[]{:S(2)}, u32[]{:S(2)}) async-start(f32[4,784,128]{2,1,0:T(8,128)} %concatenate.81), calls=%async_computation.1 | async-start | bytes 3211264 | tf_op jit(solution)/shard_map/all_to_all | solution.py:201
  133.3 1.0 fusion.11
  134.5 0.9 pad_maximum_fusion.1
  137.2 16.2 %all-to-all-done.1 = f32[4,784,128]{2,1,0:T(8,128)S(1)} async-done(((f32[4,784,128]{2,1,0:T(8,128)}), f32[4,784,128]{2,1,0:T(8,128)S(1)}, u32[]{:S(2)}, u32[]{:S(2)}) %all-to-all-start.1) | async-done | bytes 1605664 | tf_op jit(solution)/shard_map/all_to_all | solution.py:201
  (88 shorter events, 17.2 us)
Async XLA Ops:
  18.7 5.3 %copy-start.1 = (s32[32]{0:T(128)S(1)}, s32[32]{0:T(128)}, u32[]{:S(2)}) copy-start(s32[32]{0:T(128)} %param.12) | copy-start | bytes 388
  19.8 15.9 %all-to-all-start = ((bf16[4,2,48,1280]{3,2,1,0:T(8,128)(2,1)}), bf16[4,2,48,1280]{3,2,1,0:T(8,128)(2,1)S(1)}, u32[]{:S(2)}, u32[]{:S(2)}) async-start(bf16[4,2,48,1280]{3,2,1,0:T(8,128)(2,1)} %broadcast_select_fusion), calls=%async_computation | async-start | bytes 1966080 | tf_op jit(solution)/shard_map/all_to_all | solution.py:138
  24.0 31.4 %copy-start.5 = (s32[2]{0:T(128)S(1)}, s32[2]{0:T(128)}, u32[]{:S(2)}) copy-start(s32[2]{0:T(128)} %param.10) | copy-start | bytes 28
  24.0 32.1 %copy-start.3 = (bf16[2,48,256]{2,1,0:T(8,128)(2,1)S(1)}, bf16[2,48,256]{2,1,0:T(8,128)(2,1)}, u32[]{:S(2)}) copy-start(bf16[2,48,256]{2,1,0:T(8,128)(2,1)} %param.8) | copy-start | bytes 147460
  24.0 32.1 %copy-start.4 = (s32[2,8]{1,0:T(2,128)S(1)}, s32[2,8]{1,0:T(2,128)}, u32[]{:S(2)}) copy-start(s32[2,8]{1,0:T(2,128)} %param.13) | copy-start | bytes 196
  48.3 35.6 %collective-permute-start = (bf16[2,4,48,1280]{3,2,1,0:T(8,128)(2,1)S(1)}, bf16[2,4,48,1280]{3,2,1,0:T(8,128)(2,1)S(1)}, u32[]{:S(2)}, u32[]{:S(2)}) collective-permute-start(bf16[2,4,48,1280]{3,2,1,0:T(8,128)(2,1)S(1)} %all_gather.8.q_ref), channel_id=1, source_target_pairs={{0,1},{1,0},{2,3},{3,2},{4,5},{5,4},{6,7},{7,6},{8,9},{9,8},{10,11... | collective-permute-start | bytes 2949128 | tf_op jit(solution)/shard_map/ppermute | solution.py:146
  99.3 0.6 copy-start
  111.2 2.7 %collective-permute-start.1 = (f32[4,392,128]{2,1,0:T(8,128)}, f32[4,392,128]{2,1,0:T(8,128)}, u32[]{:S(2)}, u32[]{:S(2)}) collective-permute-start(f32[4,392,128]{2,1,0:T(8,128)} %get-tuple-element.33), channel_id=1, source_target_pairs={{0,1},{1,0},{2,3},{3,2},{4,5},{5,4},{6,7},{7,6},{8,9},{9,8},{10,11... | collective-permute-start | bytes 2408456 | tf_op jit(solution)/shard_map/ppermute | solution.py:196
  112.0 1.8 %copy-start.2 = (f32[4,392,128]{2,1,0:T(8,128)S(1)}, f32[4,392,128]{2,1,0:T(8,128)}, u32[]{:S(2)}) copy-start(f32[4,392,128]{2,1,0:T(8,128)} %get-tuple-element.32) | copy-start | bytes 2408452
  112.0 3.0 %collective-permute-start.2 = (f32[4,392,128]{2,1,0:T(8,128)}, f32[4,392,128]{2,1,0:T(8,128)}, u32[]{:S(2)}, u32[]{:S(2)}) collective-permute-start(f32[4,392,128]{2,1,0:T(8,128)} %get-tuple-element.19), channel_id=1, source_target_pairs={{0,1},{1,0},{2,3},{3,2},{4,5},{5,4},{6,7},{7,6},{8,9},{9,8},{10,11... | collective-permute-start | bytes 2408456 | tf_op jit(solution)/shard_map/ppermute | solution.py:191
  128.9 24.5 %all-to-all-start.1 = ((f32[4,784,128]{2,1,0:T(8,128)}), f32[4,784,128]{2,1,0:T(8,128)S(1)}, u32[]{:S(2)}, u32[]{:S(2)}) async-start(f32[4,784,128]{2,1,0:T(8,128)} %concatenate.81), calls=%async_computation.1 | async-start | bytes 3211264 | tf_op jit(solution)/shard_map/all_to_all | solution.py:201

commit v9 on v6

--- a/solution.py
+++ b/solution.py
@@ -190,7 +190,12 @@
     )
     pk = lax.all_to_all(pk, "c", 1, 1, tiled=True)
     m1, l1, a1 = merge_pair(*unpack(pk), axis=1)
-    pk = lax.all_to_all(pack(a1, m1, l1), "x", 0, 0, tiled=True)
+    send = pack(a1, m1, l1)
+    pieces = [lax.dynamic_index_in_dim(send, xi, 0, keepdims=False)]
+    for shift in range(1, nx):
+        piece = lax.dynamic_index_in_dim(send, (xi + shift) % nx, 0, keepdims=False)
+        pieces.append(lax.ppermute(piece, "x", perm=[(i, (i + shift) % nx) for i in range(nx)]))
+    pk = jnp.stack(pieces, axis=0)
     rm, rl, acc = unpack(pk)
 
     my_slot = position // per_slot

time: 131 us -> 139 us (1.061)
  local copies, waits for them, and re-layouts: 12.3 us -> 21 us
  starting transfers between devices: 15.1 us -> 13.7 us
  waiting for transfers between devices: 29 us -> 30.4 us
    ppermute x0 -> x3, waiting for transfers between devices: none -> 18.8 us  [body(): lax.ppermute(piece, 'x', perm=[(i, (i + shift) % nx) for i in range(nx)])]
    all_to_all x1 -> x0, waiting for transfers between devices: 17.3 us -> none  [body(): pk = lax.all_to_all(pack(a1, m1, l1), 'x', 0, 0, tiled=True)]
    all_to_all x1 -> x0, starting transfers between devices: 3.56 us -> none  [body(): pk = lax.all_to_all(pack(a1, m1, l1), 'x', 0, 0, tiled=True)]
    ppermute x0 -> x3, starting transfers between devices: none -> 2.04 us  [body(): lax.ppermute(piece, 'x', perm=[(i, (i + shift) % nx) for i in range(nx)])]
    slice x1, local copies, waits for them, and re-layouts: 0.28 us -> 2.12 us  [body(): d_slot[:, :, 1]]
    reshape x1, local copies, waits for them, and re-layouts: 0.15 us -> 1.77 us  [body(): lax.dynamic_slice_in_dim(mine_all[..., :q_cols], my_tok0, tok, 1)]
    reshape x1, local copies, waits for them, and re-layouts: 0.05 us -> 1.65 us  [body(): d_slot = mine_all[..., q_cols:].reshape(kv_heads, tree_len, 2, HEAD_WIDTH)]
    another operation x4, local copies, waits for them, and re-layouts: 2.13 us -> 3.61 us  [dest_major(): rows_arr[:, :, 0, :].reshape(local_reqs, kv_heads, groups, per_slot, tok)]
  transfers between devices with their start and end apart: 3 -> 5, of which waited for: 2 -> 4; matrix products, arithmetic and copies ran while one was open for 5% -> 3% of each run, Pallas kernels for 12% -> 11%
where the time goes in v9:
time: 139 us; the launch traced here: 138 us
  blocking collectives  33.3 us (24%)
  Pallas kernels  30.8 us (22%)
  waiting for transfers between devices  30.4 us (22%)
  local copies, waits for them, and re-layouts  21 us (15%)
  starting transfers between devices  13.7 us (10%)
  other arithmetic  6.31 us (5%)
  matrix products  1.49 us (1%)
    pallas_call x2, Pallas kernels, local_attention(): pl.pallas_call(kern, grid_spec=grid_spec, out_shape=[jax.ShapeDtypeStruct...  30.8 us
    ppermute x3, waiting for transfers between devices, body(): lax.ppermute(piece, 'x', perm=[(i, (i + shift) % nx) for i in range(nx)])  18.8 us
    all_gather x1, blocking collectives, body(): held = lax.all_gather(both, 'z', axis=0, tiled=True)  15 us
    all_gather x1, blocking collectives, body(): own_x = lax.all_gather(own, 'x', axis=1, tiled=False)  12.4 us
    all_to_all x1, waiting for transfers between devices, body(): recv = lax.all_to_all(send, 'y', 0, 0, tiled=True)  11.6 us
    ppermute x1, starting transfers between devices, body(): other_x = lax.ppermute(own_x, 'c', perm=[(0, 1), (1, 0)])  7.33 us
    all_to_all x1, blocking collectives, body(): pk = lax.all_to_all(pk, 'c', 1, 1, tiled=True)  5.95 us
    all_to_all x1, starting transfers between devices, body(): recv = lax.all_to_all(send, 'y', 0, 0, tiled=True)  4.31 us
  transfers between devices with their start and end apart: 5, of which 4 were waited for; matrix products, arithmetic and copies ran while one was open for 3% of the time, Pallas kernels for 11%

profile of v9, /device:TPU:1, one launch (start us, length us, event | category | flops | bytes accessed | tf_op | source)
XLA Modules:
  0.0 138.1 jit_solution(18198665466203172906)
XLA Ops:
  0.7 1.3 gather_fusion
  2.1 1.0 pad_maximum_fusion.1
  3.1 15.0 %all_gather.7 = bf16[8,48,1280]{2,1,0:T(8,128)(2,1)S(1)} all-gather(bf16[2,48,1280]{2,1,0:T(8,128)(2,1)S(1)} %pad_maximum_fusion.1), channel_id=1, replica_groups=mesh['z'=4,'y'=4,'x'=4,'c'=2] {'z'}, dimensions={0}, use_global_device_ids=true | all-gather | bytes 1228800 | tf_op jit(solution)/shard_map/all_gather | solution.py:133
  18.7 1.1 broadcast_select_fusion
  19.8 4.3 %all-to-all-start = ((bf16[4,2,48,1280]{3,2,1,0:T(8,128)(2,1)}), bf16[4,2,48,1280]{3,2,1,0:T(8,128)(2,1)S(1)}, u32[]{:S(2)}, u32[]{:S(2)}) async-start(bf16[4,2,48,1280]{3,2,1,0:T(8,128)(2,1)} %broadcast_select_fusion), calls=%async_computation | async-start | bytes 1966080 | tf_op jit(solution)/shard_map/all_to_all | solution.py:139
  24.2 11.6 %all-to-all-done = bf16[4,2,48,1280]{3,2,1,0:T(8,128)(2,1)S(1)} async-done(((bf16[4,2,48,1280]{3,2,1,0:T(8,128)(2,1)}), bf16[4,2,48,1280]{3,2,1,0:T(8,128)(2,1)S(1)}, u32[]{:S(2)}, u32[]{:S(2)}) %all-to-all-start) | async-done | bytes 983072 | tf_op jit(solution)/shard_map/all_to_all | solution.py:139
  36.5 12.4 %all_gather.8.q_ref = bf16[2,4,48,1280]{3,2,1,0:T(8,128)(2,1)} all-gather(bf16[2,1,48,1280]{3,2,1,0:T(8,128)(2,1)S(1)} %bitcast_select_fusion), channel_id=1, replica_groups=mesh['z'=4,'y'=4,'x'=4,'c'=2] {'x'}, dimensions={1}, use_global_device_ids=true | all-gather | bytes 1228800 | tf_op jit(solution)/shard_map/all_gather | solution.py:146
  48.9 7.3 %collective-permute-start = (bf16[2,4,48,1280]{3,2,1,0:T(8,128)(2,1)}, bf16[2,4,48,1280]{3,2,1,0:T(8,128)(2,1)}, u32[]{:S(2)}, u32[]{:S(2)}) collective-permute-start(bf16[2,4,48,1280]{3,2,1,0:T(8,128)(2,1)} %all_gather.8.q_ref), channel_id=1, source_target_pairs={{0,1},{1,0},{2,3},{3,2},{4,5},{5,4},{6,7},{7,6},{8,9},{9,8},{10,11... | collective-permute-start | bytes 2949128 | tf_op jit(solution)/shard_map/ppermute | solution.py:147
  56.4 0.7 fusion.17
  57.1 0.8 convolution_convert_fusion
  57.9 15.4 %shard_map.86 = (f32[2,8,8,384]{3,2,1,0:T(8,128)S(1)}, f32[2,8,8,384]{3,2,1,0:T(8,128)S(1)}, f32[8,8,96,128]{3,2,1,0:T(8,128)S(1)}) custom-call(s32[3]{0:T(128)S(1)} %get-tuple-element.29.live_ref, bf16[2,4,48,1280]{3,2,1,0:T(8,128)(2,1)} %all_gather.8.q_ref, bf16[2,2048,2048]{2,1,0:T(8,128)(2,1)} %kv_ref.3), custom_call_target="tpu_custom_call" | custom-call | tf_op jit(solution)/shard_map/pallas_call | solution.py:89
  73.3 1.1 dynamic-slice_bitcast_fusion.1
  74.4 1.1 dynamic-slice_bitcast_fusion
  76.4 0.8 constant_dynamic-slice_fusion
  77.2 1.8 %reshape.313 = bf16[8,12,8,128]{3,2,1,0:T(8,128)(2,1)} reshape(bf16[8,12,1024]{2,1,0:T(8,128)(2,1)} %constant_dynamic-slice_fusion) | data formatting | bytes 393216 | tf_op jit(solution)/shard_map/reshape | solution.py:210
  79.0 1.7 %reshape.279 = bf16[8,48,2,128]{3,2,1,0:T(2,128)(2,1)} reshape(bf16[8,48,256]{2,1,0:T(8,128)(2,1)} %slice.57) | data formatting | bytes 393216 | tf_op jit(solution)/shard_map/reshape | solution.py:213
  80.7 2.1 %fusion.33 = (bf16[8,48,1,128]{3,2,1,0:T(2,128)(2,1)}, bf16[8,48,1,128]{3,2,1,0:T(2,128)(2,1)}) fusion(bf16[8,48,2,128]{3,2,1,0:T(2,128)(2,1)} %reshape.279), kind=kLoop, calls=%fused_computation.114 | loop fusion | bytes 393216 | tf_op jit(solution)/shard_map/slice | solution.py:225
  82.8 15.4 %shard_map.87 = (f32[2,8,8,384]{3,2,1,0:T(8,128)S(1)}, f32[2,8,8,384]{3,2,1,0:T(8,128)S(1)}, f32[8,8,96,128]{3,2,1,0:T(8,128)S(1)}) custom-call(s32[3]{0:T(128)S(1)} %get-tuple-element.30.live_ref, bf16[2,4,48,1280]{3,2,1,0:T(8,128)(2,1)} %collective-permute-done.q_ref, ...), custom_call_target="tpu_custom_call", output_to_operand_aliasing={{0}: (3, {}), {1}: (4, {}), {2}: (5, {})} | custom-call | tf_op jit(solution)/shard_map/pallas_call | solution.py:89
  98.9 1.1 reshape_squeeze.7
  100.0 0.7 copy.74
  100.7 1.1 reshape_reshape_reshape.7
  101.8 1.1 reshape_squeeze.6
  102.9 0.7 copy.75
  103.6 1.1 reshape_reshape_reshape.6
  105.1 6.0 %all_to_all.10 = f32[4,2,784,128]{3,2,0,1:T(8,128)S(1)} all-to-all(f32[4,2,784,128]{3,2,0,1:T(8,128)S(1)} %maximum_maximum_fusion), channel_id=1, replica_groups=mesh['z'=4,'y'=4,'x'=4,'c'=2] {'c'}, dimensions={1} | all-to-all | bytes 6422528 | tf_op jit(solution)/shard_map/all_to_all | solution.py:191
  111.1 1.1 fusion
  112.4 1.0 constant_dynamic-slice_fusion.1
  113.4 0.8 collective-permute-start.3
  116.9 7.2 %collective-permute-done.3 = f32[784,128]{1,0:T(8,128)S(1)} collective-permute-done((f32[784,128]{1,0:T(8,128)}, f32[784,128]{1,0:T(8,128)S(1)}, u32[]{:S(2)}, u32[]{:S(2)}) %collective-permute-start.3) | collective-permute-done | bytes 401440 | tf_op jit(solution)/shard_map/ppermute | solution.py:197
  124.1 2.1 %collective-permute-done.2 = f32[784,128]{1,0:T(8,128)S(1)} collective-permute-done((f32[784,128]{1,0:T(8,128)}, f32[784,128]{1,0:T(8,128)S(1)}, u32[]{:S(2)}, u32[]{:S(2)}) %collective-permute-start.2) | collective-permute-done | bytes 401440 | tf_op jit(solution)/shard_map/ppermute | solution.py:197
  126.2 9.6 %collective-permute-done.1 = f32[784,128]{1,0:T(8,128)S(1)} collective-permute-done((f32[784,128]{1,0:T(8,128)S(1)}, f32[784,128]{1,0:T(8,128)S(1)}, u32[]{:S(2)}, u32[]{:S(2)}) %collective-permute-start.1) | collective-permute-done | bytes 401440 | tf_op jit(solution)/shard_map/ppermute | solution.py:197
  137.2 0.9 copy.49
  (64 shorter events, 7.9 us)
Async XLA Ops:
  18.7 5.4 %copy-start = (s32[32]{0:T(128)S(1)}, s32[32]{0:T(128)}, u32[]{:S(2)}) copy-start(s32[32]{0:T(128)} %param.12) | copy-start | bytes 388
  19.8 36.5 %copy-start.6 = (s32[2]{0:T(128)S(1)}, s32[2]{0:T(128)}, u32[]{:S(2)}) copy-start(s32[2]{0:T(128)} %param.10) | copy-start | bytes 28
  19.8 37.3 %copy-start.4 = (bf16[2,48,256]{2,1,0:T(8,128)(2,1)S(1)}, bf16[2,48,256]{2,1,0:T(8,128)(2,1)}, u32[]{:S(2)}) copy-start(bf16[2,48,256]{2,1,0:T(8,128)(2,1)} %param.8) | copy-start | bytes 147460
  19.8 37.3 %copy-start.5 = (s32[2,8]{1,0:T(2,128)S(1)}, s32[2,8]{1,0:T(2,128)}, u32[]{:S(2)}) copy-start(s32[2,8]{1,0:T(2,128)} %param.13) | copy-start | bytes 196
  19.8 16.0 %all-to-all-start = ((bf16[4,2,48,1280]{3,2,1,0:T(8,128)(2,1)}), bf16[4,2,48,1280]{3,2,1,0:T(8,128)(2,1)S(1)}, u32[]{:S(2)}, u32[]{:S(2)}) async-start(bf16[4,2,48,1280]{3,2,1,0:T(8,128)(2,1)} %broadcast_select_fusion), calls=%async_computation | async-start | bytes 1966080 | tf_op jit(solution)/shard_map/all_to_all | solution.py:139
  48.9 25.5 %collective-permute-start = (bf16[2,4,48,1280]{3,2,1,0:T(8,128)(2,1)}, bf16[2,4,48,1280]{3,2,1,0:T(8,128)(2,1)}, u32[]{:S(2)}, u32[]{:S(2)}) collective-permute-start(bf16[2,4,48,1280]{3,2,1,0:T(8,128)(2,1)} %all_gather.8.q_ref), channel_id=1, source_target_pairs={{0,1},{1,0},{2,3},{3,2},{4,5},{5,4},{6,7},{7,6},{8,9},{9,8},{10,11... | collective-permute-start | bytes 2949128 | tf_op jit(solution)/shard_map/ppermute | solution.py:147
  112.4 3.1 %copy-start.2 = (bf16[8,12,8,128]{3,2,1,0:T(8,128)(2,1)S(1)}, bf16[8,12,8,128]{3,2,1,0:T(8,128)(2,1)}, u32[]{:S(2)}) copy-start(bf16[8,12,8,128]{3,2,1,0:T(8,128)(2,1)} %reshape.313) | copy-start | bytes 589828
  112.4 3.1 %copy-start.3 = (bf16[8,48,1,128]{3,2,1,0:T(2,128)(2,1)S(1)}, bf16[8,48,1,128]{3,2,1,0:T(2,128)(2,1)}, u32[]{:S(2)}) copy-start(bf16[8,48,1,128]{3,2,1,0:T(2,128)(2,1)} %get-tuple-element.26) | copy-start | bytes 294916
  112.4 3.6 %copy-start.1 = (bf16[8,48,1,128]{3,2,1,0:T(2,128)(2,1)S(1)}, bf16[8,48,1,128]{3,2,1,0:T(2,128)(2,1)}, u32[]{:S(2)}) copy-start(bf16[8,48,1,128]{3,2,1,0:T(2,128)(2,1)} %get-tuple-element.25) | copy-start | bytes 294916
  113.4 10.7 %collective-permute-start.3 = (f32[784,128]{1,0:T(8,128)}, f32[784,128]{1,0:T(8,128)S(1)}, u32[]{:S(2)}, u32[]{:S(2)}) collective-permute-start(f32[784,128]{1,0:T(8,128)} %get-tuple-element.22), channel_id=1, source_target_pairs={{0,6},{2,0},{4,2},{6,4},{1,7},{3,1},{5,3},{7,5},{8,14},{10,8},{12,... | collective-permute-start | bytes 1204232 | tf_op jit(solution)/shard_map/ppermute | solution.py:197
  114.2 11.9 %collective-permute-start.2 = (f32[784,128]{1,0:T(8,128)}, f32[784,128]{1,0:T(8,128)S(1)}, u32[]{:S(2)}, u32[]{:S(2)}) collective-permute-start(f32[784,128]{1,0:T(8,128)} %get-tuple-element.23), channel_id=1, source_target_pairs={{0,4},{2,6},{4,0},{6,2},{1,5},{3,7},{5,1},{7,3},{8,12},{10,14},{12... | collective-permute-start | bytes 1204232 | tf_op jit(solution)/shard_map/ppermute | solution.py:197
  114.8 21.0 %collective-permute-start.1 = (f32[784,128]{1,0:T(8,128)S(1)}, f32[784,128]{1,0:T(8,128)S(1)}, u32[]{:S(2)}, u32[]{:S(2)}) collective-permute-start(f32[784,128]{1,0:T(8,128)S(1)} %get-tuple-element.24), channel_id=1, source_target_pairs={{0,2},{2,4},{4,6},{6,0},{1,3},{3,5},{5,7},{7,1},{8,10},{10,12},{12... | collective-permute-start | bytes 1204232 | tf_op jit(solution)/shard_map/ppermute | solution.py:197

commit v10 on v6

--- a/solution.py
+++ b/solution.py
@@ -43,10 +43,23 @@
             fb = jnp.exp(mb - nm)
             run = (nm, rl * fa + lb * fb, ra * fa + ob * fb)
     rm, rl, ra = run
-    m_ref[...] = jnp.transpose(jnp.broadcast_to(rm, (rows, HEAD_WIDTH)))[0:8]
-    l_ref[...] = jnp.transpose(jnp.broadcast_to(rl, (rows, HEAD_WIDTH)))[0:8]
     parts = acc_ref.shape[0]
     tok = tree_len // parts
+    gap = jnp.zeros((HEAD_WIDTH - groups * tok, 1), jnp.float32)
+
+    def lane_rows(col, out_ref):
+        pieces = []
+        for j in range(parts):
+            for g in range(groups):
+                pieces.append(col[g * tree_len + j * tok:g * tree_len + (j + 1) * tok])
+            pieces.append(gap)
+        wide = jnp.concatenate(pieces, axis=0)
+        flat = jnp.transpose(jnp.broadcast_to(wide, (parts * HEAD_WIDTH, HEAD_WIDTH)))[0:1]
+        for j in range(parts):
+            out_ref[j:j + 1, :] = flat[:, j * HEAD_WIDTH:(j + 1) * HEAD_WIDTH]
+
+    lane_rows(rm, m_ref)
+    lane_rows(rl, l_ref)
     for j in range(parts):
         for g in range(groups):
             src = slice(g * tree_len + j * tok, g * tree_len + (j + 1) * tok)
@@ -79,8 +92,8 @@
         grid=(slots, kh),
         in_specs=in_specs,
         out_specs=[
-            pl.BlockSpec((None, None, 8, rows), lambda i, k, lv: (i, lv[slots] * kh + k, 0, 0)),
-            pl.BlockSpec((None, None, 8, rows), lambda i, k, lv: (i, lv[slots] * kh + k, 0, 0)),
+            pl.BlockSpec((None, None, per_slot, HEAD_WIDTH), lambda i, k, lv: (lv[slots] * kh + k, i, 0, 0)),
+            pl.BlockSpec((None, None, per_slot, HEAD_WIDTH), lambda i, k, lv: (lv[slots] * kh + k, i, 0, 0)),
             pl.BlockSpec(
                 (per_slot, None, sub, HEAD_WIDTH), lambda i, k, lv: (i, lv[slots] * kh + k, 0, 0)
             ),
@@ -90,8 +103,8 @@
         kern,
         grid_spec=grid_spec,
         out_shape=[
-            jax.ShapeDtypeStruct((slots, kvh, 8, rows), jnp.float32),
-            jax.ShapeDtypeStruct((slots, kvh, 8, rows), jnp.float32),
+            jax.ShapeDtypeStruct((kvh, slots, per_slot, HEAD_WIDTH), jnp.float32),
+            jax.ShapeDtypeStruct((kvh, slots, per_slot, HEAD_WIDTH), jnp.float32),
             jax.ShapeDtypeStruct((seq_count, kvh, sub, HEAD_WIDTH), jnp.float32),
         ],
         input_output_aliases=aliases,
@@ -157,40 +170,33 @@
     first = ci == 0
     per_slot = seq_count // local_reqs
     tok = tree_len // per_slot
-
-    def dest_major(rows_arr):
-        r = rows_arr[:, :, 0, :].reshape(local_reqs, kv_heads, groups, per_slot, tok)
-        return r.transpose(0, 3, 1, 2, 4).reshape(seq_count, kv_heads, groups * tok)
-
-    part_m = dest_major(m_rows)
-    part_l = dest_major(l_rows)
     sub = part_acc.shape[2]
     rows_acc = kv_heads * sub
-    stat_rows = rows_acc // HEAD_WIDTH
-    pad = (-(rows_acc + 2 * stat_rows)) % 8
+
+    def dest_rows(r):
+        return r.reshape(kv_heads, seq_count, HEAD_WIDTH).transpose(1, 0, 2).reshape(
+            nx, nc, kv_heads, HEAD_WIDTH
+        )
 
     def pack(acc, m, l):
-        lead = acc.shape[:-2]
-        parts = [acc, m.reshape(lead + (stat_rows, HEAD_WIDTH)), l.reshape(lead + (stat_rows, HEAD_WIDTH))]
-        if pad:
-            parts.append(jnp.zeros(lead + (pad, HEAD_WIDTH), jnp.float32))
-        return jnp.concatenate(parts, axis=-2)
+        return jnp.concatenate([acc, m, l], axis=-2)
 
     def unpack(pk):
+        acc = pk[..., :rows_acc, :]
+        m = pk[..., rows_acc:rows_acc + kv_heads, :sub]
+        l = pk[..., rows_acc + kv_heads:, :sub]
         lead = pk.shape[:-2]
-        acc = pk[..., :rows_acc, :]
-        m = pk[..., rows_acc:rows_acc + stat_rows, :].reshape(lead + (rows_acc,))
-        l = pk[..., rows_acc + stat_rows:rows_acc + 2 * stat_rows, :].reshape(lead + (rows_acc,))
-        return m, l, acc
-
-    pk = pack(
-        part_acc.reshape(nx, nc, rows_acc, HEAD_WIDTH),
-        part_m.reshape(nx, nc, rows_acc),
-        part_l.reshape(nx, nc, rows_acc),
-    )
+        return m.reshape(lead + (rows_acc,)), l.reshape(lead + (rows_acc,)), acc
+
+    def rows_of(v):
+        lead = v.shape[:-1]
+        v = v.reshape(lead + (kv_heads, sub))
+        return jnp.pad(v, [(0, 0)] * len(lead) + [(0, 0), (0, HEAD_WIDTH - sub)])
+
+    pk = pack(part_acc.reshape(nx, nc, rows_acc, HEAD_WIDTH), dest_rows(m_rows), dest_rows(l_rows))
     pk = lax.all_to_all(pk, "c", 1, 1, tiled=True)
     m1, l1, a1 = merge_pair(*unpack(pk), axis=1)
-    pk = lax.all_to_all(pack(a1, m1, l1), "x", 0, 0, tiled=True)
+    pk = lax.all_to_all(pack(a1, rows_of(m1), rows_of(l1)), "x", 0, 0, tiled=True)
     rm, rl, acc = unpack(pk)
 
     my_slot = position // per_slot

time: 131 us -> 133 us (1.015)
  local copies, waits for them, and re-layouts: 12.3 us -> 7.15 us
  Pallas kernels: 30.8 us -> 35.4 us
  other arithmetic: 7.38 us -> 9.45 us
    pallas_call x2, Pallas kernels: 30.8 us -> 35.4 us  [local_attention(): pl.pallas_call(kern, grid_spec=grid_spec, out_shape=[jax.ShapeDtypeStruct...]
    another operation x6 -> x0, local copies, waits for them, and re-layouts: 4.37 us -> none  [the longest x4 2.13 us: dest_major(): rows_arr[:, :, 0, :].reshape(local_reqs, kv_heads, groups, per_slot, tok)]
    squeeze x1, local copies, waits for them, and re-layouts: 1.86 us -> 0.04 us  [body(): mine_own = lax.dynamic_index_in_dim(own_x, my_slot, 0, keepdims=False)]
    unnamed x15 -> x13, local copies, waits for them, and re-layouts: 0.94 us -> 2.59 us
    reduce_sum x2, other arithmetic: 1.75 us -> 3.17 us  [merge_pair(): jnp.sum(f[..., None] * acc, axis=axis)]
  transfers between devices with their start and end apart: 3 -> 3, of which waited for: 2 -> 2; matrix products, arithmetic and copies ran while one was open for 5% -> 3% of each run, Pallas kernels for 12% -> 13%
where the time goes in v10:
time: 133 us; the launch traced here: 132 us
  Pallas kernels  35.4 us (27%)
  blocking collectives  32.9 us (25%)
  waiting for transfers between devices  30 us (23%)
  starting transfers between devices  14.9 us (11%)
  other arithmetic  9.45 us (7%)
  local copies, waits for them, and re-layouts  7.15 us (5%)
  matrix products  1.48 us (1%)
    pallas_call x2, Pallas kernels, local_attention(): pl.pallas_call(kern, grid_spec=grid_spec, out_shape=[jax.ShapeDtypeStruct...  35.4 us
    all_to_all x1, waiting for transfers between devices, body(): lax.all_to_all(pack(a1, rows_of(m1), rows_of(l1)), 'x', 0, 0, tiled=True)  18.4 us
    all_gather x1, blocking collectives, body(): held = lax.all_gather(both, 'z', axis=0, tiled=True)  15 us
    all_gather x1, blocking collectives, body(): own_x = lax.all_gather(own, 'x', axis=1, tiled=False)  12 us
    all_to_all x1, waiting for transfers between devices, body(): recv = lax.all_to_all(send, 'y', 0, 0, tiled=True)  11.6 us
    ppermute x1, starting transfers between devices, body(): other_x = lax.ppermute(own_x, 'c', perm=[(0, 1), (1, 0)])  7.01 us
    all_to_all x1, blocking collectives, body(): pk = lax.all_to_all(pk, 'c', 1, 1, tiled=True)  5.95 us
    all_to_all x1, starting transfers between devices, body(): recv = lax.all_to_all(send, 'y', 0, 0, tiled=True)  4.31 us
  transfers between devices with their start and end apart: 3, of which 2 were waited for; matrix products, arithmetic and copies ran while one was open for 3% of the time, Pallas kernels for 13%

profile of v10, /device:TPU:1, one launch (start us, length us, event | category | flops | bytes accessed | tf_op | source)
XLA Modules:
  0.0 132.2 jit_solution(14254167939506450146)
XLA Ops:
  0.7 1.3 gather_fusion
  2.1 1.0 pad_maximum_fusion.1
  3.1 15.0 %all_gather.7 = bf16[8,48,1280]{2,1,0:T(8,128)(2,1)S(1)} all-gather(bf16[2,48,1280]{2,1,0:T(8,128)(2,1)S(1)} %pad_maximum_fusion.1), channel_id=1, replica_groups=mesh['z'=4,'y'=4,'x'=4,'c'=2] {'z'}, dimensions={0}, use_global_device_ids=true | all-gather | bytes 1228800 | tf_op jit(solution)/shard_map/all_gather | solution.py:146
  18.1 0.6 gather_fusion.1
  18.7 1.1 broadcast_select_fusion
  19.8 4.3 %all-to-all-start = ((bf16[4,2,48,1280]{3,2,1,0:T(8,128)(2,1)}), bf16[4,2,48,1280]{3,2,1,0:T(8,128)(2,1)S(1)}, u32[]{:S(2)}, u32[]{:S(2)}) async-start(bf16[4,2,48,1280]{3,2,1,0:T(8,128)(2,1)} %broadcast_select_fusion), calls=%async_computation | async-start | bytes 1966080 | tf_op jit(solution)/shard_map/all_to_all | solution.py:152
  24.2 11.6 %all-to-all-done = bf16[4,2,48,1280]{3,2,1,0:T(8,128)(2,1)S(1)} async-done(((bf16[4,2,48,1280]{3,2,1,0:T(8,128)(2,1)}), bf16[4,2,48,1280]{3,2,1,0:T(8,128)(2,1)S(1)}, u32[]{:S(2)}, u32[]{:S(2)}) %all-to-all-start) | async-done | bytes 983072 | tf_op jit(solution)/shard_map/all_to_all | solution.py:152
  35.9 0.6 gather_fusion.2
  36.5 12.0 %all_gather.8.q_ref = bf16[2,4,48,1280]{3,2,1,0:T(8,128)(2,1)S(1)} all-gather(bf16[2,1,48,1280]{3,2,1,0:T(8,128)(2,1)S(1)} %bitcast_select_fusion), channel_id=1, replica_groups=mesh['z'=4,'y'=4,'x'=4,'c'=2] {'x'}, dimensions={1}, use_global_device_ids=true | all-gather | bytes 1228800 | tf_op jit(solution)/shard_map/all_gather | solution.py:159
  48.5 7.0 %collective-permute-start = (bf16[2,4,48,1280]{3,2,1,0:T(8,128)(2,1)S(1)}, bf16[2,4,48,1280]{3,2,1,0:T(8,128)(2,1)S(1)}, u32[]{:S(2)}, u32[]{:S(2)}) collective-permute-start(bf16[2,4,48,1280]{3,2,1,0:T(8,128)(2,1)S(1)} %all_gather.8.q_ref), channel_id=1, source_target_pairs={{0,1},{1,0},{2,3},{3,2},{4,5},{5,4},{6,7},{7,6},{8,9},{9,8},{10,11... | collective-permute-start | bytes 2949128 | tf_op jit(solution)/shard_map/ppermute | solution.py:160
  55.6 0.7 fusion.17
  56.3 0.8 convolution_convert_fusion
  57.1 17.7 %shard_map.86 = (f32[8,2,4,128]{3,2,1,0:T(4,128)S(1)}, f32[8,2,4,128]{3,2,1,0:T(4,128)S(1)}, f32[8,8,96,128]{3,2,1,0:T(8,128)S(1)}) custom-call(s32[3]{0:T(128)S(1)} %get-tuple-element.25.live_ref, bf16[2,4,48,1280]{3,2,1,0:T(8,128)(2,1)S(1)} %all_gather.8.q_ref, bf16[2,2048,2048]{2,1,0:T(8,128)(2,1)} %kv_ref.3), custom_call_target="tpu_custom_call" | custom-call | tf_op jit(solution)/shard_map/pallas_call | solution.py:102
  74.9 17.7 %shard_map.87 = (f32[8,2,4,128]{3,2,1,0:T(4,128)S(1)}, f32[8,2,4,128]{3,2,1,0:T(4,128)S(1)}, f32[8,8,96,128]{3,2,1,0:T(8,128)S(1)}) custom-call(s32[3]{0:T(128)S(1)} %get-tuple-element.26.live_ref, bf16[2,4,48,1280]{3,2,1,0:T(8,128)(2,1)S(1)} %collective-permute-done.q_ref, ...), custom_call_target="tpu_custom_call", output_to_operand_aliasing={{0}: (3, {}), {1}: (4, {}), {2}: (5, {})} | custom-call | tf_op jit(solution)/shard_map/pallas_call | solution.py:102
  92.6 0.2 pad_maximum_fusion
  92.8 0.2 copy.55
  93.1 6.0 %all_to_all.15 = f32[4,2,784,128]{3,2,0,1:T(8,128)S(1)} all-to-all(f32[4,2,784,128]{3,2,0,1:T(8,128)S(1)} %copy.55), channel_id=1, replica_groups=mesh['z'=4,'y'=4,'x'=4,'c'=2] {'c'}, dimensions={1} | all-to-all | bytes 6422528 | tf_op jit(solution)/shard_map/all_to_all | solution.py:197
  99.0 1.7 %copy-done.1 = f32[4,2,784,128]{3,2,0,1:T(8,128)} copy-done((f32[4,2,784,128]{3,2,0,1:T(8,128)}, f32[4,2,784,128]{3,2,0,1:T(8,128)S(1)}, u32[]{:S(2)}) %copy-start.1) | copy-done | bytes 3211288
  100.9 0.8 fusion.14
  101.7 2.5 %fusion = f32[4,768,128]{2,1,0:T(8,128)S(1)} fusion(f32[4,2,784,128]{3,2,0,1:T(8,128)} %copy-done.1, f32[4,2,768]{2,0,1:T(4,128)S(1)} %bitcast.82), kind=kLoop, calls=%fused_computation.5 | loop fusion | flops 1179648 | bytes 4743168 | tf_op jit(solution)/shard_map/reduce_sum | solution.py:124
  104.2 1.3 select_maximum_fusion
  105.4 3.6 %all-to-all-start.2 = ((f32[4,784,128]{2,1,0:T(8,128)}), f32[4,784,128]{2,1,0:T(8,128)S(1)}, u32[]{:S(2)}, u32[]{:S(2)}) async-start(f32[4,784,128]{2,1,0:T(8,128)} %select_maximum_fusion), calls=%async_computation.2 | async-start | bytes 3211264 | tf_op jit(solution)/shard_map/all_to_all | solution.py:199
  109.1 0.2 maximum_select_fusion
  109.4 0.1 reshape.328
  109.7 0.3 fusion.33
  109.9 0.4 fusion.34
  110.5 0.3 fusion.7
  110.9 0.4 fusion.5
  111.4 18.4 %all-to-all-done.2 = f32[4,784,128]{2,1,0:T(8,128)S(1)} async-done(((f32[4,784,128]{2,1,0:T(8,128)}), f32[4,784,128]{2,1,0:T(8,128)S(1)}, u32[]{:S(2)}, u32[]{:S(2)}) %all-to-all-start.2) | async-done | bytes 1605664 | tf_op jit(solution)/shard_map/all_to_all | solution.py:199
  130.3 0.7 fusion.1
  131.0 0.2 fusion.12
  131.3 0.9 copy.60
  (49 shorter events, 1.9 us)
Async XLA Ops:
  18.7 5.4 %copy-start = (s32[32]{0:T(128)S(1)}, s32[32]{0:T(128)}, u32[]{:S(2)}) copy-start(s32[32]{0:T(128)} %param.12) | copy-start | bytes 388
  19.8 35.7 %copy-start.4 = (s32[2]{0:T(128)S(1)}, s32[2]{0:T(128)}, u32[]{:S(2)}) copy-start(s32[2]{0:T(128)} %param.10) | copy-start | bytes 28
  19.8 36.5 %copy-start.2 = (bf16[2,48,256]{2,1,0:T(8,128)(2,1)S(1)}, bf16[2,48,256]{2,1,0:T(8,128)(2,1)}, u32[]{:S(2)}) copy-start(bf16[2,48,256]{2,1,0:T(8,128)(2,1)} %param.8) | copy-start | bytes 147460
  19.8 36.5 %copy-start.3 = (s32[2,8]{1,0:T(2,128)S(1)}, s32[2,8]{1,0:T(2,128)}, u32[]{:S(2)}) copy-start(s32[2,8]{1,0:T(2,128)} %param.13) | copy-start | bytes 196
  19.8 16.0 %all-to-all-start = ((bf16[4,2,48,1280]{3,2,1,0:T(8,128)(2,1)}), bf16[4,2,48,1280]{3,2,1,0:T(8,128)(2,1)S(1)}, u32[]{:S(2)}, u32[]{:S(2)}) async-start(bf16[4,2,48,1280]{3,2,1,0:T(8,128)(2,1)} %broadcast_select_fusion), calls=%async_computation | async-start | bytes 1966080 | tf_op jit(solution)/shard_map/all_to_all | solution.py:152
  48.5 26.4 %collective-permute-start = (bf16[2,4,48,1280]{3,2,1,0:T(8,128)(2,1)S(1)}, bf16[2,4,48,1280]{3,2,1,0:T(8,128)(2,1)S(1)}, u32[]{:S(2)}, u32[]{:S(2)}) collective-permute-start(bf16[2,4,48,1280]{3,2,1,0:T(8,128)(2,1)S(1)} %all_gather.8.q_ref), channel_id=1, source_target_pairs={{0,1},{1,0},{2,3},{3,2},{4,5},{5,4},{6,7},{7,6},{8,9},{9,8},{10,11... | collective-permute-start | bytes 2949128 | tf_op jit(solution)/shard_map/ppermute | solution.py:160
  99.0 1.7 %copy-start.1 = (f32[4,2,784,128]{3,2,0,1:T(8,128)}, f32[4,2,784,128]{3,2,0,1:T(8,128)S(1)}, u32[]{:S(2)}) copy-start(f32[4,2,784,128]{3,2,0,1:T(8,128)S(1)} %all_to_all.15) | copy-start | bytes 9633796
  105.4 24.3 %all-to-all-start.2 = ((f32[4,784,128]{2,1,0:T(8,128)}), f32[4,784,128]{2,1,0:T(8,128)S(1)}, u32[]{:S(2)}, u32[]{:S(2)}) async-start(f32[4,784,128]{2,1,0:T(8,128)} %select_maximum_fusion), calls=%async_computation.2 | async-start | bytes 3211264 | tf_op jit(solution)/shard_map/all_to_all | solution.py:199

commit v11 on v6

--- a/solution.py
+++ b/solution.py
@@ -29,9 +29,10 @@
             q, keys, (((1,), (1,)), ((), ())), preferred_element_type=jnp.float32
         ) * scale
         pos = b * BLK + lax.broadcasted_iota(jnp.int32, (1, BLK), 1)
-        s = s + jnp.where(pos < live, jnp.float32(0.0), jnp.float32(NEG))
+        allowed = pos < live
+        s = jnp.where(allowed, s, jnp.float32(NEG))
         mb = jnp.max(s, axis=1, keepdims=True)
-        w = jnp.exp(s - mb)
+        w = jnp.where(allowed, jnp.exp(s - mb), jnp.float32(0.0))
         lb = jnp.sum(w, axis=1, keepdims=True)
         ob = jnp.dot(w.astype(jnp.bfloat16), vals, preferred_element_type=jnp.float32)
         if run is None:

time: 131 us -> 133 us (1.015)
  Pallas kernels: 30.8 us -> 32.9 us
    pallas_call x2, Pallas kernels: 30.8 us -> 32.9 us  [local_attention(): pl.pallas_call(kern, grid_spec=grid_spec, out_shape=[jax.ShapeDtypeStruct...]
where the time goes in v11:
time: 133 us; the launch traced here: 132 us
  blocking collectives  33.3 us (25%)
  Pallas kernels  32.9 us (25%)
  waiting for transfers between devices  29 us (22%)
  starting transfers between devices  15.1 us (11%)
  local copies, waits for them, and re-layouts  12.3 us (9%)
  other arithmetic  7.38 us (6%)
  matrix products  1.48 us (1%)
    pallas_call x2, Pallas kernels, local_attention(): pl.pallas_call(kern, grid_spec=grid_spec, out_shape=[jax.ShapeDtypeStruct...  32.9 us
    all_to_all x1, waiting for transfers between devices, body(): pk = lax.all_to_all(pack(a1, m1, l1), 'x', 0, 0, tiled=True)  17.3 us
    all_gather x1, blocking collectives, body(): held = lax.all_gather(both, 'z', axis=0, tiled=True)  15 us
    all_gather x1, blocking collectives, body(): own_x = lax.all_gather(own, 'x', axis=1, tiled=False)  12.4 us
    all_to_all x1, waiting for transfers between devices, body(): recv = lax.all_to_all(send, 'y', 0, 0, tiled=True)  11.6 us
    ppermute x1, starting transfers between devices, body(): other_x = lax.ppermute(own_x, 'c', perm=[(0, 1), (1, 0)])  7.33 us
    all_to_all x1, blocking collectives, body(): pk = lax.all_to_all(pk, 'c', 1, 1, tiled=True)  5.95 us
    all_to_all x1, starting transfers between devices, body(): recv = lax.all_to_all(send, 'y', 0, 0, tiled=True)  4.18 us
  transfers between devices with their start and end apart: 3, of which 2 were waited for; matrix products, arithmetic and copies ran while one was open for 5% of the time, Pallas kernels for 12%

profile of v11, /device:TPU:1, one launch (start us, length us, event | category | flops | bytes accessed | tf_op | source)
XLA Modules:
  0.0 132.4 jit_solution(10858067746644546408)
XLA Ops:
  0.7 1.3 gather_fusion
  2.1 1.0 pad_maximum_fusion
  3.1 15.0 %all_gather.7 = bf16[8,48,1280]{2,1,0:T(8,128)(2,1)S(1)} all-gather(bf16[2,48,1280]{2,1,0:T(8,128)(2,1)S(1)} %pad_maximum_fusion), channel_id=1, replica_groups=mesh['z'=4,'y'=4,'x'=4,'c'=2] {'z'}, dimensions={0}, use_global_device_ids=true | all-gather | bytes 1228800 | tf_op jit(solution)/shard_map/all_gather | solution.py:134
  18.1 0.6 gather_fusion.1
  18.7 1.1 broadcast_select_fusion
  19.8 4.2 %all-to-all-start = ((bf16[4,2,48,1280]{3,2,1,0:T(8,128)(2,1)}), bf16[4,2,48,1280]{3,2,1,0:T(8,128)(2,1)S(1)}, u32[]{:S(2)}, u32[]{:S(2)}) async-start(bf16[4,2,48,1280]{3,2,1,0:T(8,128)(2,1)} %broadcast_select_fusion), calls=%async_computation | async-start | bytes 1966080 | tf_op jit(solution)/shard_map/all_to_all | solution.py:140
  24.1 11.6 %all-to-all-done = bf16[4,2,48,1280]{3,2,1,0:T(8,128)(2,1)S(1)} async-done(((bf16[4,2,48,1280]{3,2,1,0:T(8,128)(2,1)}), bf16[4,2,48,1280]{3,2,1,0:T(8,128)(2,1)S(1)}, u32[]{:S(2)}, u32[]{:S(2)}) %all-to-all-start) | async-done | bytes 983072 | tf_op jit(solution)/shard_map/all_to_all | solution.py:140
  35.7 0.6 gather_fusion.2
  36.4 12.4 %all_gather.8.q_ref = bf16[2,4,48,1280]{3,2,1,0:T(8,128)(2,1)} all-gather(bf16[2,1,48,1280]{3,2,1,0:T(8,128)(2,1)S(1)} %bitcast_select_fusion), channel_id=1, replica_groups=mesh['z'=4,'y'=4,'x'=4,'c'=2] {'x'}, dimensions={1}, use_global_device_ids=true | all-gather | bytes 1228800 | tf_op jit(solution)/shard_map/all_gather | solution.py:147
  48.8 7.3 %collective-permute-start = (bf16[2,4,48,1280]{3,2,1,0:T(8,128)(2,1)}, bf16[2,4,48,1280]{3,2,1,0:T(8,128)(2,1)}, u32[]{:S(2)}, u32[]{:S(2)}) collective-permute-start(bf16[2,4,48,1280]{3,2,1,0:T(8,128)(2,1)} %all_gather.8.q_ref), channel_id=1, source_target_pairs={{0,1},{1,0},{2,3},{3,2},{4,5},{5,4},{6,7},{7,6},{8,9},{9,8},{10,11... | collective-permute-start | bytes 2949128 | tf_op jit(solution)/shard_map/ppermute | solution.py:148
  56.3 0.7 fusion.17
  57.0 0.8 convolution_convert_fusion
  57.8 16.5 %shard_map.86 = (f32[2,8,8,384]{3,2,1,0:T(8,128)S(1)}, f32[2,8,8,384]{3,2,1,0:T(8,128)S(1)}, f32[8,8,96,128]{3,2,1,0:T(8,128)S(1)}) custom-call(s32[3]{0:T(128)S(1)} %get-tuple-element.25.live_ref, bf16[2,4,48,1280]{3,2,1,0:T(8,128)(2,1)} %all_gather.8.q_ref, bf16[2,2048,2048]{2,1,0:T(8,128)(2,1)} %kv_ref.3), custom_call_target="tpu_custom_call" | custom-call | tf_op jit(solution)/shard_map/pallas_call | solution.py:90
  74.3 1.9 %dynamic-slice_bitcast_fusion.1 = bf16[4,48,1280]{2,1,0:T(8,128)(2,1)} fusion(bf16[2,4,48,1280]{3,2,1,0:T(8,128)(2,1)} %all_gather.8.q_ref, s32[]{:T(128)S(6)} %select_n.167), kind=kLoop, calls=%fused_computation.18 | loop fusion | bytes 983044 | tf_op jit(solution)/shard_map/jit(dynamic_index_in_dim)/squeeze | solution.py:199
  76.1 16.5 %shard_map.87 = (f32[2,8,8,384]{3,2,1,0:T(8,128)S(1)}, f32[2,8,8,384]{3,2,1,0:T(8,128)S(1)}, f32[8,8,96,128]{3,2,1,0:T(8,128)S(1)}) custom-call(s32[3]{0:T(128)S(1)} %get-tuple-element.26.live_ref, bf16[2,4,48,1280]{3,2,1,0:T(8,128)(2,1)} %collective-permute-done.q_ref, ...), custom_call_target="tpu_custom_call", output_to_operand_aliasing={{0}: (3, {}), {1}: (4, {}), {2}: (5, {})} | custom-call | tf_op jit(solution)/shard_map/pallas_call | solution.py:90
  92.7 0.3 reshape_squeeze.7
  93.1 0.7 copy.74
  93.8 1.1 reshape_reshape_reshape.7
  94.9 0.3 reshape_squeeze.6
  95.3 0.7 copy.75
  96.0 1.1 reshape_reshape_reshape.6
  97.4 6.0 %all_to_all.15 = f32[4,2,784,128]{3,2,0,1:T(8,128)S(1)} all-to-all(f32[4,2,784,128]{3,2,0,1:T(8,128)S(1)} %maximum_maximum_fusion), channel_id=1, replica_groups=mesh['z'=4,'y'=4,'x'=4,'c'=2] {'c'}, dimensions={1} | all-to-all | bytes 6422528 | tf_op jit(solution)/shard_map/all_to_all | solution.py:192
  103.5 1.1 fusion
  104.6 1.3 %maximum_maximum_fusion.1 = f32[4,784,128]{2,1,0:T(8,128)} fusion(f32[4,6,128]{2,1,0:T(8,128)S(1)} %fusion.13, f32[4,6,128]{2,1,0:T(8,128)S(1)} %get-tuple-element.17, f32[4,768,128]{2,1,0:T(8,128)S(1)} %fusion, f32[784]{0:T(1024)S(1)} %pad.17.clone), kind=kLoop, calls=%fused_computation.8 | loop fusion | flops 1204224 | bytes 3206208 | tf_op jit(solution)/shard_map/concatenate | solution.py:178
  105.9 3.6 %all-to-all-start.2 = ((f32[4,784,128]{2,1,0:T(8,128)}), f32[4,784,128]{2,1,0:T(8,128)S(1)}, u32[]{:S(2)}, u32[]{:S(2)}) async-start(f32[4,784,128]{2,1,0:T(8,128)} %maximum_maximum_fusion.1), calls=%async_computation.2 | async-start | bytes 3211264 | tf_op jit(solution)/shard_map/all_to_all | solution.py:194
  109.5 1.1 dynamic-slice_bitcast_fusion
  111.4 0.4 fusion.33
  112.0 0.3 fusion.6
  112.4 0.4 fusion.4
  112.9 17.3 %all-to-all-done.2 = f32[4,784,128]{2,1,0:T(8,128)S(1)} async-done(((f32[4,784,128]{2,1,0:T(8,128)}), f32[4,784,128]{2,1,0:T(8,128)S(1)}, u32[]{:S(2)}, u32[]{:S(2)}) %all-to-all-start.2) | async-done | bytes 1605664 | tf_op jit(solution)/shard_map/all_to_all | solution.py:194
  130.5 0.7 fusion.1
  131.6 0.9 copy.49
  (54 shorter events, 2.7 us)
Async XLA Ops:
  18.1 6.0 %copy-start = (s32[32]{0:T(128)S(1)}, s32[32]{0:T(128)}, u32[]{:S(2)}) copy-start(s32[32]{0:T(128)} %param.12) | copy-start | bytes 388
  18.7 37.5 %copy-start.4 = (s32[2]{0:T(128)S(1)}, s32[2]{0:T(128)}, u32[]{:S(2)}) copy-start(s32[2]{0:T(128)} %param.10) | copy-start | bytes 28
  18.7 38.3 %copy-start.2 = (bf16[2,48,256]{2,1,0:T(8,128)(2,1)S(1)}, bf16[2,48,256]{2,1,0:T(8,128)(2,1)}, u32[]{:S(2)}) copy-start(bf16[2,48,256]{2,1,0:T(8,128)(2,1)} %param.8) | copy-start | bytes 147460
  18.7 38.3 %copy-start.3 = (s32[2,8]{1,0:T(2,128)S(1)}, s32[2,8]{1,0:T(2,128)}, u32[]{:S(2)}) copy-start(s32[2,8]{1,0:T(2,128)} %param.13) | copy-start | bytes 196
  19.8 15.9 %all-to-all-start = ((bf16[4,2,48,1280]{3,2,1,0:T(8,128)(2,1)}), bf16[4,2,48,1280]{3,2,1,0:T(8,128)(2,1)S(1)}, u32[]{:S(2)}, u32[]{:S(2)}) async-start(bf16[4,2,48,1280]{3,2,1,0:T(8,128)(2,1)} %broadcast_select_fusion), calls=%async_computation | async-start | bytes 1966080 | tf_op jit(solution)/shard_map/all_to_all | solution.py:140
  48.8 27.3 %collective-permute-start = (bf16[2,4,48,1280]{3,2,1,0:T(8,128)(2,1)}, bf16[2,4,48,1280]{3,2,1,0:T(8,128)(2,1)}, u32[]{:S(2)}, u32[]{:S(2)}) collective-permute-start(bf16[2,4,48,1280]{3,2,1,0:T(8,128)(2,1)} %all_gather.8.q_ref), channel_id=1, source_target_pairs={{0,1},{1,0},{2,3},{3,2},{4,5},{5,4},{6,7},{7,6},{8,9},{9,8},{10,11... | collective-permute-start | bytes 2949128 | tf_op jit(solution)/shard_map/ppermute | solution.py:148
  104.5 6.0 %copy-start.1 = (bf16[4,48,1280]{2,1,0:T(8,128)(2,1)S(1)}, bf16[4,48,1280]{2,1,0:T(8,128)(2,1)}, u32[]{:S(2)}) copy-start(bf16[4,48,1280]{2,1,0:T(8,128)(2,1)} %dynamic-slice_bitcast_fusion.1) | copy-start | bytes 1474564
  105.9 24.3 %all-to-all-start.2 = ((f32[4,784,128]{2,1,0:T(8,128)}), f32[4,784,128]{2,1,0:T(8,128)S(1)}, u32[]{:S(2)}, u32[]{:S(2)}) async-start(f32[4,784,128]{2,1,0:T(8,128)} %maximum_maximum_fusion.1), calls=%async_computation.2 | async-start | bytes 3211264 | tf_op jit(solution)/shard_map/all_to_all | solution.py:194

commit v12 on v11

--- a/solution.py
+++ b/solution.py
@@ -32,7 +32,7 @@
         allowed = pos < live
         s = jnp.where(allowed, s, jnp.float32(NEG))
         mb = jnp.max(s, axis=1, keepdims=True)
-        w = jnp.where(allowed, jnp.exp(s - mb), jnp.float32(0.0))
+        w = jnp.exp(s - jnp.where(live > b * BLK, mb, jnp.float32(0.0)))
         lb = jnp.sum(w, axis=1, keepdims=True)
         ob = jnp.dot(w.astype(jnp.bfloat16), vals, preferred_element_type=jnp.float32)
         if run is None:

time: 133 us -> 132 us (level)
  no operation moved by 1% of the time
where the time goes in v12:
time: 132 us
  blocking collectives  33.3 us (25%)
  Pallas kernels  32.3 us (24%)
  waiting for transfers between devices  29 us (22%)
  starting transfers between devices  15.1 us (11%)
  local copies, waits for them, and re-layouts  12.3 us (9%)
  other arithmetic  7.38 us (6%)
  matrix products  1.48 us (1%)
    pallas_call x2, Pallas kernels, local_attention(): pl.pallas_call(kern, grid_spec=grid_spec, out_shape=[jax.ShapeDtypeStruct...  32.3 us
    all_to_all x1, waiting for transfers between devices, body(): pk = lax.all_to_all(pack(a1, m1, l1), 'x', 0, 0, tiled=True)  17.3 us
    all_gather x1, blocking collectives, body(): held = lax.all_gather(both, 'z', axis=0, tiled=True)  15 us
    all_gather x1, blocking collectives, body(): own_x = lax.all_gather(own, 'x', axis=1, tiled=False)  12.4 us
    all_to_all x1, waiting for transfers between devices, body(): recv = lax.all_to_all(send, 'y', 0, 0, tiled=True)  11.6 us
    ppermute x1, starting transfers between devices, body(): other_x = lax.ppermute(own_x, 'c', perm=[(0, 1), (1, 0)])  7.33 us
    all_to_all x1, blocking collectives, body(): pk = lax.all_to_all(pk, 'c', 1, 1, tiled=True)  5.95 us
    all_to_all x1, starting transfers between devices, body(): recv = lax.all_to_all(send, 'y', 0, 0, tiled=True)  4.18 us
  transfers between devices with their start and end apart: 3, of which 2 were waited for; matrix products, arithmetic and copies ran while one was open for 5% of the time, Pallas kernels for 12%

profile of v12, /device:TPU:1, one launch (start us, length us, event | category | flops | bytes accessed | tf_op | source)
XLA Modules:
  0.0 131.9 jit_solution(15414206068651973213)
XLA Ops:
  0.7 1.3 gather_fusion
  2.1 1.0 pad_maximum_fusion
  3.1 15.0 %all_gather.7 = bf16[8,48,1280]{2,1,0:T(8,128)(2,1)S(1)} all-gather(bf16[2,48,1280]{2,1,0:T(8,128)(2,1)S(1)} %pad_maximum_fusion), channel_id=1, replica_groups=mesh['z'=4,'y'=4,'x'=4,'c'=2] {'z'}, dimensions={0}, use_global_device_ids=true | all-gather | bytes 1228800 | tf_op jit(solution)/shard_map/all_gather | solution.py:134
  18.1 0.6 gather_fusion.1
  18.7 1.1 broadcast_select_fusion
  19.8 4.2 %all-to-all-start = ((bf16[4,2,48,1280]{3,2,1,0:T(8,128)(2,1)}), bf16[4,2,48,1280]{3,2,1,0:T(8,128)(2,1)S(1)}, u32[]{:S(2)}, u32[]{:S(2)}) async-start(bf16[4,2,48,1280]{3,2,1,0:T(8,128)(2,1)} %broadcast_select_fusion), calls=%async_computation | async-start | bytes 1966080 | tf_op jit(solution)/shard_map/all_to_all | solution.py:140
  24.1 11.6 %all-to-all-done = bf16[4,2,48,1280]{3,2,1,0:T(8,128)(2,1)S(1)} async-done(((bf16[4,2,48,1280]{3,2,1,0:T(8,128)(2,1)}), bf16[4,2,48,1280]{3,2,1,0:T(8,128)(2,1)S(1)}, u32[]{:S(2)}, u32[]{:S(2)}) %all-to-all-start) | async-done | bytes 983072 | tf_op jit(solution)/shard_map/all_to_all | solution.py:140
  35.7 0.6 gather_fusion.2
  36.4 12.4 %all_gather.8.q_ref = bf16[2,4,48,1280]{3,2,1,0:T(8,128)(2,1)} all-gather(bf16[2,1,48,1280]{3,2,1,0:T(8,128)(2,1)S(1)} %bitcast_select_fusion), channel_id=1, replica_groups=mesh['z'=4,'y'=4,'x'=4,'c'=2] {'x'}, dimensions={1}, use_global_device_ids=true | all-gather | bytes 1228800 | tf_op jit(solution)/shard_map/all_gather | solution.py:147
  48.8 7.3 %collective-permute-start = (bf16[2,4,48,1280]{3,2,1,0:T(8,128)(2,1)}, bf16[2,4,48,1280]{3,2,1,0:T(8,128)(2,1)}, u32[]{:S(2)}, u32[]{:S(2)}) collective-permute-start(bf16[2,4,48,1280]{3,2,1,0:T(8,128)(2,1)} %all_gather.8.q_ref), channel_id=1, source_target_pairs={{0,1},{1,0},{2,3},{3,2},{4,5},{5,4},{6,7},{7,6},{8,9},{9,8},{10,11... | collective-permute-start | bytes 2949128 | tf_op jit(solution)/shard_map/ppermute | solution.py:148
  56.3 0.7 fusion.17
  57.0 0.8 convolution_convert_fusion
  57.8 16.2 %shard_map.86 = (f32[2,8,8,384]{3,2,1,0:T(8,128)S(1)}, f32[2,8,8,384]{3,2,1,0:T(8,128)S(1)}, f32[8,8,96,128]{3,2,1,0:T(8,128)S(1)}) custom-call(s32[3]{0:T(128)S(1)} %get-tuple-element.25.live_ref, bf16[2,4,48,1280]{3,2,1,0:T(8,128)(2,1)} %all_gather.8.q_ref, bf16[2,2048,2048]{2,1,0:T(8,128)(2,1)} %kv_ref.3), custom_call_target="tpu_custom_call" | custom-call | tf_op jit(solution)/shard_map/pallas_call | solution.py:90
  74.0 1.9 %dynamic-slice_bitcast_fusion.1 = bf16[4,48,1280]{2,1,0:T(8,128)(2,1)} fusion(bf16[2,4,48,1280]{3,2,1,0:T(8,128)(2,1)} %all_gather.8.q_ref, s32[]{:T(128)S(6)} %select_n.167), kind=kLoop, calls=%fused_computation.18 | loop fusion | bytes 983044 | tf_op jit(solution)/shard_map/jit(dynamic_index_in_dim)/squeeze | solution.py:199
  75.9 16.2 %shard_map.87 = (f32[2,8,8,384]{3,2,1,0:T(8,128)S(1)}, f32[2,8,8,384]{3,2,1,0:T(8,128)S(1)}, f32[8,8,96,128]{3,2,1,0:T(8,128)S(1)}) custom-call(s32[3]{0:T(128)S(1)} %get-tuple-element.26.live_ref, bf16[2,4,48,1280]{3,2,1,0:T(8,128)(2,1)} %collective-permute-done.q_ref, ...), custom_call_target="tpu_custom_call", output_to_operand_aliasing={{0}: (3, {}), {1}: (4, {}), {2}: (5, {})} | custom-call | tf_op jit(solution)/shard_map/pallas_call | solution.py:90
  92.2 0.3 reshape_squeeze.7
  92.5 0.7 copy.74
  93.2 1.1 reshape_reshape_reshape.7
  94.3 0.3 reshape_squeeze.6
  94.7 0.7 copy.75
  95.4 1.1 reshape_reshape_reshape.6
  96.8 6.0 %all_to_all.15 = f32[4,2,784,128]{3,2,0,1:T(8,128)S(1)} all-to-all(f32[4,2,784,128]{3,2,0,1:T(8,128)S(1)} %maximum_maximum_fusion), channel_id=1, replica_groups=mesh['z'=4,'y'=4,'x'=4,'c'=2] {'c'}, dimensions={1} | all-to-all | bytes 6422528 | tf_op jit(solution)/shard_map/all_to_all | solution.py:192
  102.9 1.1 fusion
  104.0 1.3 %maximum_maximum_fusion.1 = f32[4,784,128]{2,1,0:T(8,128)} fusion(f32[4,6,128]{2,1,0:T(8,128)S(1)} %fusion.13, f32[4,6,128]{2,1,0:T(8,128)S(1)} %get-tuple-element.17, f32[4,768,128]{2,1,0:T(8,128)S(1)} %fusion, f32[784]{0:T(1024)S(1)} %pad.17.clone), kind=kLoop, calls=%fused_computation.8 | loop fusion | flops 1204224 | bytes 3206208 | tf_op jit(solution)/shard_map/concatenate | solution.py:178
  105.3 3.6 %all-to-all-start.2 = ((f32[4,784,128]{2,1,0:T(8,128)}), f32[4,784,128]{2,1,0:T(8,128)S(1)}, u32[]{:S(2)}, u32[]{:S(2)}) async-start(f32[4,784,128]{2,1,0:T(8,128)} %maximum_maximum_fusion.1), calls=%async_computation.2 | async-start | bytes 3211264 | tf_op jit(solution)/shard_map/all_to_all | solution.py:194
  108.9 1.1 dynamic-slice_bitcast_fusion
  110.8 0.4 fusion.33
  111.4 0.3 fusion.6
  111.8 0.4 fusion.4
  112.3 17.3 %all-to-all-done.2 = f32[4,784,128]{2,1,0:T(8,128)S(1)} async-done(((f32[4,784,128]{2,1,0:T(8,128)}), f32[4,784,128]{2,1,0:T(8,128)S(1)}, u32[]{:S(2)}, u32[]{:S(2)}) %all-to-all-start.2) | async-done | bytes 1605664 | tf_op jit(solution)/shard_map/all_to_all | solution.py:194
  129.9 0.7 fusion.1
  131.0 0.9 copy.49
  (54 shorter events, 2.7 us)
Async XLA Ops:
  18.1 6.0 %copy-start = (s32[32]{0:T(128)S(1)}, s32[32]{0:T(128)}, u32[]{:S(2)}) copy-start(s32[32]{0:T(128)} %param.12) | copy-start | bytes 388
  18.7 37.5 %copy-start.4 = (s32[2]{0:T(128)S(1)}, s32[2]{0:T(128)}, u32[]{:S(2)}) copy-start(s32[2]{0:T(128)} %param.10) | copy-start | bytes 28
  18.7 38.3 %copy-start.2 = (bf16[2,48,256]{2,1,0:T(8,128)(2,1)S(1)}, bf16[2,48,256]{2,1,0:T(8,128)(2,1)}, u32[]{:S(2)}) copy-start(bf16[2,48,256]{2,1,0:T(8,128)(2,1)} %param.8) | copy-start | bytes 147460
  18.7 38.3 %copy-start.3 = (s32[2,8]{1,0:T(2,128)S(1)}, s32[2,8]{1,0:T(2,128)}, u32[]{:S(2)}) copy-start(s32[2,8]{1,0:T(2,128)} %param.13) | copy-start | bytes 196
  19.8 15.9 %all-to-all-start = ((bf16[4,2,48,1280]{3,2,1,0:T(8,128)(2,1)}), bf16[4,2,48,1280]{3,2,1,0:T(8,128)(2,1)S(1)}, u32[]{:S(2)}, u32[]{:S(2)}) async-start(bf16[4,2,48,1280]{3,2,1,0:T(8,128)(2,1)} %broadcast_select_fusion), calls=%async_computation | async-start | bytes 1966080 | tf_op jit(solution)/shard_map/all_to_all | solution.py:140
  48.8 27.0 %collective-permute-start = (bf16[2,4,48,1280]{3,2,1,0:T(8,128)(2,1)}, bf16[2,4,48,1280]{3,2,1,0:T(8,128)(2,1)}, u32[]{:S(2)}, u32[]{:S(2)}) collective-permute-start(bf16[2,4,48,1280]{3,2,1,0:T(8,128)(2,1)} %all_gather.8.q_ref), channel_id=1, source_target_pairs={{0,1},{1,0},{2,3},{3,2},{4,5},{5,4},{6,7},{7,6},{8,9},{9,8},{10,11... | collective-permute-start | bytes 2949128 | tf_op jit(solution)/shard_map/ppermute | solution.py:148
  104.0 6.0 %copy-start.1 = (bf16[4,48,1280]{2,1,0:T(8,128)(2,1)S(1)}, bf16[4,48,1280]{2,1,0:T(8,128)(2,1)}, u32[]{:S(2)}) copy-start(bf16[4,48,1280]{2,1,0:T(8,128)(2,1)} %dynamic-slice_bitcast_fusion.1) | copy-start | bytes 1474564
  105.3 24.3 %all-to-all-start.2 = ((f32[4,784,128]{2,1,0:T(8,128)}), f32[4,784,128]{2,1,0:T(8,128)S(1)}, u32[]{:S(2)}, u32[]{:S(2)}) async-start(f32[4,784,128]{2,1,0:T(8,128)} %maximum_maximum_fusion.1), calls=%async_computation.2 | async-start | bytes 3211264 | tf_op jit(solution)/shard_map/all_to_all | solution.py:194

commit v13 on v12

--- a/solution.py
+++ b/solution.py
@@ -196,8 +196,9 @@
 
     my_slot = position // per_slot
     my_tok0 = (position % per_slot) * tok
-    mine_own = lax.dynamic_index_in_dim(own_x, my_slot, 0, keepdims=False)
-    mine_other = lax.dynamic_index_in_dim(other_x, my_slot, 0, keepdims=False)
+    late_own, late_other, _ = lax.optimization_barrier((own_x, other_x, part_acc))
+    mine_own = lax.dynamic_index_in_dim(late_own, my_slot, 0, keepdims=False)
+    mine_other = lax.dynamic_index_in_dim(late_other, my_slot, 0, keepdims=False)
     mine_all = jnp.where(
         first,
         jnp.concatenate([mine_own, mine_other], axis=0),

time: 132 us -> 131 us (level)
  local copies, waits for them, and re-layouts: 12.3 us -> 10.6 us
    squeeze x2 -> x1, local copies, waits for them, and re-layouts: 2.93 us -> 1.25 us  [body(): lax.dynamic_index_in_dim(late_other, my_slot, 0, keepdims=False)]
  transfers between devices with their start and end apart: 3 -> 3, of which waited for: 2 -> 2; matrix products, arithmetic and copies ran while one was open for 5% -> 4% of each run, Pallas kernels for 12% -> 12%
where the time goes in v13:
time: 131 us; the launch traced here: 130 us
  blocking collectives  33.3 us (25%)
  Pallas kernels  32.3 us (25%)
  waiting for transfers between devices  28.8 us (22%)
  starting transfers between devices  15.1 us (12%)
  local copies, waits for them, and re-layouts  10.6 us (8%)
  other arithmetic  7.38 us (6%)
  matrix products  1.48 us (1%)
    pallas_call x2, Pallas kernels, local_attention(): pl.pallas_call(kern, grid_spec=grid_spec, out_shape=[jax.ShapeDtypeStruct...  32.3 us
    all_to_all x1, waiting for transfers between devices, body(): pk = lax.all_to_all(pack(a1, m1, l1), 'x', 0, 0, tiled=True)  17.2 us
    all_gather x1, blocking collectives, body(): held = lax.all_gather(both, 'z', axis=0, tiled=True)  15 us
    all_gather x1, blocking collectives, body(): own_x = lax.all_gather(own, 'x', axis=1, tiled=False)  12.4 us
    all_to_all x1, waiting for transfers between devices, body(): recv = lax.all_to_all(send, 'y', 0, 0, tiled=True)  11.6 us
    ppermute x1, starting transfers between devices, body(): other_x = lax.ppermute(own_x, 'c', perm=[(0, 1), (1, 0)])  7.31 us
    all_to_all x1, blocking collectives, body(): pk = lax.all_to_all(pk, 'c', 1, 1, tiled=True)  5.95 us
    all_to_all x1, starting transfers between devices, body(): recv = lax.all_to_all(send, 'y', 0, 0, tiled=True)  4.18 us
  transfers between devices with their start and end apart: 3, of which 2 were waited for; matrix products, arithmetic and copies ran while one was open for 4% of the time, Pallas kernels for 12%

profile of v13, /device:TPU:1, one launch (start us, length us, event | category | flops | bytes accessed | tf_op | source)
XLA Modules:
  0.0 130.0 jit_solution(12043035667075119005)
XLA Ops:
  0.7 1.3 gather_fusion
  2.1 1.0 pad_maximum_fusion
  3.1 15.0 %all_gather.7 = bf16[8,48,1280]{2,1,0:T(8,128)(2,1)S(1)} all-gather(bf16[2,48,1280]{2,1,0:T(8,128)(2,1)S(1)} %pad_maximum_fusion), channel_id=1, replica_groups=mesh['z'=4,'y'=4,'x'=4,'c'=2] {'z'}, dimensions={0}, use_global_device_ids=true | all-gather | bytes 1228800 | tf_op jit(solution)/shard_map/all_gather | solution.py:134
  18.1 0.6 gather_fusion.1
  18.7 1.1 broadcast_select_fusion
  19.8 4.2 %all-to-all-start = ((bf16[4,2,48,1280]{3,2,1,0:T(8,128)(2,1)}), bf16[4,2,48,1280]{3,2,1,0:T(8,128)(2,1)S(1)}, u32[]{:S(2)}, u32[]{:S(2)}) async-start(bf16[4,2,48,1280]{3,2,1,0:T(8,128)(2,1)} %broadcast_select_fusion), calls=%async_computation | async-start | bytes 1966080 | tf_op jit(solution)/shard_map/all_to_all | solution.py:140
  24.1 11.6 %all-to-all-done = bf16[4,2,48,1280]{3,2,1,0:T(8,128)(2,1)S(1)} async-done(((bf16[4,2,48,1280]{3,2,1,0:T(8,128)(2,1)}), bf16[4,2,48,1280]{3,2,1,0:T(8,128)(2,1)S(1)}, u32[]{:S(2)}, u32[]{:S(2)}) %all-to-all-start) | async-done | bytes 983072 | tf_op jit(solution)/shard_map/all_to_all | solution.py:140
  35.8 0.6 gather_fusion.2
  36.4 12.4 %all_gather.8.q_ref = bf16[2,4,48,1280]{3,2,1,0:T(8,128)(2,1)} all-gather(bf16[2,1,48,1280]{3,2,1,0:T(8,128)(2,1)S(1)} %bitcast_select_fusion), channel_id=1, replica_groups=mesh['z'=4,'y'=4,'x'=4,'c'=2] {'x'}, dimensions={1}, use_global_device_ids=true | all-gather | bytes 1228800 | tf_op jit(solution)/shard_map/all_gather | solution.py:147
  48.8 7.3 %collective-permute-start = (bf16[2,4,48,1280]{3,2,1,0:T(8,128)(2,1)}, bf16[2,4,48,1280]{3,2,1,0:T(8,128)(2,1)}, u32[]{:S(2)}, u32[]{:S(2)}) collective-permute-start(bf16[2,4,48,1280]{3,2,1,0:T(8,128)(2,1)} %all_gather.8.q_ref), channel_id=1, source_target_pairs={{0,1},{1,0},{2,3},{3,2},{4,5},{5,4},{6,7},{7,6},{8,9},{9,8},{10,11... | collective-permute-start | bytes 2949128 | tf_op jit(solution)/shard_map/ppermute | solution.py:148
  56.3 0.7 fusion.17
  57.0 0.8 convolution_convert_fusion
  57.8 16.2 %shard_map.86 = (f32[2,8,8,384]{3,2,1,0:T(8,128)S(1)}, f32[2,8,8,384]{3,2,1,0:T(8,128)S(1)}, f32[8,8,96,128]{3,2,1,0:T(8,128)S(1)}) custom-call(s32[3]{0:T(128)S(1)} %get-tuple-element.29.live_ref, bf16[2,4,48,1280]{3,2,1,0:T(8,128)(2,1)} %all_gather.8.q_ref, bf16[2,2048,2048]{2,1,0:T(8,128)(2,1)} %kv_ref.3), custom_call_target="tpu_custom_call" | custom-call | tf_op jit(solution)/shard_map/pallas_call | solution.py:90
  74.0 16.2 %shard_map.87 = (f32[2,8,8,384]{3,2,1,0:T(8,128)S(1)}, f32[2,8,8,384]{3,2,1,0:T(8,128)S(1)}, f32[8,8,96,128]{3,2,1,0:T(8,128)S(1)}) custom-call(s32[3]{0:T(128)S(1)} %get-tuple-element.30.live_ref, bf16[2,4,48,1280]{3,2,1,0:T(8,128)(2,1)} %collective-permute-done.q_ref, ...), custom_call_target="tpu_custom_call", output_to_operand_aliasing={{0}: (3, {}), {1}: (4, {}), {2}: (5, {})} | custom-call | tf_op jit(solution)/shard_map/pallas_call | solution.py:90
  90.3 0.3 reshape_squeeze.6
  90.6 0.7 copy.75
  91.4 1.1 reshape_reshape_reshape.6
  92.5 0.3 reshape_squeeze.7
  92.8 0.7 copy.74
  93.6 1.1 reshape_reshape_reshape.7
  95.0 6.0 %all_to_all.15 = f32[4,2,784,128]{3,2,0,1:T(8,128)S(1)} all-to-all(f32[4,2,784,128]{3,2,0,1:T(8,128)S(1)} %maximum_maximum_fusion), channel_id=1, replica_groups=mesh['z'=4,'y'=4,'x'=4,'c'=2] {'c'}, dimensions={1} | all-to-all | bytes 6422528 | tf_op jit(solution)/shard_map/all_to_all | solution.py:192
  101.0 1.1 fusion
  102.1 1.3 %maximum_maximum_fusion.1 = f32[4,784,128]{2,1,0:T(8,128)} fusion(f32[4,6,128]{2,1,0:T(8,128)S(1)} %fusion.13, f32[4,6,128]{2,1,0:T(8,128)S(1)} %get-tuple-element.21, f32[4,768,128]{2,1,0:T(8,128)S(1)} %fusion, f32[784]{0:T(1024)S(1)} %pad.17.clone), kind=kLoop, calls=%fused_computation.8 | loop fusion | flops 1204224 | bytes 3206208 | tf_op jit(solution)/shard_map/concatenate | solution.py:178
  103.5 3.6 %all-to-all-start.2 = ((f32[4,784,128]{2,1,0:T(8,128)}), f32[4,784,128]{2,1,0:T(8,128)S(1)}, u32[]{:S(2)}, u32[]{:S(2)}) async-start(f32[4,784,128]{2,1,0:T(8,128)} %maximum_maximum_fusion.1), calls=%async_computation.2 | async-start | bytes 3211264 | tf_op jit(solution)/shard_map/all_to_all | solution.py:194
  107.0 1.2 dynamic-slice_bitcast_fusion
  108.9 0.3 fusion.32
  109.2 0.4 fusion.33
  109.7 0.3 fusion.6
  110.1 0.4 fusion.4
  110.6 17.2 %all-to-all-done.2 = f32[4,784,128]{2,1,0:T(8,128)S(1)} async-done(((f32[4,784,128]{2,1,0:T(8,128)}), f32[4,784,128]{2,1,0:T(8,128)S(1)}, u32[]{:S(2)}, u32[]{:S(2)}) %all-to-all-start.2) | async-done | bytes 1605664 | tf_op jit(solution)/shard_map/all_to_all | solution.py:194
  128.0 0.7 fusion.1
  129.1 0.9 copy.49
  (51 shorter events, 2.5 us)
Async XLA Ops:
  18.0 6.0 %copy-start = (s32[32]{0:T(128)S(1)}, s32[32]{0:T(128)}, u32[]{:S(2)}) copy-start(s32[32]{0:T(128)} %param.12) | copy-start | bytes 388
  18.7 37.5 %copy-start.3 = (s32[2]{0:T(128)S(1)}, s32[2]{0:T(128)}, u32[]{:S(2)}) copy-start(s32[2]{0:T(128)} %param.10) | copy-start | bytes 28
  18.7 38.3 %copy-start.1 = (bf16[2,48,256]{2,1,0:T(8,128)(2,1)S(1)}, bf16[2,48,256]{2,1,0:T(8,128)(2,1)}, u32[]{:S(2)}) copy-start(bf16[2,48,256]{2,1,0:T(8,128)(2,1)} %param.8) | copy-start | bytes 147460
  18.7 38.3 %copy-start.2 = (s32[2,8]{1,0:T(2,128)S(1)}, s32[2,8]{1,0:T(2,128)}, u32[]{:S(2)}) copy-start(s32[2,8]{1,0:T(2,128)} %param.13) | copy-start | bytes 196
  19.8 15.9 %all-to-all-start = ((bf16[4,2,48,1280]{3,2,1,0:T(8,128)(2,1)}), bf16[4,2,48,1280]{3,2,1,0:T(8,128)(2,1)S(1)}, u32[]{:S(2)}, u32[]{:S(2)}) async-start(bf16[4,2,48,1280]{3,2,1,0:T(8,128)(2,1)} %broadcast_select_fusion), calls=%async_computation | async-start | bytes 1966080 | tf_op jit(solution)/shard_map/all_to_all | solution.py:140
  48.8 25.2 %collective-permute-start = (bf16[2,4,48,1280]{3,2,1,0:T(8,128)(2,1)}, bf16[2,4,48,1280]{3,2,1,0:T(8,128)(2,1)}, u32[]{:S(2)}, u32[]{:S(2)}) collective-permute-start(bf16[2,4,48,1280]{3,2,1,0:T(8,128)(2,1)} %all_gather.8.q_ref), channel_id=1, source_target_pairs={{0,1},{1,0},{2,3},{3,2},{4,5},{5,4},{6,7},{7,6},{8,9},{9,8},{10,11... | collective-permute-start | bytes 2949128 | tf_op jit(solution)/shard_map/ppermute | solution.py:148
  103.5 24.3 %all-to-all-start.2 = ((f32[4,784,128]{2,1,0:T(8,128)}), f32[4,784,128]{2,1,0:T(8,128)S(1)}, u32[]{:S(2)}, u32[]{:S(2)}) async-start(f32[4,784,128]{2,1,0:T(8,128)} %maximum_maximum_fusion.1), calls=%async_computation.2 | async-start | bytes 3211264 | tf_op jit(solution)/shard_map/all_to_all | solution.py:194

commit v14 on v13

--- a/solution.py
+++ b/solution.py
@@ -116,12 +116,6 @@
 def body(queries, draft_key_value, kv_cache, cache_lengths, ancestors, dealing, accepted_path):
     local_reqs = kv_cache.shape[0]
     tree_len = queries.shape[1]
-    picker = (
-        accepted_path[:, :, None] == jnp.arange(tree_len, dtype=jnp.int32)[None, None, :]
-    ).astype(jnp.bfloat16)
-    kept_entries = jnp.einsum(
-        "rit,rtc->ric", picker, draft_key_value, preferred_element_type=jnp.float32
-    ).astype(jnp.bfloat16)
 
     nz, ny, nx, nc = (lax.axis_size(a) for a in ("z", "y", "x", "c"))
     zi, yi, xi, ci = (lax.axis_index(a) for a in ("z", "y", "x", "c"))
@@ -196,6 +190,13 @@
 
     my_slot = position // per_slot
     my_tok0 = (position % per_slot) * tok
+    late_draft, late_path, _ = lax.optimization_barrier((draft_key_value, accepted_path, part_acc))
+    picker = (
+        late_path[:, :, None] == jnp.arange(tree_len, dtype=jnp.int32)[None, None, :]
+    ).astype(jnp.bfloat16)
+    kept_entries = jnp.einsum(
+        "rit,rtc->ric", picker, late_draft, preferred_element_type=jnp.float32
+    ).astype(jnp.bfloat16)
     late_own, late_other, _ = lax.optimization_barrier((own_x, other_x, part_acc))
     mine_own = lax.dynamic_index_in_dim(late_own, my_slot, 0, keepdims=False)
     mine_other = lax.dynamic_index_in_dim(late_other, my_slot, 0, keepdims=False)

time: 131 us -> 132 us (level)
  transfers between devices with their start and end apart: 3 -> 3, of which waited for: 2 -> 2; matrix products, arithmetic and copies ran while one was open for 4% -> 3% of each run, Pallas kernels for 12% -> 12%
where the time goes in v14:
time: 132 us; the launch traced here: 131 us
  blocking collectives  33.3 us (25%)
  Pallas kernels  32.3 us (24%)
  waiting for transfers between devices  29.5 us (22%)
  starting transfers between devices  15.1 us (11%)
  local copies, waits for them, and re-layouts  11.3 us (9%)
  other arithmetic  7.38 us (6%)
  matrix products  1.48 us (1%)
    pallas_call x2, Pallas kernels, local_attention(): pl.pallas_call(kern, grid_spec=grid_spec, out_shape=[jax.ShapeDtypeStruct...  32.3 us
    all_to_all x1, waiting for transfers between devices, body(): pk = lax.all_to_all(pack(a1, m1, l1), 'x', 0, 0, tiled=True)  17.9 us
    all_gather x1, blocking collectives, body(): held = lax.all_gather(both, 'z', axis=0, tiled=True)  15 us
    all_gather x1, blocking collectives, body(): own_x = lax.all_gather(own, 'x', axis=1, tiled=False)  12.4 us
    all_to_all x1, waiting for transfers between devices, body(): recv = lax.all_to_all(send, 'y', 0, 0, tiled=True)  11.6 us
    ppermute x1, starting transfers between devices, body(): other_x = lax.ppermute(own_x, 'c', perm=[(0, 1), (1, 0)])  7.33 us
    all_to_all x1, blocking collectives, body(): pk = lax.all_to_all(pk, 'c', 1, 1, tiled=True)  5.95 us
    all_to_all x1, starting transfers between devices, body(): recv = lax.all_to_all(send, 'y', 0, 0, tiled=True)  4.18 us
  transfers between devices with their start and end apart: 3, of which 2 were waited for; matrix products, arithmetic and copies ran while one was open for 3% of the time, Pallas kernels for 12%

profile of v14, /device:TPU:1, one launch (start us, length us, event | category | flops | bytes accessed | tf_op | source)
XLA Modules:
  0.0 131.4 jit_solution(9064544850719392203)
XLA Ops:
  0.7 1.3 gather_fusion
  2.1 1.0 pad_maximum_fusion
  3.1 15.0 %all_gather.7 = bf16[8,48,1280]{2,1,0:T(8,128)(2,1)S(1)} all-gather(bf16[2,48,1280]{2,1,0:T(8,128)(2,1)S(1)} %pad_maximum_fusion), channel_id=1, replica_groups=mesh['z'=4,'y'=4,'x'=4,'c'=2] {'z'}, dimensions={0}, use_global_device_ids=true | all-gather | bytes 1228800 | tf_op jit(solution)/shard_map/all_gather | solution.py:128
  18.1 0.6 gather_fusion.1
  18.7 1.1 broadcast_select_fusion
  19.8 4.2 %all-to-all-start = ((bf16[4,2,48,1280]{3,2,1,0:T(8,128)(2,1)}), bf16[4,2,48,1280]{3,2,1,0:T(8,128)(2,1)S(1)}, u32[]{:S(2)}, u32[]{:S(2)}) async-start(bf16[4,2,48,1280]{3,2,1,0:T(8,128)(2,1)} %broadcast_select_fusion), calls=%async_computation | async-start | bytes 1966080 | tf_op jit(solution)/shard_map/all_to_all | solution.py:134
  24.1 11.6 %all-to-all-done = bf16[4,2,48,1280]{3,2,1,0:T(8,128)(2,1)S(1)} async-done(((bf16[4,2,48,1280]{3,2,1,0:T(8,128)(2,1)}), bf16[4,2,48,1280]{3,2,1,0:T(8,128)(2,1)S(1)}, u32[]{:S(2)}, u32[]{:S(2)}) %all-to-all-start) | async-done | bytes 983072 | tf_op jit(solution)/shard_map/all_to_all | solution.py:134
  35.7 0.6 gather_fusion.2
  36.4 12.4 %all_gather.8.q_ref = bf16[2,4,48,1280]{3,2,1,0:T(8,128)(2,1)} all-gather(bf16[2,1,48,1280]{3,2,1,0:T(8,128)(2,1)S(1)} %bitcast_select_fusion), channel_id=1, replica_groups=mesh['z'=4,'y'=4,'x'=4,'c'=2] {'x'}, dimensions={1}, use_global_device_ids=true | all-gather | bytes 1228800 | tf_op jit(solution)/shard_map/all_gather | solution.py:141
  48.8 7.3 %collective-permute-start = (bf16[2,4,48,1280]{3,2,1,0:T(8,128)(2,1)}, bf16[2,4,48,1280]{3,2,1,0:T(8,128)(2,1)}, u32[]{:S(2)}, u32[]{:S(2)}) collective-permute-start(bf16[2,4,48,1280]{3,2,1,0:T(8,128)(2,1)} %all_gather.8.q_ref), channel_id=1, source_target_pairs={{0,1},{1,0},{2,3},{3,2},{4,5},{5,4},{6,7},{7,6},{8,9},{9,8},{10,11... | collective-permute-start | bytes 2949128 | tf_op jit(solution)/shard_map/ppermute | solution.py:142
  56.3 0.7 fusion.17
  57.0 16.2 %shard_map.86 = (f32[2,8,8,384]{3,2,1,0:T(8,128)S(1)}, f32[2,8,8,384]{3,2,1,0:T(8,128)S(1)}, f32[8,8,96,128]{3,2,1,0:T(8,128)S(1)}) custom-call(s32[3]{0:T(128)S(1)} %get-tuple-element.33.live_ref, bf16[2,4,48,1280]{3,2,1,0:T(8,128)(2,1)} %all_gather.8.q_ref, bf16[2,2048,2048]{2,1,0:T(8,128)(2,1)} %kv_ref.3), custom_call_target="tpu_custom_call" | custom-call | tf_op jit(solution)/shard_map/pallas_call | solution.py:90
  73.2 16.2 %shard_map.87 = (f32[2,8,8,384]{3,2,1,0:T(8,128)S(1)}, f32[2,8,8,384]{3,2,1,0:T(8,128)S(1)}, f32[8,8,96,128]{3,2,1,0:T(8,128)S(1)}) custom-call(s32[3]{0:T(128)S(1)} %get-tuple-element.34.live_ref, bf16[2,4,48,1280]{3,2,1,0:T(8,128)(2,1)} %collective-permute-done.q_ref, ...), custom_call_target="tpu_custom_call", output_to_operand_aliasing={{0}: (3, {}), {1}: (4, {}), {2}: (5, {})} | custom-call | tf_op jit(solution)/shard_map/pallas_call | solution.py:90
  89.4 1.2 dynamic-slice_bitcast_fusion
  90.9 0.8 copy-done.1
  91.7 0.3 reshape_squeeze.7
  92.1 0.7 copy.74
  92.8 1.1 reshape_reshape_reshape.7
  93.9 0.3 reshape_squeeze.6
  94.3 0.7 copy.75
  95.0 1.1 reshape_reshape_reshape.6
  96.4 6.0 %all_to_all.15 = f32[4,2,784,128]{3,2,0,1:T(8,128)S(1)} all-to-all(f32[4,2,784,128]{3,2,0,1:T(8,128)S(1)} %maximum_maximum_fusion), channel_id=1, replica_groups=mesh['z'=4,'y'=4,'x'=4,'c'=2] {'c'}, dimensions={1} | all-to-all | bytes 6422528 | tf_op jit(solution)/shard_map/all_to_all | solution.py:186
  102.5 1.1 fusion
  103.5 1.3 %maximum_maximum_fusion.1 = f32[4,784,128]{2,1,0:T(8,128)} fusion(f32[4,6,128]{2,1,0:T(8,128)S(1)} %fusion.13, f32[4,6,128]{2,1,0:T(8,128)S(1)} %get-tuple-element.25, f32[4,768,128]{2,1,0:T(8,128)S(1)} %fusion, f32[784]{0:T(1024)S(1)} %pad.17.clone), kind=kLoop, calls=%fused_computation.8 | loop fusion | flops 1204224 | bytes 3206208 | tf_op jit(solution)/shard_map/concatenate | solution.py:172
  104.9 3.6 %all-to-all-start.2 = ((f32[4,784,128]{2,1,0:T(8,128)}), f32[4,784,128]{2,1,0:T(8,128)S(1)}, u32[]{:S(2)}, u32[]{:S(2)}) async-start(f32[4,784,128]{2,1,0:T(8,128)} %maximum_maximum_fusion.1), calls=%async_computation.2 | async-start | bytes 3211264 | tf_op jit(solution)/shard_map/all_to_all | solution.py:188
  109.1 0.4 fusion.33
  109.7 0.3 fusion.6
  110.1 0.4 fusion.4
  110.6 0.8 convolution_convert_fusion
  111.4 17.9 %all-to-all-done.2 = f32[4,784,128]{2,1,0:T(8,128)S(1)} async-done(((f32[4,784,128]{2,1,0:T(8,128)}), f32[4,784,128]{2,1,0:T(8,128)S(1)}, u32[]{:S(2)}, u32[]{:S(2)}) %all-to-all-start.2) | async-done | bytes 1605664 | tf_op jit(solution)/shard_map/all_to_all | solution.py:188
  129.5 0.7 fusion.1
  130.6 0.9 copy.49
  (55 shorter events, 2.6 us)
Async XLA Ops:
  18.1 5.9 %copy-start = (s32[32]{0:T(128)S(1)}, s32[32]{0:T(128)}, u32[]{:S(2)}) copy-start(s32[32]{0:T(128)} %param.12) | copy-start | bytes 388
  18.7 37.5 %copy-start.4 = (s32[2]{0:T(128)S(1)}, s32[2]{0:T(128)}, u32[]{:S(2)}) copy-start(s32[2]{0:T(128)} %param.10) | copy-start | bytes 28
  19.8 15.9 %all-to-all-start = ((bf16[4,2,48,1280]{3,2,1,0:T(8,128)(2,1)}), bf16[4,2,48,1280]{3,2,1,0:T(8,128)(2,1)S(1)}, u32[]{:S(2)}, u32[]{:S(2)}) async-start(bf16[4,2,48,1280]{3,2,1,0:T(8,128)(2,1)} %broadcast_select_fusion), calls=%async_computation | async-start | bytes 1966080 | tf_op jit(solution)/shard_map/all_to_all | solution.py:134
  48.8 24.4 %collective-permute-start = (bf16[2,4,48,1280]{3,2,1,0:T(8,128)(2,1)}, bf16[2,4,48,1280]{3,2,1,0:T(8,128)(2,1)}, u32[]{:S(2)}, u32[]{:S(2)}) collective-permute-start(bf16[2,4,48,1280]{3,2,1,0:T(8,128)(2,1)} %all_gather.8.q_ref), channel_id=1, source_target_pairs={{0,1},{1,0},{2,3},{3,2},{4,5},{5,4},{6,7},{7,6},{8,9},{9,8},{10,11... | collective-permute-start | bytes 2949128 | tf_op jit(solution)/shard_map/ppermute | solution.py:142
  90.8 0.9 copy-start.1
  103.5 4.9 %slice-start.1 = ((bf16[8,48,1280]{2,1,0:T(8,128)(2,1)}), bf16[8,48,1024]{2,1,0:T(8,128)(2,1)S(1)}, s32[]{:S(2)}) async-start(bf16[8,48,1280]{2,1,0:T(8,128)(2,1)} %copy-done.1), calls=%async_computation.4 | async-start | bytes 1572864 | tf_op jit(solution)/shard_map/slice | solution.py:208
  103.5 5.2 %slice-start = ((bf16[8,48,1280]{2,1,0:T(8,128)(2,1)}), bf16[8,48,256]{2,1,0:T(8,128)(2,1)S(1)}, s32[]{:S(2)}) async-start(bf16[8,48,1280]{2,1,0:T(8,128)(2,1)} %copy-done.1), calls=%async_computation.3 | async-start | bytes 393216 | tf_op jit(solution)/shard_map/slice | solution.py:211
  104.9 24.3 %all-to-all-start.2 = ((f32[4,784,128]{2,1,0:T(8,128)}), f32[4,784,128]{2,1,0:T(8,128)S(1)}, u32[]{:S(2)}, u32[]{:S(2)}) async-start(f32[4,784,128]{2,1,0:T(8,128)} %maximum_maximum_fusion.1), calls=%async_computation.2 | async-start | bytes 3211264 | tf_op jit(solution)/shard_map/all_to_all | solution.py:188
  108.5 2.1 %copy-start.2 = (bf16[2,48,256]{2,1,0:T(8,128)(2,1)S(1)}, bf16[2,48,256]{2,1,0:T(8,128)(2,1)}, u32[]{:S(2)}) copy-start(bf16[2,48,256]{2,1,0:T(8,128)(2,1)} %param.8) | copy-start | bytes 147460
  108.5 2.1 %copy-start.3 = (s32[2,8]{1,0:T(2,128)S(1)}, s32[2,8]{1,0:T(2,128)}, u32[]{:S(2)}) copy-start(s32[2,8]{1,0:T(2,128)} %param.13) | copy-start | bytes 196
